TPU v7x, 128 devices: a whole 4x4x4 slice. The times are simulated.
128 devices in a mesh: gx: 8 (over z, core), gy: 16 (over y, x).
Axes of the slice: x: 4, y: 4, z: 4, core: 2. Of those that a mesh axis runs over, the one named last changes fastest.
Arguments:
- hidden_in: bfloat16 [32768, 3584], P(('gx', 'gy')), may hold values from -6 to 6
- lengths: int32 [8, 4], P('gx'), may hold values from 1 to 2048, 4096 in all within a row
- attn_norm: float32 [3584], replicated, may hold values from 0.5 to 1.5
- qkv_weight: bfloat16 [3584, 4608], P('gx', 'gy'), may hold values from -0.09375 to 0.09375
- qkv_bias: float32 [4608], replicated, may hold values from -5 to 5
Outputs:
- attn: bfloat16 [32768, 3584], P(('gx', 'gy'))
- kv_rows: bfloat16 [32768, 1024], P(('gx', 'gy'))
Inputs may be any that keep to these rules, and one draw needn't show every extreme that they name: Each row of lengths sums to 4096; the longest of each row is exactly 2048.
All inputs are finite; a program needn't handle non-finite values.
Results may differ from a plain program's by a relative error of at most 0.0035.
The roundings to bfloat16 on the way count: a program that leaves them out, or rounds other values in their place, can miss the bound.
Values may be sent and summed in bfloat16 or wider, within the bound.
No kernel may reach another device: no remote copies, remote signals or barrier semaphores. Data moves between devices by JAX's collectives and lax.ppermute only.
A program may use at most 128 MiB of HBM per device.

v0:
```python
import math

import jax
import jax.numpy as jnp
from jax import lax
from jax.sharding import PartitionSpec as P
from jax.experimental import pallas as pl
from jax.experimental.pallas import tpu as pltpu

HEADS = 28
KV_HEADS = 4
HEAD_DIM = 128


BLOCK = 256


LANES = 128


def flash_body(meta, q_ref, k_ref, v_ref, o_ref, bias_ref, m_ref, l_ref, acc_ref):
    step = pl.program_id(1)
    last = pl.num_programs(1) - 1
    first = meta[4] * BLOCK
    block = jnp.minimum(meta[5] + step, meta[4])
    group = HEADS // KV_HEADS

    @pl.when(step == 0)
    def _():
        m_ref[...] = jnp.full(m_ref.shape, -1e30, jnp.float32)
        l_ref[...] = jnp.zeros(l_ref.shape, jnp.float32)
        acc_ref[...] = jnp.zeros(acc_ref.shape, jnp.float32)

    @pl.when(meta[5] + step <= meta[4])
    def _():
        krow = block * BLOCK + lax.broadcasted_iota(jnp.int32, (BLOCK, 1), 0)
        qcol = first + lax.broadcasted_iota(jnp.int32, (1, BLOCK), 1)
        qstart = jnp.zeros((1, BLOCK), jnp.int32)
        for s in range(4):
            end = meta[s]
            qstart = jnp.where(end <= qcol, end, qstart)
        allowed = (krow >= qstart) & (krow <= qcol)
        bias_ref[...] = jnp.where(allowed, 0.0, -1e30).astype(jnp.float32)
        keys = k_ref[...]
        values = v_ref[...]
        scale = 1.0 / HEAD_DIM**0.5
        for h in range(group):
            heads = slice(h * HEAD_DIM, (h + 1) * HEAD_DIM)
            for c in range(BLOCK // LANES):
                cols = slice(c * LANES, (c + 1) * LANES)
                q = q_ref[heads, cols]
                scores = (
                    jnp.dot(keys, q, preferred_element_type=jnp.float32) * scale
                    + bias_ref[:, cols]
                )
                m_prev = m_ref[h, :, cols]
                m_new = jnp.maximum(m_prev, jnp.max(scores, axis=0, keepdims=True))
                shrink = jnp.exp(m_prev - m_new)
                weights = jnp.exp(scores - m_new)
                l_ref[h, :, cols] = l_ref[h, :, cols] * shrink + jnp.sum(
                    weights, axis=0, keepdims=True
                )
                acc_ref[h, :, cols] = acc_ref[h, :, cols] * shrink + jnp.dot(
                    values, weights.astype(jnp.bfloat16), preferred_element_type=jnp.float32
                )
                m_ref[h, :, cols] = m_new

    @pl.when(step == last)
    def _():
        for h in range(group):
            o_ref[h * HEAD_DIM : (h + 1) * HEAD_DIM, :] = (acc_ref[h] / l_ref[h]).astype(
                o_ref.dtype
            )


def flash(meta, queries_t, keys, values_t, steps):
    rows = queries_t.shape[1]
    group = HEADS // KV_HEADS
    width = group * HEAD_DIM

    def key_map(g, t, meta):
        return (jnp.minimum(meta[5] + t, meta[4]), g)

    def value_map(g, t, meta):
        return (g, jnp.minimum(meta[5] + t, meta[4]))

    spec = pltpu.PrefetchScalarGridSpec(
        num_scalar_prefetch=1,
        grid=(KV_HEADS, steps),
        in_specs=[
            pl.BlockSpec((width, rows), lambda g, t, meta: (g, 0)),
            pl.BlockSpec((BLOCK, HEAD_DIM), key_map),
            pl.BlockSpec((HEAD_DIM, BLOCK), value_map),
        ],
        out_specs=pl.BlockSpec((width, rows), lambda g, t, meta: (g, 0)),
        scratch_shapes=[
            pltpu.VMEM((BLOCK, rows), jnp.float32),
            pltpu.VMEM((group, 1, rows), jnp.float32),
            pltpu.VMEM((group, 1, rows), jnp.float32),
            pltpu.VMEM((group, HEAD_DIM, rows), jnp.float32),
        ],
    )
    return pl.pallas_call(
        flash_body,
        grid_spec=spec,
        out_shape=jax.ShapeDtypeStruct((HEADS * HEAD_DIM, rows), jnp.bfloat16),
        compiler_params=pltpu.CompilerParams(dimension_semantics=("arbitrary", "arbitrary")),
    )(meta, queries_t, keys, values_t)


def norm_rows(values, gain):
    wide = values.astype(jnp.float32)
    scale = lax.rsqrt(jnp.mean(wide * wide, axis=1, keepdims=True) + 1e-06)
    return (wide * scale * gain[None, :]).astype(jnp.bfloat16)


def segment_of(index, ends):
    return jnp.sum((ends[None, :] <= index[:, None]).astype(jnp.int32), axis=1)


def rotate(block, pos, heads):
    half = HEAD_DIM // 2
    freqs = 1000000.0 ** (-2.0 * jnp.arange(half, dtype=jnp.float32) / HEAD_DIM)
    angle = pos.astype(jnp.float32)[:, None, None] * freqs[None, None, :]
    wide = block.astype(jnp.float32).reshape(block.shape[0], heads, HEAD_DIM)
    first, second = (wide[..., :half], wide[..., half:])
    turned = jnp.concatenate(
        [
            first * jnp.cos(angle) - second * jnp.sin(angle),
            second * jnp.cos(angle) + first * jnp.sin(angle),
        ],
        axis=2,
    )
    return turned.reshape(block.shape[0], heads * HEAD_DIM).astype(jnp.bfloat16)


def project_joined(normed, weight, bias):
    rows, width = normed.shape[0], weight.shape[1]
    n_x = lax.axis_size("x")
    n_y = lax.axis_size("y")
    grouped = lax.all_gather(normed, "x", axis=0, tiled=True)
    pieces = lax.all_gather(weight, ("z", "c", "y"), axis=0, tiled=False)
    pieces = pieces.reshape(-1, n_y, weight.shape[0], width)
    summed = jnp.einsum(
        "tie,iyec->tyc",
        grouped.reshape(grouped.shape[0], pieces.shape[0], weight.shape[0]),
        pieces,
        preferred_element_type=jnp.float32,
    )
    bias_block = bias.reshape(n_y, n_x, width)
    bias_block = lax.dynamic_index_in_dim(bias_block, lax.axis_index("x"), 1, keepdims=False)
    block_out = (summed + bias_block[None]).astype(jnp.bfloat16)
    swapped = lax.all_to_all(block_out, "x", split_axis=0, concat_axis=1, tiled=True)
    swapped = swapped.reshape(rows, n_x, n_y, width)
    return jnp.transpose(swapped, (0, 2, 1, 3)).reshape(rows, n_y * n_x * width)


def on_device(hidden_in, lengths, attn_norm, qkv_weight, qkv_bias):
    rows = hidden_in.shape[0]
    gy_index = lax.axis_index("y") * lax.axis_size("x") + lax.axis_index("x")
    first = gy_index * rows
    row_lengths = lengths[0]
    qdim = HEADS * HEAD_DIM
    kdim = KV_HEADS * HEAD_DIM
    group = HEADS // KV_HEADS
    normed = norm_rows(hidden_in, attn_norm)
    joined = project_joined(normed, qkv_weight, qkv_bias)
    ends = jnp.cumsum(row_lengths)
    tokens_here = first + jnp.arange(rows, dtype=jnp.int32)
    before = ends[None, :] <= tokens_here[:, None]
    seg_here = jnp.sum(before.astype(jnp.int32), axis=1)
    begin = jnp.sum(jnp.where(before, row_lengths[None, :], 0), axis=1)
    pos = tokens_here - begin
    queries = rotate(joined[:, :qdim], pos, HEADS).reshape(rows, KV_HEADS, group, HEAD_DIM)
    keys = rotate(joined[:, qdim : qdim + kdim], pos, KV_HEADS)
    kv_rows = jnp.concatenate([keys, joined[:, qdim + kdim :]], axis=1)
    piece = lax.all_gather(kv_rows, ("y", "x"), axis=0, tiled=True)
    lead = jnp.max(jnp.where(ends <= first, ends, 0))
    meta = jnp.concatenate(
        [ends, jnp.stack([gy_index, lead // BLOCK, 0, 0]).astype(jnp.int32)]
    ).astype(jnp.int32)
    steps = min(piece.shape[0] // BLOCK, 9)
    queries_t = jnp.transpose(queries.reshape(rows, qdim))
    values_t = jnp.transpose(piece[:, kdim:])
    attn = jnp.transpose(flash(meta, queries_t, piece[:, :kdim], values_t, steps))
    return (attn, kv_rows)


def solution(mesh):
    n_z = len({d.coords[2] for d in mesh.devices.flat})
    grid = mesh.devices.reshape(n_z, -1, *mesh.devices.shape[1:])
    n_y = len({d.coords[1] for d in mesh.devices.flat})
    grid = grid.reshape(grid.shape[0], grid.shape[1], n_y, -1)
    split = jax.sharding.Mesh(grid, ("z", "c", "y", "x"))
    tokens = P(("z", "c", "y", "x"), None)
    placed = (tokens, P(("z", "c"), None), P(), P(("z", "c"), ("y", "x")), P())
    return jax.shard_map(
        on_device,
        mesh=split,
        in_specs=placed,
        out_specs=(tokens, tokens),
        check_vma=False,
    )
```

profile of v0, /device:TPU:28, one launch (start us, length us, event | category | flops | bytes accessed | tf_op | source)
XLA Modules:
  0.0 347.5 jit_solution(3244701723739601814)
XLA Ops:
  7.2 0.0 all-gather.6.cloned.1.call-start
  7.2 1.9 fusion.1
  9.2 3.2 fusion.3
  12.4 0.0 all-gather.10.cloned.1.call-start
  12.5 0.7 all-gather.10.cloned.1.call-update
  13.2 0.1 reshape.148
  13.3 75.2 %all-gather.6.cloned.1.call-done = bf16[1024,3584]{1,0:T(8,128)(2,1)} async-done(((bf16[256,3584]{1,0:T(8,128)(2,1)}), bf16[1024,3584]{1,0:T(8,128)(2,1)}) %all-gather.6.cloned.1.call-update) | async-done | bytes 7340048 | tf_op jit(solution)/shard_map/all_gather | solution.py:141
  88.5 10.4 %copy.25 = bf16[1024,3584]{0,1:T(8,128)(2,1)} copy(bf16[1024,3584]{1,0:T(8,128)(2,1)} %all-gather.6.cloned.1.call-done) | data formatting | bytes 14680064 | tf_op jit(solution)/shard_map/all_gather | solution.py:141
  98.9 48.5 %all-gather.10.cloned.1.call-done = bf16[32,448,288]{1,2,0:T(8,128)(2,1)} async-done(((bf16[1,448,288]{1,2,0:T(8,128)(2,1)}), bf16[32,448,288]{1,2,0:T(8,128)(2,1)}) %all-gather.10.cloned.1.call-update) | async-done | bytes 8257552 | tf_op jit(solution)/shard_map/all_gather | solution.py:142
  147.4 13.2 %fusion = bf16[1024,4,288]{0,2,1:T(8,128)(2,1)S(1)} fusion(f32[4,288]{1,0:T(4,128)S(1)} %bitcast.50, bf16[1024,8,448,1]{0,2,3,1:T(8,128)(2,1)} %bitcast.43, bf16[8,4,448,288]{2,3,1,0:T(8,128)(2,1)} %bitcast.55), kind=kOutput, calls=%fused_computation.1 | convolution fusion | flops 8458076160 | bytes 17961472 | tf_op jit(solution)/shard_map/tie,iyec->tyc/dot_general | solution.py:144
  160.6 3.8 %copy.27 = bf16[1024,4,288]{2,1,0:T(4,128)(2,1)} copy(bf16[1024,4,288]{0,2,1:T(8,128)(2,1)S(1)} %fusion) | data formatting | bytes 4718592 | tf_op jit(solution)/shard_map/convert_element_type | solution.py:152
  164.4 4.9 %all-to-all-start = ((bf16[1024,4,288]{2,1,0:T(4,128)(2,1)}), bf16[1024,4,288]{2,1,0:T(4,128)(2,1)S(1)}, u32[]{:S(2)}, u32[]{:S(2)}) async-start(bf16[1024,4,288]{2,1,0:T(4,128)(2,1)} %copy.27), calls=%async_computation | async-start | bytes 6291456 | tf_op jit(solution)/shard_map/all_to_all | solution.py:153
  169.3 0.2 reduce-window.8
  169.5 0.1 select_reduce_fusion
  169.6 0.3 multiply_cosine_fusion
  169.9 34.4 %all-to-all-done = bf16[1024,4,288]{2,1,0:T(4,128)(2,1)S(1)} async-done(((bf16[1024,4,288]{2,1,0:T(4,128)(2,1)}), bf16[1024,4,288]{2,1,0:T(4,128)(2,1)S(1)}, u32[]{:S(2)}, u32[]{:S(2)}) %all-to-all-start) | async-done | bytes 2359328 | tf_op jit(solution)/shard_map/all_to_all | solution.py:153
  204.3 4.2 %copy.28 = bf16[4,256,4,288]{1,3,0,2:T(8,128)(2,1)} copy(bf16[4,256,4,288]{3,2,1,0:T(4,128)(2,1)S(1)} %bitcast.40) | data formatting | bytes 4718592 | tf_op jit(solution)/shard_map/all_to_all | solution.py:153
  208.5 1.2 fusion.5
  209.8 0.1 subtract_convert_fusion.1
  209.9 0.8 pad_maximum_fusion.1
  210.8 0.6 fusion.4
  214.0 0.6 pad_add_fusion.meta
  214.6 1.3 slice.36
  215.9 1.0 copy.31
  216.9 1.9 convert.18
  218.9 0.6 subtract_convert_fusion
  219.5 1.4 pad_maximum_fusion
  220.9 65.4 %all-gather.8.cloned.1.call-done = bf16[4096,1024]{0,1:T(8,128)(2,1)} async-done(((bf16[256,1024]{0,1:T(8,128)(2,1)}), bf16[4096,1024]{0,1:T(8,128)(2,1)}) %all-gather.8.cloned.1.call-update) | async-done | bytes 8388624 | tf_op jit(solution)/shard_map/all_gather | solution.py:177
  286.2 5.9 %slice_bitcast_fusion = (bf16[512,4096]{1,0:T(8,128)(2,1)}, bf16[4096,512]{0,1:T(8,128)(2,1)}) fusion(bf16[4096,1024]{0,1:T(8,128)(2,1)} %all-gather.8.cloned.1.call-done), kind=kLoop, calls=%fused_computation.4 | loop fusion | bytes 16777216 | tf_op jit(solution)/shard_map/transpose | solution.py:184
  292.1 6.5 %copy.29.k_ref = bf16[4096,512]{1,0:T(8,128)(2,1)} copy(bf16[4096,512]{0,1:T(8,128)(2,1)} %get-tuple-element.11) | data formatting | bytes 8388608 | tf_op jit(solution)/shard_map/slice | solution.py:185
  298.6 38.6 %shard_map.68 = bf16[3584,256]{1,0:T(8,128)(2,1)} custom-call(s32[8]{0:T(128)} %pad_add_fusion.meta, bf16[3584,256]{1,0:T(8,128)(2,1)} %bitcast.44, bf16[4096,512]{1,0:T(8,128)(2,1)} %copy.29.k_ref, bf16[512,4096]{1,0:T(8,128)(2,1)} %get-tuple-element.10.v_ref), custom_call_target="tpu_custom_call" | custom-call | tf_op jit(solution)/shard_map/pallas_call | solution.py:103
  337.2 3.8 %copy.30 = bf16[256,3584]{1,0:T(8,128)(2,1)} copy(bf16[256,3584]{0,1:T(8,128)(2,1)} %bitcast.45) | data formatting | bytes 3670016
  (20 shorter events, 0.2 us)
Async XLA Ops:
  7.2 6.0 %copy-start.2 = (f32[4608]{0:T(1024)S(1)}, f32[4608]{0:T(1024)}, u32[]{:S(2)}) copy-start(f32[4608]{0:T(1024)} %param.9) | copy-start | bytes 55300
  7.2 81.4 %all-gather.6.cloned.1.call-start = ((), (), s32[]{:S(2)}) async-start(), calls=%async_computation.1 | async-start | bytes 9175040 | tf_op jit(solution)/shard_map/all_gather | solution.py:141
  12.4 135.0 %all-gather.10.cloned.1.call-start = ((), (), s32[]{:S(2)}) async-start(), calls=%async_computation.3 | async-start | bytes 9732096 | tf_op jit(solution)/shard_map/all_gather | solution.py:142
  164.4 4.9 %copy-start.3 = (s32[1,4]{1,0:T(1,128)S(1)}, s32[1,4]{1,0:T(1,128)}, u32[]{:S(2)}) copy-start(s32[1,4]{1,0:T(1,128)} %param.6) | copy-start | bytes 52
  164.4 39.9 %all-to-all-start = ((bf16[1024,4,288]{2,1,0:T(4,128)(2,1)}), bf16[1024,4,288]{2,1,0:T(4,128)(2,1)S(1)}, u32[]{:S(2)}, u32[]{:S(2)}) async-start(bf16[1024,4,288]{2,1,0:T(4,128)(2,1)} %copy.27), calls=%async_computation | async-start | bytes 6291456 | tf_op jit(solution)/shard_map/all_to_all | solution.py:153
  169.3 116.9 %all-gather.8.cloned.1.call-start = ((), (), s32[]{:S(2)}) async-start(), calls=%async_computation.2 | async-start | bytes 8912896 | tf_op jit(solution)/shard_map/all_gather | solution.py:177
  208.5 6.0 %copy-start = (bf16[4,256,4,288]{1,3,0,2:T(8,128)(2,1)S(1)}, bf16[4,256,4,288]{1,3,0,2:T(8,128)(2,1)}, u32[]{:S(2)}) copy-start(bf16[4,256,4,288]{1,3,0,2:T(8,128)(2,1)} %copy.28) | copy-start | bytes 7077892
  210.7 5.2 %copy-start.1 = (bf16[256,1024]{0,1:T(8,128)(2,1)S(1)}, bf16[256,1024]{0,1:T(8,128)(2,1)}, u32[]{:S(2)}) copy-start(bf16[256,1024]{0,1:T(8,128)(2,1)} %pad_maximum_fusion.1) | copy-start | bytes 1572868
Sparse Core Ops, SparseCore 0:
  12.6 75.9 all-gather.5
  90.8 56.5 all-gather.9
  210.9 75.2 all-gather.7
where the time goes:
time: 349 us; the launch traced here: 347 us
  waiting for transfers between devices  224 us (64%)
  Pallas kernels  38.6 us (11%)
  local copies, waits for them, and re-layouts  38.3 us (11%)
  between operations  16.5 us (5%)
  matrix products  13.2 us (4%)
  other arithmetic  11.9 us (3%)
  starting transfers between devices  5.01 us (1%)
    all_gather x1, waiting for transfers between devices, project_joined(): grouped = lax.all_gather(normed, 'x', axis=0, tiled=True)  75.2 us
    all_gather x1, waiting for transfers between devices, on_device(): piece = lax.all_gather(kv_rows, ('y', 'x'), axis=0, tiled=True)  65.4 us
    all_gather x1, waiting for transfers between devices, project_joined(): pieces = lax.all_gather(weight, ('z', 'c', 'y'), axis=0, tiled=False)  48.5 us
    pallas_call x1, Pallas kernels, flash(): pl.pallas_call(flash_body, grid_spec=spec, out_shape=jax.ShapeDtypeStruct...  38.6 us
    all_to_all x1, waiting for transfers between devices, project_joined(): lax.all_to_all(block_out, 'x', split_axis=0, concat_axis=1, tiled=True)  34.4 us
    dot_general x1, matrix products, project_joined(): jnp.einsum('tie,iyec->tyc', grouped.reshape(grouped.shape[0], pieces.shap...  13.2 us
    all_gather x1, local copies, waits for them, and re-layouts, project_joined(): grouped = lax.all_gather(normed, 'x', axis=0, tiled=True)  10.4 us
  transfers between devices with their start and end apart: 4, of which 4 were waited for; matrix products, arithmetic and copies ran while one was open for 5% of the time, Pallas kernels for 0%

commit v1 on v0

--- a/solution.py
+++ b/solution.py
@@ -138,12 +138,19 @@
     rows, width = normed.shape[0], weight.shape[1]
     n_x = lax.axis_size("x")
     n_y = lax.axis_size("y")
-    grouped = lax.all_gather(normed, "x", axis=0, tiled=True)
-    pieces = lax.all_gather(weight, ("z", "c", "y"), axis=0, tiled=False)
-    pieces = pieces.reshape(-1, n_y, weight.shape[0], width)
+    here = lax.axis_index("x")
+    shifted = [normed]
+    for step in range(1, n_x):
+        pairs = [(s, (s + step) % n_x) for s in range(n_x)]
+        shifted.append(lax.ppermute(normed, "x", pairs))
+    slots = jnp.stack(shifted)
+    order = (here - jnp.arange(n_x)) % n_x
+    grouped = jnp.take(slots, order, axis=0).reshape(n_x * rows, -1)
+    pieces = lax.all_gather(weight, ("y", "z", "c"), axis=0, tiled=False)
+    pieces = pieces.reshape(n_y, -1, width)
     summed = jnp.einsum(
-        "tie,iyec->tyc",
-        grouped.reshape(grouped.shape[0], pieces.shape[0], weight.shape[0]),
+        "td,ydc->tyc",
+        grouped,
         pieces,
         preferred_element_type=jnp.float32,
     )

time: 349 us -> 352 us (level)
  waiting for transfers between devices: 224 us -> 181 us
  local copies, waits for them, and re-layouts: 38.3 us -> 66.7 us
  other arithmetic: 11.9 us -> 25.6 us
    all_gather x2 -> x1, waiting for transfers between devices: 124 us -> 0.01 us  [project_joined(): pieces = lax.all_gather(weight, ('y', 'z', 'c'), axis=0, tiled=False)]
    ppermute x0 -> x3, waiting for transfers between devices: none -> 78.7 us  [project_joined(): shifted.append(lax.ppermute(normed, 'x', pairs))]
    reshape x0 -> x1, local copies, waits for them, and re-layouts: none -> 19 us  [project_joined(): pieces = pieces.reshape(n_y, -1, width)]
    gather x0 -> x1, local copies, waits for them, and re-layouts: none -> 7.12 us  [project_joined(): grouped = jnp.take(slots, order, axis=0).reshape(n_x * rows, -1)]
    select_n x0 -> x2, other arithmetic: none -> 6.87 us  [project_joined(): grouped = jnp.take(slots, order, axis=0).reshape(n_x * rows, -1)]
    another operation x3 -> x5, other arithmetic: 0.88 us -> 7.57 us  [the longest x2 6.69 us: project_joined(): slots = jnp.stack(shifted)]
  transfers between devices with their start and end apart: 4 -> 6, of which waited for: 4 -> 4; matrix products, arithmetic and copies ran while one was open for 5% -> 10% of each run, Pallas kernels for 0% -> 0%
where the time goes in v1:
time: 352 us; the launch traced here: 351 us
  waiting for transfers between devices  181 us (51%)
  local copies, waits for them, and re-layouts  66.7 us (19%)
  Pallas kernels  38.6 us (11%)
  other arithmetic  25.6 us (7%)
  between operations  16.8 us (5%)
  matrix products  13.4 us (4%)
  starting transfers between devices  8.2 us (2%)
    ppermute x3, waiting for transfers between devices, project_joined(): shifted.append(lax.ppermute(normed, 'x', pairs))  78.7 us
    all_gather x1, waiting for transfers between devices, on_device(): piece = lax.all_gather(kv_rows, ('y', 'x'), axis=0, tiled=True)  67.9 us
    pallas_call x1, Pallas kernels, flash(): pl.pallas_call(flash_body, grid_spec=spec, out_shape=jax.ShapeDtypeStruct...  38.6 us
    all_to_all x1, waiting for transfers between devices, project_joined(): lax.all_to_all(block_out, 'x', split_axis=0, concat_axis=1, tiled=True)  34.2 us
    reshape x1, local copies, waits for them, and re-layouts, project_joined(): pieces = pieces.reshape(n_y, -1, width)  19 us
    dot_general x1, matrix products, project_joined(): jnp.einsum('td,ydc->tyc', grouped, pieces, preferred_element_type=jnp.flo...  13.4 us
    all_gather x1, local copies, waits for them, and re-layouts, project_joined(): pieces = lax.all_gather(weight, ('y', 'z', 'c'), axis=0, tiled=False)  12.7 us
    gather x1, local copies, waits for them, and re-layouts, project_joined(): grouped = jnp.take(slots, order, axis=0).reshape(n_x * rows, -1)  7.12 us
  transfers between devices with their start and end apart: 6, of which 4 were waited for; matrix products, arithmetic and copies ran while one was open for 10% of the time, Pallas kernels for 0%

profile of v1, /device:TPU:28, one launch (start us, length us, event | category | flops | bytes accessed | tf_op | source)
XLA Modules:
  0.0 350.6 jit_solution(9046971021558633507)
XLA Ops:
  7.2 0.7 all-gather.7.cloned.1.call-update
  7.9 1.9 fusion.2
  9.9 3.2 fusion.4
  13.1 0.5 collective-permute-start.1
  13.6 2.1 collective-permute-start
  16.0 0.5 fusion.13
  16.5 41.3 %collective-permute-done.1 = bf16[256,3584]{1,0:T(8,128)(2,1)} collective-permute-done((bf16[256,3584]{1,0:T(8,128)(2,1)}, bf16[256,3584]{1,0:T(8,128)(2,1)}, u32[]{:S(2)}, u32[]{:S(2)}) %collective-permute-start.1) | collective-permute-done | bytes 1835040 | tf_op jit(solution)/shard_map/ppermute | solution.py:145
  57.8 37.4 %collective-permute-done = bf16[256,3584]{1,0:T(8,128)(2,1)} collective-permute-done((bf16[256,3584]{1,0:T(8,128)(2,1)}, bf16[256,3584]{1,0:T(8,128)(2,1)}, u32[]{:S(2)}, u32[]{:S(2)}) %collective-permute-start) | collective-permute-done | bytes 1835040 | tf_op jit(solution)/shard_map/ppermute | solution.py:145
  95.2 6.2 %pad_maximum_fusion = bf16[4,256,3584]{2,1,0:T(8,128)(2,1)} fusion(bf16[1,256,3584]{2,1,0:T(8,128)(2,1)} %bitcast.7, bf16[1,256,3584]{2,1,0:T(8,128)(2,1)} %bitcast.6, bf16[1,256,3584]{2,1,0:T(8,128)(2,1)} %bitcast.5, bf16[1,256,3584]{2,1,0:T(8,128)(2,1)S(1)} %fusion.13), kind=kLoop, calls=%fused_computation.3 | loop fusion | flops 11010048 | bytes 14680064 | tf_op jit(solution)/shard_map/stack | solution.py:146
  101.4 7.1 %gather_fusion = bf16[4,256,3584]{2,1,0:T(8,128)(2,1)} fusion(bf16[4,256,3584]{2,1,0:T(8,128)(2,1)} %pad_maximum_fusion, s32[1024]{0:T(1024)S(1)} %pad_clamp_fusion), kind=kCustom, calls=%fused_computation | custom fusion | bytes 14680080 | tf_op jit(solution)/shard_map/jit(_take)/gather | solution.py:148
  108.5 6.9 %broadcast_select_fusion = bf16[4,256,3584]{2,1,0:T(8,128)(2,1)} fusion(bf16[4,256,3584]{2,1,0:T(8,128)(2,1)} %gather_fusion, pred[4]{0:T(512)(128)(4,1)S(1)} %compare_and_fusion), kind=kLoop, calls=%fused_computation.4 | loop fusion | flops 3670016 | bytes 14680068 | tf_op jit(solution)/shard_map/jit(_take)/select_n | solution.py:148
  115.4 12.7 %copy.24 = bf16[32,448,288]{1,0,2:T(8,128)(2,1)} copy(bf16[32,448,288]{1,2,0:T(8,128)(2,1)} %all-gather.7.cloned.1.call-done) | data formatting | bytes 16515072 | tf_op jit(solution)/shard_map/all_gather | solution.py:149
  128.0 19.0 %reshape.230 = bf16[4,3584,288]{1,0,2:T(4,128)(2,1)} reshape(bf16[32,448,288]{1,0,2:T(8,128)(2,1)} %copy.24) | data formatting | bytes 16515072 | tf_op jit(solution)/shard_map/reshape | solution.py:150
  147.0 13.4 %add_convert_fusion = bf16[1024,4,288]{0,2,1:T(8,128)(2,1)S(1)} fusion(f32[4,288]{1,0:T(4,128)S(1)} %bitcast.48, bf16[1024,3584,1]{1,0,2:T(8,128)(2,1)} %bitcast.41, bf16[4,3584,288]{1,0,2:T(4,128)(2,1)} %reshape.230), kind=kOutput, calls=%fused_computation.5 | convolution fusion | flops 8458076160 | bytes 17961472 | tf_op jit(solution)/shard_map/td,ydc->tyc/dot_general | solution.py:151
  160.4 3.8 %copy.26 = bf16[1024,4,288]{2,1,0:T(4,128)(2,1)} copy(bf16[1024,4,288]{0,2,1:T(8,128)(2,1)S(1)} %add_convert_fusion) | data formatting | bytes 4718592 | tf_op jit(solution)/shard_map/convert_element_type | solution.py:159
  164.3 5.5 %all-to-all-start = ((bf16[1024,4,288]{2,1,0:T(4,128)(2,1)}), bf16[1024,4,288]{2,1,0:T(4,128)(2,1)S(1)}, u32[]{:S(2)}, u32[]{:S(2)}) async-start(bf16[1024,4,288]{2,1,0:T(4,128)(2,1)} %copy.26), calls=%async_computation | async-start | bytes 6291456 | tf_op jit(solution)/shard_map/all_to_all | solution.py:160
  170.4 34.2 %all-to-all-done = bf16[1024,4,288]{2,1,0:T(4,128)(2,1)S(1)} async-done(((bf16[1024,4,288]{2,1,0:T(4,128)(2,1)}), bf16[1024,4,288]{2,1,0:T(4,128)(2,1)S(1)}, u32[]{:S(2)}, u32[]{:S(2)}) %all-to-all-start) | async-done | bytes 2359328 | tf_op jit(solution)/shard_map/all_to_all | solution.py:160
  204.5 4.2 %copy.27 = bf16[4,256,4,288]{1,3,0,2:T(8,128)(2,1)} copy(bf16[4,256,4,288]{3,2,1,0:T(4,128)(2,1)S(1)} %bitcast.38) | data formatting | bytes 4718592 | tf_op jit(solution)/shard_map/all_to_all | solution.py:160
  208.7 1.2 fusion.11
  210.1 0.9 pad_maximum_fusion.2
  211.0 0.6 fusion.9
  214.2 0.6 pad_add_fusion.meta
  214.9 1.3 slice.38
  216.2 1.0 copy.30
  217.2 1.9 convert.18
  219.2 0.6 subtract_convert_fusion
  219.8 1.4 pad_maximum_fusion.1
  221.2 67.9 %all-gather.5.cloned.1.call-done = bf16[4096,1024]{0,1:T(8,128)(2,1)} async-done(((bf16[256,1024]{0,1:T(8,128)(2,1)}), bf16[4096,1024]{0,1:T(8,128)(2,1)}) %all-gather.5.cloned.1.call-update) | async-done | bytes 8388624 | tf_op jit(solution)/shard_map/all_gather | solution.py:184
  289.0 5.9 %slice_bitcast_fusion = (bf16[512,4096]{1,0:T(8,128)(2,1)}, bf16[4096,512]{0,1:T(8,128)(2,1)}) fusion(bf16[4096,1024]{0,1:T(8,128)(2,1)} %all-gather.5.cloned.1.call-done), kind=kLoop, calls=%fused_computation.8 | loop fusion | bytes 16777216 | tf_op jit(solution)/shard_map/transpose | solution.py:191
  294.9 6.5 %copy.28.k_ref = bf16[4096,512]{1,0:T(8,128)(2,1)} copy(bf16[4096,512]{0,1:T(8,128)(2,1)} %get-tuple-element.11) | data formatting | bytes 8388608 | tf_op jit(solution)/shard_map/slice | solution.py:192
  301.4 38.6 %shard_map.68 = bf16[3584,256]{1,0:T(8,128)(2,1)} custom-call(s32[8]{0:T(128)} %pad_add_fusion.meta, bf16[3584,256]{1,0:T(8,128)(2,1)} %bitcast.42, bf16[4096,512]{1,0:T(8,128)(2,1)} %copy.28.k_ref, bf16[512,4096]{1,0:T(8,128)(2,1)} %get-tuple-element.10.v_ref), custom_call_target="tpu_custom_call" | custom-call | tf_op jit(solution)/shard_map/pallas_call | solution.py:103
  340.0 3.8 %copy.29 = bf16[256,3584]{1,0:T(8,128)(2,1)} copy(bf16[256,3584]{0,1:T(8,128)(2,1)} %bitcast.43) | data formatting | bytes 3670016
  (35 shorter events, 1.0 us)
Async XLA Ops:
  7.2 8.8 %copy-start = (bf16[256,3584]{1,0:T(8,128)(2,1)S(1)}, bf16[256,3584]{1,0:T(8,128)(2,1)}, u32[]{:S(2)}) copy-start(bf16[256,3584]{1,0:T(8,128)(2,1)} %param.5) | copy-start | bytes 5505028
  7.2 8.8 %copy-start.3 = (f32[3584]{0:T(1024)S(1)}, f32[3584]{0:T(1024)}, u32[]{:S(2)}) copy-start(f32[3584]{0:T(1024)} %param.7) | copy-start | bytes 43012
  7.2 8.6 %copy-start.4 = (f32[4608]{0:T(1024)S(1)}, f32[4608]{0:T(1024)}, u32[]{:S(2)}) copy-start(f32[4608]{0:T(1024)} %param.9) | copy-start | bytes 55300
  7.2 108.2 %all-gather.7.cloned.1.call-start = ((), (), s32[]{:S(2)}) async-start(), calls=%async_computation.2 | async-start | bytes 9732096 | tf_op jit(solution)/shard_map/all_gather | solution.py:149
  13.1 44.7 %collective-permute-start.1 = (bf16[256,3584]{1,0:T(8,128)(2,1)}, bf16[256,3584]{1,0:T(8,128)(2,1)}, u32[]{:S(2)}, u32[]{:S(2)}) collective-permute-start(bf16[256,3584]{1,0:T(8,128)(2,1)} %fusion.4), channel_id=1, source_target_pairs={{0,2},{1,3},{2,0},{3,1},{4,6},{5,7},{6,4},{7,5},{8,10},{9,11},{10,... | collective-permute-start | bytes 5505032 | tf_op jit(solution)/shard_map/ppermute | solution.py:145
  13.6 81.6 %collective-permute-start = (bf16[256,3584]{1,0:T(8,128)(2,1)}, bf16[256,3584]{1,0:T(8,128)(2,1)}, u32[]{:S(2)}, u32[]{:S(2)}) collective-permute-start(bf16[256,3584]{1,0:T(8,128)(2,1)} %fusion.4), channel_id=1, source_target_pairs={{0,1},{1,2},{2,3},{3,0},{4,5},{5,6},{6,7},{7,4},{8,9},{9,10},{10,1... | collective-permute-start | bytes 5505032 | tf_op jit(solution)/shard_map/ppermute | solution.py:145
  15.7 79.5 %collective-permute-start.2 = (bf16[256,3584]{1,0:T(8,128)(2,1)}, bf16[256,3584]{1,0:T(8,128)(2,1)}, u32[]{:S(2)}, u32[]{:S(2)}) collective-permute-start(bf16[256,3584]{1,0:T(8,128)(2,1)} %fusion.4), channel_id=1, source_target_pairs={{0,3},{1,0},{2,1},{3,2},{4,7},{5,4},{6,5},{7,6},{8,11},{9,8},{10,9... | collective-permute-start | bytes 5505032 | tf_op jit(solution)/shard_map/ppermute | solution.py:145
  164.2 5.5 %copy-start.5 = (s32[1,4]{1,0:T(1,128)S(1)}, s32[1,4]{1,0:T(1,128)}, u32[]{:S(2)}) copy-start(s32[1,4]{1,0:T(1,128)} %param.6) | copy-start | bytes 52
  164.3 40.3 %all-to-all-start = ((bf16[1024,4,288]{2,1,0:T(4,128)(2,1)}), bf16[1024,4,288]{2,1,0:T(4,128)(2,1)S(1)}, u32[]{:S(2)}, u32[]{:S(2)}) async-start(bf16[1024,4,288]{2,1,0:T(4,128)(2,1)} %copy.26), calls=%async_computation | async-start | bytes 6291456 | tf_op jit(solution)/shard_map/all_to_all | solution.py:160
  169.7 119.3 %all-gather.5.cloned.1.call-start = ((), (), s32[]{:S(2)}) async-start(), calls=%async_computation.1 | async-start | bytes 8912896 | tf_op jit(solution)/shard_map/all_gather | solution.py:184
  208.7 6.2 %copy-start.1 = (bf16[4,256,4,288]{1,3,0,2:T(8,128)(2,1)S(1)}, bf16[4,256,4,288]{1,3,0,2:T(8,128)(2,1)}, u32[]{:S(2)}) copy-start(bf16[4,256,4,288]{1,3,0,2:T(8,128)(2,1)} %copy.27) | copy-start | bytes 7077892
  210.9 5.3 %copy-start.2 = (bf16[256,1024]{0,1:T(8,128)(2,1)S(1)}, bf16[256,1024]{0,1:T(8,128)(2,1)}, u32[]{:S(2)}) copy-start(bf16[256,1024]{0,1:T(8,128)(2,1)} %pad_maximum_fusion.2) | copy-start | bytes 1572868
Sparse Core Ops, SparseCore 0:
  10.3 57.3 all-gather.6
  211.1 77.8 all-gather.4

commit v2 on v0

--- a/solution.py
+++ b/solution.py
@@ -138,7 +138,15 @@
     rows, width = normed.shape[0], weight.shape[1]
     n_x = lax.axis_size("x")
     n_y = lax.axis_size("y")
-    grouped = lax.all_gather(normed, "x", axis=0, tiled=True)
+    here = lax.axis_index("x")
+    shifted = [normed]
+    for step in range(1, n_x):
+        pairs = [(s, (s + step) % n_x) for s in range(n_x)]
+        shifted.append(lax.ppermute(normed, "x", pairs))
+    grouped = jnp.zeros((n_x * rows, normed.shape[1]), normed.dtype)
+    for step, piece in enumerate(shifted):
+        at = ((here - step) % n_x) * rows
+        grouped = lax.dynamic_update_slice_in_dim(grouped, piece, at, 0)
     pieces = lax.all_gather(weight, ("z", "c", "y"), axis=0, tiled=False)
     pieces = pieces.reshape(-1, n_y, weight.shape[0], width)
     summed = jnp.einsum(

time: 349 us -> 310 us (0.89)
  the two profiles are of different devices: /device:TPU:28 before, /device:TPU:14 now
where the time goes in v2:
time: 310 us; the launch traced here: 306 us
  waiting for transfers between devices  168 us (54%)
  local copies, waits for them, and re-layouts  51.6 us (17%)
  Pallas kernels  34.4 us (11%)
  between operations  16.8 us (5%)
  matrix products  13.1 us (4%)
  starting transfers between devices  11.6 us (4%)
  other arithmetic  10.7 us (3%)
    all_gather x1, waiting for transfers between devices, on_device(): piece = lax.all_gather(kv_rows, ('y', 'x'), axis=0, tiled=True)  67.4 us
    ppermute x3, waiting for transfers between devices, project_joined(): shifted.append(lax.ppermute(normed, 'x', pairs))  65.1 us
    pallas_call x1, Pallas kernels, flash(): pl.pallas_call(flash_body, grid_spec=spec, out_shape=jax.ShapeDtypeStruct...  34.4 us
    all_to_all x1, waiting for transfers between devices, project_joined(): lax.all_to_all(block_out, 'x', split_axis=0, concat_axis=1, tiled=True)  34.3 us
    dot_general x1, matrix products, project_joined(): jnp.einsum('tie,iyec->tyc', grouped.reshape(grouped.shape[0], pieces.shap...  13.1 us
    ppermute x3, local copies, waits for them, and re-layouts, project_joined(): shifted.append(lax.ppermute(normed, 'x', pairs))  11.7 us
    unnamed x21, local copies, waits for them, and re-layouts  8.99 us
    all_to_all x1, starting transfers between devices, project_joined(): lax.all_to_all(block_out, 'x', split_axis=0, concat_axis=1, tiled=True)  8.58 us
  transfers between devices with their start and end apart: 6, of which 4 were waited for; matrix products, arithmetic and copies ran while one was open for 10% of the time, Pallas kernels for 0%

profile of v2, /device:TPU:14, one launch (start us, length us, event | category | flops | bytes accessed | tf_op | source)
XLA Modules:
  0.0 305.8 jit_solution(2645947785435331931)
XLA Ops:
  7.2 0.7 all-gather.7.cloned.1.call-update
  7.9 1.9 fusion.1
  9.9 2.0 fusion.3
  12.4 2.4 collective-permute-start.1
  14.9 2.2 copy.34
  17.3 0.9 broadcast_in_dim.31
  19.1 2.9 copy-done.5
  22.0 33.0 %collective-permute-done = bf16[256,3584]{1,0:T(8,128)(2,1)} collective-permute-done((bf16[256,3584]{1,0:T(8,128)(2,1)S(1)}, bf16[256,3584]{1,0:T(8,128)(2,1)}, u32[]{:S(2)}, u32[]{:S(2)}) %collective-permute-start) | collective-permute-done | bytes 1835040 | tf_op jit(solution)/shard_map/ppermute | solution.py:145
  54.9 3.8 %copy.35 = bf16[256,3584]{0,1:T(8,128)(2,1)} copy(bf16[256,3584]{1,0:T(8,128)(2,1)} %collective-permute-done) | data formatting | bytes 3670016 | tf_op jit(solution)/shard_map/ppermute | solution.py:145
  58.7 4.0 %copy.36 = bf16[256,3584]{0,1:T(8,128)(2,1)} copy(bf16[256,3584]{1,0:T(8,128)(2,1)} %collective-permute-done.1) | data formatting | bytes 3670016 | tf_op jit(solution)/shard_map/ppermute | solution.py:145
  62.7 32.1 %collective-permute-done.2 = bf16[256,3584]{1,0:T(8,128)(2,1)} collective-permute-done((bf16[256,3584]{1,0:T(8,128)(2,1)S(1)}, bf16[256,3584]{1,0:T(8,128)(2,1)}, u32[]{:S(2)}, u32[]{:S(2)}) %collective-permute-start.2) | collective-permute-done | bytes 1835040 | tf_op jit(solution)/shard_map/ppermute | solution.py:145
  94.8 3.9 %copy.37 = bf16[256,3584]{0,1:T(8,128)(2,1)} copy(bf16[256,3584]{1,0:T(8,128)(2,1)} %collective-permute-done.2) | data formatting | bytes 3670016 | tf_op jit(solution)/shard_map/ppermute | solution.py:145
  98.8 1.5 constant_dynamic-update-slice_fusion.2
  100.3 0.7 copy-done.3
  101.0 1.4 constant_dynamic-update-slice_fusion.1
  102.4 1.5 constant_dynamic-update-slice_fusion
  103.9 13.1 %fusion = bf16[1024,4,288]{0,2,1:T(8,128)(2,1)S(1)} fusion(f32[4,288]{1,0:T(4,128)S(1)} %bitcast.50, bf16[1024,8,448,1]{0,2,3,1:T(8,128)(2,1)} %bitcast.43, bf16[8,4,448,288]{2,3,1,0:T(8,128)(2,1)} %bitcast.55), kind=kOutput, calls=%fused_computation.1 | convolution fusion | flops 8458076160 | bytes 17961472 | tf_op jit(solution)/shard_map/tie,iyec->tyc/dot_general | solution.py:152
  117.0 3.8 %copy.39 = bf16[1024,4,288]{2,1,0:T(4,128)(2,1)} copy(bf16[1024,4,288]{0,2,1:T(8,128)(2,1)S(1)} %fusion) | data formatting | bytes 4718592 | tf_op jit(solution)/shard_map/convert_element_type | solution.py:160
  120.9 8.6 %all-to-all-start = ((bf16[1024,4,288]{2,1,0:T(4,128)(2,1)}), bf16[1024,4,288]{2,1,0:T(4,128)(2,1)S(1)}, u32[]{:S(2)}, u32[]{:S(2)}) async-start(bf16[1024,4,288]{2,1,0:T(4,128)(2,1)} %copy.39), calls=%async_computation | async-start | bytes 6291456 | tf_op jit(solution)/shard_map/all_to_all | solution.py:161
  130.1 34.3 %all-to-all-done = bf16[1024,4,288]{2,1,0:T(4,128)(2,1)S(1)} async-done(((bf16[1024,4,288]{2,1,0:T(4,128)(2,1)}), bf16[1024,4,288]{2,1,0:T(4,128)(2,1)S(1)}, u32[]{:S(2)}, u32[]{:S(2)}) %all-to-all-start) | async-done | bytes 2359328 | tf_op jit(solution)/shard_map/all_to_all | solution.py:161
  164.4 4.2 %copy.40 = bf16[4,256,4,288]{1,3,0,2:T(8,128)(2,1)} copy(bf16[4,256,4,288]{3,2,1,0:T(4,128)(2,1)S(1)} %bitcast.40) | data formatting | bytes 4718592 | tf_op jit(solution)/shard_map/all_to_all | solution.py:161
  168.5 1.2 fusion.5
  169.9 0.8 pad_maximum_fusion.1
  174.7 1.3 slice.36
  176.0 1.0 copy.43
  177.0 1.9 convert.18
  179.6 1.4 pad_maximum_fusion
  181.0 67.4 %all-gather.5.cloned.1.call-done = bf16[4096,1024]{0,1:T(8,128)(2,1)} async-done(((bf16[256,1024]{0,1:T(8,128)(2,1)}), bf16[4096,1024]{0,1:T(8,128)(2,1)}) %all-gather.5.cloned.1.call-update) | async-done | bytes 8388624 | tf_op jit(solution)/shard_map/all_gather | solution.py:185
  248.4 5.9 %slice_bitcast_fusion = (bf16[512,4096]{1,0:T(8,128)(2,1)}, bf16[4096,512]{0,1:T(8,128)(2,1)}) fusion(bf16[4096,1024]{0,1:T(8,128)(2,1)} %all-gather.5.cloned.1.call-done), kind=kLoop, calls=%fused_computation.4 | loop fusion | bytes 16777216 | tf_op jit(solution)/shard_map/transpose | solution.py:192
  254.3 6.5 %copy.41.k_ref = bf16[4096,512]{1,0:T(8,128)(2,1)} copy(bf16[4096,512]{0,1:T(8,128)(2,1)} %get-tuple-element.11) | data formatting | bytes 8388608 | tf_op jit(solution)/shard_map/slice | solution.py:193
  260.8 34.4 %shard_map.68 = bf16[3584,256]{1,0:T(8,128)(2,1)} custom-call(s32[8]{0:T(128)} %pad_add_fusion.meta, bf16[3584,256]{1,0:T(8,128)(2,1)} %bitcast.44, bf16[4096,512]{1,0:T(8,128)(2,1)} %copy.41.k_ref, bf16[512,4096]{1,0:T(8,128)(2,1)} %get-tuple-element.10.v_ref), custom_call_target="tpu_custom_call" | custom-call | tf_op jit(solution)/shard_map/pallas_call | solution.py:103
  295.2 3.8 %copy.42 = bf16[256,3584]{1,0:T(8,128)(2,1)} copy(bf16[256,3584]{0,1:T(8,128)(2,1)} %bitcast.45) | data formatting | bytes 3670016
  (41 shorter events, 4.2 us)
Async XLA Ops:
  7.2 96.7 %all-gather.7.cloned.1.call-start = ((), (), s32[]{:S(2)}) async-start(), calls=%async_computation.2 | async-start | bytes 9732096 | tf_op jit(solution)/shard_map/all_gather | solution.py:150
  9.8 7.3 %copy-start.7 = (f32[4608]{0:T(1024)S(1)}, f32[4608]{0:T(1024)}, u32[]{:S(2)}) copy-start(f32[4608]{0:T(1024)} %param.9) | copy-start | bytes 55300
  11.9 43.1 %collective-permute-start = (bf16[256,3584]{1,0:T(8,128)(2,1)S(1)}, bf16[256,3584]{1,0:T(8,128)(2,1)}, u32[]{:S(2)}, u32[]{:S(2)}) collective-permute-start(bf16[256,3584]{1,0:T(8,128)(2,1)S(1)} %fusion.3), channel_id=1, source_target_pairs={{0,1},{1,2},{2,3},{3,0},{4,5},{5,6},{6,7},{7,4},{8,9},{9,10},{10,1... | collective-permute-start | bytes 5505032 | tf_op jit(solution)/shard_map/ppermute | solution.py:145
  12.4 46.3 %collective-permute-start.1 = (bf16[256,3584]{1,0:T(8,128)(2,1)S(1)}, bf16[256,3584]{1,0:T(8,128)(2,1)}, u32[]{:S(2)}, u32[]{:S(2)}) collective-permute-start(bf16[256,3584]{1,0:T(8,128)(2,1)S(1)} %fusion.3), channel_id=1, source_target_pairs={{0,2},{1,3},{2,0},{3,1},{4,6},{5,7},{6,4},{7,5},{8,10},{9,11},{10,... | collective-permute-start | bytes 5505032 | tf_op jit(solution)/shard_map/ppermute | solution.py:145
  14.9 80.0 %collective-permute-start.2 = (bf16[256,3584]{1,0:T(8,128)(2,1)S(1)}, bf16[256,3584]{1,0:T(8,128)(2,1)}, u32[]{:S(2)}, u32[]{:S(2)}) collective-permute-start(bf16[256,3584]{1,0:T(8,128)(2,1)S(1)} %fusion.3), channel_id=1, source_target_pairs={{0,3},{1,0},{2,1},{3,2},{4,7},{5,4},{6,5},{7,6},{8,11},{9,8},{10,9... | collective-permute-start | bytes 5505032 | tf_op jit(solution)/shard_map/ppermute | solution.py:145
  17.3 1.5 copy-start.1
  19.1 2.9 copy-start.5
  94.8 4.0 %copy-start.2 = (bf16[256,3584]{0,1:T(8,128)(2,1)S(1)}, bf16[256,3584]{0,1:T(8,128)(2,1)}, u32[]{:S(2)}) copy-start(bf16[256,3584]{0,1:T(8,128)(2,1)} %copy.35) | copy-start | bytes 5505028
  98.8 2.2 copy-start.3
  98.8 3.6 %copy-start.4 = (bf16[256,3584]{0,1:T(8,128)(2,1)S(1)}, bf16[256,3584]{0,1:T(8,128)(2,1)}, u32[]{:S(2)}) copy-start(bf16[256,3584]{0,1:T(8,128)(2,1)} %copy.37) | copy-start | bytes 5505028
  120.9 8.6 %copy-start.8 = (s32[1,4]{1,0:T(1,128)S(1)}, s32[1,4]{1,0:T(1,128)}, u32[]{:S(2)}) copy-start(s32[1,4]{1,0:T(1,128)} %param.6) | copy-start | bytes 52
  120.9 43.5 %all-to-all-start = ((bf16[1024,4,288]{2,1,0:T(4,128)(2,1)}), bf16[1024,4,288]{2,1,0:T(4,128)(2,1)S(1)}, u32[]{:S(2)}, u32[]{:S(2)}) async-start(bf16[1024,4,288]{2,1,0:T(4,128)(2,1)} %copy.39), calls=%async_computation | async-start | bytes 6291456 | tf_op jit(solution)/shard_map/all_to_all | solution.py:161
  129.4 119.0 %all-gather.5.cloned.1.call-start = ((), (), s32[]{:S(2)}) async-start(), calls=%async_computation.1 | async-start | bytes 8912896 | tf_op jit(solution)/shard_map/all_gather | solution.py:185
  168.5 6.1 %copy-start = (bf16[4,256,4,288]{1,3,0,2:T(8,128)(2,1)S(1)}, bf16[4,256,4,288]{1,3,0,2:T(8,128)(2,1)}, u32[]{:S(2)}) copy-start(bf16[4,256,4,288]{1,3,0,2:T(8,128)(2,1)} %copy.40) | copy-start | bytes 7077892
  170.8 5.3 %copy-start.6 = (bf16[256,1024]{0,1:T(8,128)(2,1)S(1)}, bf16[256,1024]{0,1:T(8,128)(2,1)}, u32[]{:S(2)}) copy-start(bf16[256,1024]{0,1:T(8,128)(2,1)} %pad_maximum_fusion.1) | copy-start | bytes 1572868
Sparse Core Ops, SparseCore 0:
  10.2 57.5 all-gather.6
  170.9 77.4 all-gather.4

commit v3 on v2

--- a/solution.py
+++ b/solution.py
@@ -158,9 +158,11 @@
     bias_block = bias.reshape(n_y, n_x, width)
     bias_block = lax.dynamic_index_in_dim(bias_block, lax.axis_index("x"), 1, keepdims=False)
     block_out = (summed + bias_block[None]).astype(jnp.bfloat16)
-    swapped = lax.all_to_all(block_out, "x", split_axis=0, concat_axis=1, tiled=True)
-    swapped = swapped.reshape(rows, n_x, n_y, width)
-    return jnp.transpose(swapped, (0, 2, 1, 3)).reshape(rows, n_y * n_x * width)
+    tail = lax.all_to_all(block_out[:, n_y - 1], "x", split_axis=0, concat_axis=1, tiled=True)
+    head = block_out[:, : n_y - 1].reshape(block_out.shape[0], -1)
+    head = lax.all_to_all(head, "x", split_axis=0, concat_axis=1, tiled=True)
+    head = jnp.transpose(head.reshape(rows, n_x, n_y - 1, width), (0, 2, 1, 3))
+    return head.reshape(rows, -1), tail
 
 
 def on_device(hidden_in, lengths, attn_norm, qkv_weight, qkv_bias):
@@ -172,16 +174,17 @@
     kdim = KV_HEADS * HEAD_DIM
     group = HEADS // KV_HEADS
     normed = norm_rows(hidden_in, attn_norm)
-    joined = project_joined(normed, qkv_weight, qkv_bias)
+    head, tail = project_joined(normed, qkv_weight, qkv_bias)
+    split = qdim - head.shape[1]
     ends = jnp.cumsum(row_lengths)
     tokens_here = first + jnp.arange(rows, dtype=jnp.int32)
     before = ends[None, :] <= tokens_here[:, None]
     seg_here = jnp.sum(before.astype(jnp.int32), axis=1)
     begin = jnp.sum(jnp.where(before, row_lengths[None, :], 0), axis=1)
     pos = tokens_here - begin
-    queries = rotate(joined[:, :qdim], pos, HEADS).reshape(rows, KV_HEADS, group, HEAD_DIM)
-    keys = rotate(joined[:, qdim : qdim + kdim], pos, KV_HEADS)
-    kv_rows = jnp.concatenate([keys, joined[:, qdim + kdim :]], axis=1)
+    keys = rotate(tail[:, split : split + kdim], pos, KV_HEADS)
+    kv_rows = jnp.concatenate([keys, tail[:, split + kdim :]], axis=1)
+    queries = rotate(jnp.concatenate([head, tail[:, :split]], axis=1), pos, HEADS)
     piece = lax.all_gather(kv_rows, ("y", "x"), axis=0, tiled=True)
     lead = jnp.max(jnp.where(ends <= first, ends, 0))
     meta = jnp.concatenate(

time: 310 us -> 287 us (0.926)
  the two profiles are of different devices: /device:TPU:14 before, /device:TPU:28 now
where the time goes in v3:
time: 287 us; the launch traced here: 285 us
  waiting for transfers between devices  142 us (49%)
  local copies, waits for them, and re-layouts  49.5 us (17%)
  Pallas kernels  38.5 us (13%)
  between operations  16.8 us (6%)
  starting transfers between devices  16.1 us (6%)
  matrix products  13.2 us (5%)
  other arithmetic  9.44 us (3%)
    ppermute x3, waiting for transfers between devices, project_joined(): shifted.append(lax.ppermute(normed, 'x', pairs))  66.8 us
    all_gather x1, waiting for transfers between devices, on_device(): piece = lax.all_gather(kv_rows, ('y', 'x'), axis=0, tiled=True)  47.4 us
    pallas_call x1, Pallas kernels, flash(): pl.pallas_call(flash_body, grid_spec=spec, out_shape=jax.ShapeDtypeStruct...  38.5 us
    all_to_all x1, waiting for transfers between devices, project_joined(): head = lax.all_to_all(head, 'x', split_axis=0, concat_axis=1, tiled=True)  20.7 us
    dot_general x1, matrix products, project_joined(): jnp.einsum('tie,iyec->tyc', grouped.reshape(grouped.shape[0], pieces.shap...  13.2 us
    ppermute x3, local copies, waits for them, and re-layouts, project_joined(): shifted.append(lax.ppermute(normed, 'x', pairs))  11.5 us
    unnamed x31, local copies, waits for them, and re-layouts  10.9 us
    all_to_all x1, starting transfers between devices, project_joined(): head = lax.all_to_all(head, 'x', split_axis=0, concat_axis=1, tiled=True)  6.64 us
  transfers between devices with their start and end apart: 7, of which 5 were waited for; matrix products, arithmetic and copies ran while one was open for 12% of the time, Pallas kernels for 0%

profile of v3, /device:TPU:28, one launch (start us, length us, event | category | flops | bytes accessed | tf_op | source)
XLA Modules:
  0.0 285.4 jit_solution(2675114856980289527)
XLA Ops:
  7.9 1.9 fusion.1
  9.9 2.0 fusion.3
  11.9 1.3 collective-permute-start
  14.0 1.1 collective-permute-start.2
  15.1 2.2 copy.57
  17.8 0.9 broadcast_in_dim.31
  19.6 2.9 %copy-done.4 = bf16[1024,3584]{0,1:T(8,128)(2,1)} copy-done((bf16[1024,3584]{0,1:T(8,128)(2,1)}, bf16[1024,3584]{0,1:T(8,128)(2,1)S(1)}, u32[]{:S(2)}) %copy-start.4) | copy-done | bytes 7340056
  22.5 32.5 %collective-permute-done = bf16[256,3584]{1,0:T(8,128)(2,1)} collective-permute-done((bf16[256,3584]{1,0:T(8,128)(2,1)S(1)}, bf16[256,3584]{1,0:T(8,128)(2,1)}, u32[]{:S(2)}, u32[]{:S(2)}) %collective-permute-start) | collective-permute-done | bytes 1835040 | tf_op jit(solution)/shard_map/ppermute | solution.py:145
  55.0 3.8 %copy.58 = bf16[256,3584]{0,1:T(8,128)(2,1)} copy(bf16[256,3584]{1,0:T(8,128)(2,1)} %collective-permute-done) | data formatting | bytes 3670016 | tf_op jit(solution)/shard_map/ppermute | solution.py:145
  58.8 34.4 %collective-permute-done.1 = bf16[256,3584]{1,0:T(8,128)(2,1)} collective-permute-done((bf16[256,3584]{1,0:T(8,128)(2,1)S(1)}, bf16[256,3584]{1,0:T(8,128)(2,1)}, u32[]{:S(2)}, u32[]{:S(2)}) %collective-permute-start.1) | collective-permute-done | bytes 1835040 | tf_op jit(solution)/shard_map/ppermute | solution.py:145
  93.2 3.8 %copy.59 = bf16[256,3584]{0,1:T(8,128)(2,1)} copy(bf16[256,3584]{1,0:T(8,128)(2,1)} %collective-permute-done.1) | data formatting | bytes 3670016 | tf_op jit(solution)/shard_map/ppermute | solution.py:145
  97.0 3.9 %copy.60 = bf16[256,3584]{0,1:T(8,128)(2,1)} copy(bf16[256,3584]{1,0:T(8,128)(2,1)} %collective-permute-done.2) | data formatting | bytes 3670016 | tf_op jit(solution)/shard_map/ppermute | solution.py:145
  100.9 1.4 constant_dynamic-update-slice_fusion.2
  103.0 1.5 constant_dynamic-update-slice_fusion.1
  104.5 1.4 constant_dynamic-update-slice_fusion
  105.9 13.2 %fusion = bf16[1024,4,288]{0,2,1:T(8,128)(2,1)S(1)} fusion(f32[4,288]{1,0:T(4,128)S(1)} %bitcast.60, bf16[1024,8,448,1]{0,2,3,1:T(8,128)(2,1)} %bitcast.49, bf16[8,4,448,288]{2,3,1,0:T(8,128)(2,1)} %bitcast.65), kind=kOutput, calls=%fused_computation.1 | convolution fusion | flops 8458076160 | bytes 17961472 | tf_op jit(solution)/shard_map/tie,iyec->tyc/dot_general | solution.py:152
  119.1 1.5 copy-done.6
  121.0 0.9 copy.64
  121.9 6.2 %all-to-all-start.1 = ((bf16[4,256,288]{1,2,0:T(8,128)(2,1)}), bf16[4,256,288]{1,2,0:T(8,128)(2,1)S(1)}, u32[]{:S(2)}, u32[]{:S(2)}) async-start(bf16[4,256,288]{1,2,0:T(8,128)(2,1)} %copy.64), calls=%async_computation.1 | async-start | bytes 1179648 | tf_op jit(solution)/shard_map/all_to_all | solution.py:161
  128.4 6.3 %all-to-all-done.1 = bf16[4,256,288]{1,2,0:T(8,128)(2,1)S(1)} async-done(((bf16[4,256,288]{1,2,0:T(8,128)(2,1)}), bf16[4,256,288]{1,2,0:T(8,128)(2,1)S(1)}, u32[]{:S(2)}, u32[]{:S(2)}) %all-to-all-start.1) | async-done | bytes 589856 | tf_op jit(solution)/shard_map/all_to_all | solution.py:161
  135.8 1.6 slice.44
  137.4 1.4 all_to_all.26
  138.8 1.4 copy.62
  140.3 6.6 %all-to-all-start = ((bf16[4,256,864]{1,2,0:T(8,128)(2,1)}), bf16[4,256,864]{1,2,0:T(8,128)(2,1)S(1)}, u32[]{:S(2)}, u32[]{:S(2)}) async-start(bf16[4,256,864]{1,2,0:T(8,128)(2,1)} %copy.62), calls=%async_computation | async-start | bytes 3538944 | tf_op jit(solution)/shard_map/all_to_all | solution.py:163
  151.6 1.0 copy.67
  152.6 20.7 %all-to-all-done = bf16[4,256,864]{1,2,0:T(8,128)(2,1)S(1)} async-done(((bf16[4,256,864]{1,2,0:T(8,128)(2,1)}), bf16[4,256,864]{1,2,0:T(8,128)(2,1)S(1)}, u32[]{:S(2)}, u32[]{:S(2)}) %all-to-all-start) | async-done | bytes 1769504 | tf_op jit(solution)/shard_map/all_to_all | solution.py:163
  175.1 1.4 pad_maximum_fusion.1
  176.5 47.4 %all-gather.5.cloned.1.call-done = bf16[4096,1024]{0,1:T(8,128)(2,1)} async-done(((bf16[256,1024]{0,1:T(8,128)(2,1)}), bf16[4096,1024]{0,1:T(8,128)(2,1)}) %all-gather.5.cloned.1.call-update) | async-done | bytes 8388624 | tf_op jit(solution)/shard_map/all_gather | solution.py:188
  223.8 5.9 %slice_bitcast_fusion = (bf16[512,4096]{1,0:T(8,128)(2,1)}, bf16[4096,512]{0,1:T(8,128)(2,1)}) fusion(bf16[4096,1024]{0,1:T(8,128)(2,1)} %all-gather.5.cloned.1.call-done), kind=kLoop, calls=%fused_computation.4 | loop fusion | bytes 16777216 | tf_op jit(solution)/shard_map/transpose | solution.py:195
  229.8 6.4 %copy.65.k_ref = bf16[4096,512]{1,0:T(8,128)(2,1)} copy(bf16[4096,512]{0,1:T(8,128)(2,1)} %get-tuple-element.15) | data formatting | bytes 8388608 | tf_op jit(solution)/shard_map/slice | solution.py:196
  236.2 38.5 %shard_map.68 = bf16[3584,256]{1,0:T(8,128)(2,1)} custom-call(s32[8]{0:T(128)} %pad_add_fusion.meta, bf16[3584,256]{1,0:T(8,128)(2,1)} %bitcast.50, bf16[4096,512]{1,0:T(8,128)(2,1)} %copy.65.k_ref, bf16[512,4096]{1,0:T(8,128)(2,1)} %get-tuple-element.14.v_ref), custom_call_target="tpu_custom_call" | custom-call | tf_op jit(solution)/shard_map/pallas_call | solution.py:103
  274.8 3.8 %copy.66 = bf16[256,3584]{1,0:T(8,128)(2,1)} copy(bf16[256,3584]{0,1:T(8,128)(2,1)} %bitcast.51) | data formatting | bytes 3670016
  (59 shorter events, 9.2 us)
Async XLA Ops:
  7.2 98.7 %all-gather.7.cloned.1.call-start = ((), (), s32[]{:S(2)}) async-start(), calls=%async_computation.3 | async-start | bytes 9732096 | tf_op jit(solution)/shard_map/all_gather | solution.py:150
  9.8 7.5 %copy-start.13 = (s32[1,4]{1,0:T(1,128)S(1)}, s32[1,4]{1,0:T(1,128)}, u32[]{:S(2)}) copy-start(s32[1,4]{1,0:T(1,128)} %param.6) | copy-start | bytes 52
  9.9 7.7 %copy-start.12 = (f32[4608]{0:T(1024)S(1)}, f32[4608]{0:T(1024)}, u32[]{:S(2)}) copy-start(f32[4608]{0:T(1024)} %param.9) | copy-start | bytes 55300
  11.9 43.1 %collective-permute-start = (bf16[256,3584]{1,0:T(8,128)(2,1)S(1)}, bf16[256,3584]{1,0:T(8,128)(2,1)}, u32[]{:S(2)}, u32[]{:S(2)}) collective-permute-start(bf16[256,3584]{1,0:T(8,128)(2,1)S(1)} %fusion.3), channel_id=1, source_target_pairs={{0,1},{1,2},{2,3},{3,0},{4,5},{5,6},{6,7},{7,4},{8,9},{9,10},{10,1... | collective-permute-start | bytes 5505032 | tf_op jit(solution)/shard_map/ppermute | solution.py:145
  13.2 80.0 %collective-permute-start.1 = (bf16[256,3584]{1,0:T(8,128)(2,1)S(1)}, bf16[256,3584]{1,0:T(8,128)(2,1)}, u32[]{:S(2)}, u32[]{:S(2)}) collective-permute-start(bf16[256,3584]{1,0:T(8,128)(2,1)S(1)} %fusion.3), channel_id=1, source_target_pairs={{0,2},{1,3},{2,0},{3,1},{4,6},{5,7},{6,4},{7,5},{8,10},{9,11},{10,... | collective-permute-start | bytes 5505032 | tf_op jit(solution)/shard_map/ppermute | solution.py:145
  14.0 83.0 %collective-permute-start.2 = (bf16[256,3584]{1,0:T(8,128)(2,1)S(1)}, bf16[256,3584]{1,0:T(8,128)(2,1)}, u32[]{:S(2)}, u32[]{:S(2)}) collective-permute-start(bf16[256,3584]{1,0:T(8,128)(2,1)S(1)} %fusion.3), channel_id=1, source_target_pairs={{0,3},{1,0},{2,1},{3,2},{4,7},{5,4},{6,5},{7,6},{8,11},{9,8},{10,9... | collective-permute-start | bytes 5505032 | tf_op jit(solution)/shard_map/ppermute | solution.py:145
  17.8 1.5 copy-start
  19.6 2.9 %copy-start.4 = (bf16[1024,3584]{0,1:T(8,128)(2,1)}, bf16[1024,3584]{0,1:T(8,128)(2,1)S(1)}, u32[]{:S(2)}) copy-start(bf16[1024,3584]{0,1:T(8,128)(2,1)S(1)} %constant_dynamic-update-slice_fusion.3) | copy-start | bytes 22020100
  97.0 3.9 %copy-start.1 = (bf16[256,3584]{0,1:T(8,128)(2,1)S(1)}, bf16[256,3584]{0,1:T(8,128)(2,1)}, u32[]{:S(2)}) copy-start(bf16[256,3584]{0,1:T(8,128)(2,1)} %copy.58) | copy-start | bytes 5505028
  100.9 2.2 copy-start.2
  100.9 3.6 %copy-start.3 = (bf16[256,3584]{0,1:T(8,128)(2,1)S(1)}, bf16[256,3584]{0,1:T(8,128)(2,1)}, u32[]{:S(2)}) copy-start(bf16[256,3584]{0,1:T(8,128)(2,1)} %copy.60) | copy-start | bytes 5505028
  119.1 1.5 copy-start.6
  121.9 12.8 %all-to-all-start.1 = ((bf16[4,256,288]{1,2,0:T(8,128)(2,1)}), bf16[4,256,288]{1,2,0:T(8,128)(2,1)S(1)}, u32[]{:S(2)}, u32[]{:S(2)}) async-start(bf16[4,256,288]{1,2,0:T(8,128)(2,1)} %copy.64), calls=%async_computation.1 | async-start | bytes 1179648 | tf_op jit(solution)/shard_map/all_to_all | solution.py:161
  128.1 95.7 %all-gather.5.cloned.1.call-start = ((), (), s32[]{:S(2)}) async-start(), calls=%async_computation.2 | async-start | bytes 8912896 | tf_op jit(solution)/shard_map/all_gather | solution.py:188
  128.4 7.4 %copy-start.8 = (f32[256,64]{0,1:T(8,128)}, f32[256,64]{0,1:T(8,128)S(1)}, u32[]{:S(2)}) copy-start(f32[256,64]{0,1:T(8,128)S(1)} %get-tuple-element.22) | copy-start | bytes 196612
  128.4 7.3 %copy-start.10 = (f32[256,64]{0,1:T(8,128)}, f32[256,64]{0,1:T(8,128)S(1)}, u32[]{:S(2)}) copy-start(f32[256,64]{0,1:T(8,128)S(1)} %get-tuple-element.23) | copy-start | bytes 196612
  134.7 1.0 copy-start.7
  140.3 11.4 %copy-start.5 = (bf16[256,1024]{0,1:T(8,128)(2,1)S(1)}, bf16[256,1024]{0,1:T(8,128)(2,1)}, u32[]{:S(2)}) copy-start(bf16[256,1024]{0,1:T(8,128)(2,1)} %pad_maximum_fusion.2) | copy-start | bytes 1572868
  140.3 33.1 %all-to-all-start = ((bf16[4,256,864]{1,2,0:T(8,128)(2,1)}), bf16[4,256,864]{1,2,0:T(8,128)(2,1)S(1)}, u32[]{:S(2)}, u32[]{:S(2)}) async-start(bf16[4,256,864]{1,2,0:T(8,128)(2,1)} %copy.62), calls=%async_computation | async-start | bytes 3538944 | tf_op jit(solution)/shard_map/all_to_all | solution.py:163
  173.6 0.8 copy-start.9
  173.6 0.9 copy-start.11
Sparse Core Ops, SparseCore 0:
  10.2 57.3 all-gather.6
  135.9 87.8 all-gather.4

commit v4 on v3

--- a/solution.py
+++ b/solution.py
@@ -42,15 +42,18 @@
         allowed = (krow >= qstart) & (krow <= qcol)
         bias_ref[...] = jnp.where(allowed, 0.0, -1e30).astype(jnp.float32)
         keys = k_ref[...]
-        values = v_ref[...]
+        values = jnp.transpose(v_ref[...].astype(jnp.float32)).astype(jnp.bfloat16)
         scale = 1.0 / HEAD_DIM**0.5
         for h in range(group):
             heads = slice(h * HEAD_DIM, (h + 1) * HEAD_DIM)
             for c in range(BLOCK // LANES):
                 cols = slice(c * LANES, (c + 1) * LANES)
-                q = q_ref[heads, cols]
+                q = q_ref[cols, heads]
                 scores = (
-                    jnp.dot(keys, q, preferred_element_type=jnp.float32) * scale
+                    lax.dot_general(
+                        keys, q, (((1,), (1,)), ((), ())), preferred_element_type=jnp.float32
+                    )
+                    * scale
                     + bias_ref[:, cols]
                 )
                 m_prev = m_ref[h, :, cols]
@@ -68,13 +71,13 @@
     @pl.when(step == last)
     def _():
         for h in range(group):
-            o_ref[h * HEAD_DIM : (h + 1) * HEAD_DIM, :] = (acc_ref[h] / l_ref[h]).astype(
-                o_ref.dtype
-            )
-
-
-def flash(meta, queries_t, keys, values_t, steps):
-    rows = queries_t.shape[1]
+            o_ref[:, h * HEAD_DIM : (h + 1) * HEAD_DIM] = jnp.transpose(
+                acc_ref[h] / l_ref[h]
+            ).astype(o_ref.dtype)
+
+
+def flash(meta, queries, kv_all, steps):
+    rows = queries.shape[0]
     group = HEADS // KV_HEADS
     width = group * HEAD_DIM
 
@@ -82,17 +85,17 @@
         return (jnp.minimum(meta[5] + t, meta[4]), g)
 
     def value_map(g, t, meta):
-        return (g, jnp.minimum(meta[5] + t, meta[4]))
+        return (jnp.minimum(meta[5] + t, meta[4]), KV_HEADS + g)
 
     spec = pltpu.PrefetchScalarGridSpec(
         num_scalar_prefetch=1,
         grid=(KV_HEADS, steps),
         in_specs=[
-            pl.BlockSpec((width, rows), lambda g, t, meta: (g, 0)),
+            pl.BlockSpec((rows, width), lambda g, t, meta: (0, g)),
             pl.BlockSpec((BLOCK, HEAD_DIM), key_map),
-            pl.BlockSpec((HEAD_DIM, BLOCK), value_map),
+            pl.BlockSpec((BLOCK, HEAD_DIM), value_map),
         ],
-        out_specs=pl.BlockSpec((width, rows), lambda g, t, meta: (g, 0)),
+        out_specs=pl.BlockSpec((rows, width), lambda g, t, meta: (0, g)),
         scratch_shapes=[
             pltpu.VMEM((BLOCK, rows), jnp.float32),
             pltpu.VMEM((group, 1, rows), jnp.float32),
@@ -103,9 +106,9 @@
     return pl.pallas_call(
         flash_body,
         grid_spec=spec,
-        out_shape=jax.ShapeDtypeStruct((HEADS * HEAD_DIM, rows), jnp.bfloat16),
+        out_shape=jax.ShapeDtypeStruct((rows, HEADS * HEAD_DIM), jnp.bfloat16),
         compiler_params=pltpu.CompilerParams(dimension_semantics=("arbitrary", "arbitrary")),
-    )(meta, queries_t, keys, values_t)
+    )(meta, queries, kv_all, kv_all)
 
 
 def norm_rows(values, gain):
@@ -191,9 +194,7 @@
         [ends, jnp.stack([gy_index, lead // BLOCK, 0, 0]).astype(jnp.int32)]
     ).astype(jnp.int32)
     steps = min(piece.shape[0] // BLOCK, 9)
-    queries_t = jnp.transpose(queries.reshape(rows, qdim))
-    values_t = jnp.transpose(piece[:, kdim:])
-    attn = jnp.transpose(flash(meta, queries_t, piece[:, :kdim], values_t, steps))
+    attn = flash(meta, queries, piece, steps)
     return (attn, kv_rows)
 
 

time: 287 us -> 272 us (0.948)
  the two profiles are of different devices: /device:TPU:28 before, /device:TPU:121 now
where the time goes in v4:
time: 272 us; the launch traced here: 271 us
  waiting for transfers between devices  139 us (51%)
  Pallas kernels  46 us (17%)
  local copies, waits for them, and re-layouts  36.7 us (13%)
  between operations  17.1 us (6%)
  matrix products  13.2 us (5%)
  starting transfers between devices  12.2 us (4%)
  other arithmetic  7.35 us (3%)
    ppermute x3, waiting for transfers between devices, project_joined(): shifted.append(lax.ppermute(normed, 'x', pairs))  66.5 us
    pallas_call x1, Pallas kernels, flash(): pl.pallas_call(flash_body, grid_spec=spec, out_shape=jax.ShapeDtypeStruct...  46 us
    all_gather x1, waiting for transfers between devices, on_device(): piece = lax.all_gather(kv_rows, ('y', 'x'), axis=0, tiled=True)  40.3 us
    all_to_all x1, waiting for transfers between devices, project_joined(): head = lax.all_to_all(head, 'x', split_axis=0, concat_axis=1, tiled=True)  23.6 us
    dot_general x1, matrix products, project_joined(): jnp.einsum('tie,iyec->tyc', grouped.reshape(grouped.shape[0], pieces.shap...  13.2 us
    ppermute x3, local copies, waits for them, and re-layouts, project_joined(): shifted.append(lax.ppermute(normed, 'x', pairs))  11.5 us
    all_to_all x1, waiting for transfers between devices, project_joined(): lax.all_to_all(block_out[:, n_y - 1], 'x', split_axis=0, concat_axis=1, t...  7.83 us
    unnamed x35, local copies, waits for them, and re-layouts  7.76 us
  transfers between devices with their start and end apart: 7, of which 5 were waited for; matrix products, arithmetic and copies ran while one was open for 12% of the time, Pallas kernels for 0%

profile of v4, /device:TPU:121, one launch (start us, length us, event | category | flops | bytes accessed | tf_op | source)
XLA Modules:
  0.0 271.4 jit_solution(16695092427665150737)
XLA Ops:
  7.9 2.1 fusion.1
  10.5 1.3 collective-permute-start
  11.8 2.5 collective-permute-start.1
  14.3 1.2 collective-permute-start.2
  15.4 2.2 copy.53
  18.1 0.9 broadcast_in_dim.31
  19.9 2.9 %copy-done.4 = bf16[1024,3584]{0,1:T(8,128)(2,1)} copy-done((bf16[1024,3584]{0,1:T(8,128)(2,1)}, bf16[1024,3584]{0,1:T(8,128)(2,1)S(1)}, u32[]{:S(2)}) %copy-start.4) | copy-done | bytes 7340056
  22.8 30.0 %collective-permute-done = bf16[256,3584]{1,0:T(8,128)(2,1)} collective-permute-done((bf16[256,3584]{1,0:T(8,128)(2,1)S(1)}, bf16[256,3584]{1,0:T(8,128)(2,1)}, u32[]{:S(2)}, u32[]{:S(2)}) %collective-permute-start) | collective-permute-done | bytes 1835040 | tf_op jit(solution)/shard_map/ppermute | solution.py:148
  52.8 3.8 %copy.54 = bf16[256,3584]{0,1:T(8,128)(2,1)} copy(bf16[256,3584]{1,0:T(8,128)(2,1)} %collective-permute-done) | data formatting | bytes 3670016 | tf_op jit(solution)/shard_map/ppermute | solution.py:148
  56.6 36.5 %collective-permute-done.1 = bf16[256,3584]{1,0:T(8,128)(2,1)} collective-permute-done((bf16[256,3584]{1,0:T(8,128)(2,1)S(1)}, bf16[256,3584]{1,0:T(8,128)(2,1)}, u32[]{:S(2)}, u32[]{:S(2)}) %collective-permute-start.1) | collective-permute-done | bytes 1835040 | tf_op jit(solution)/shard_map/ppermute | solution.py:148
  93.1 3.8 %copy.55 = bf16[256,3584]{0,1:T(8,128)(2,1)} copy(bf16[256,3584]{1,0:T(8,128)(2,1)} %collective-permute-done.1) | data formatting | bytes 3670016 | tf_op jit(solution)/shard_map/ppermute | solution.py:148
  97.0 3.9 %copy.56 = bf16[256,3584]{0,1:T(8,128)(2,1)} copy(bf16[256,3584]{1,0:T(8,128)(2,1)} %collective-permute-done.2) | data formatting | bytes 3670016 | tf_op jit(solution)/shard_map/ppermute | solution.py:148
  100.9 1.4 constant_dynamic-update-slice_fusion.2
  102.3 0.8 copy-done.2
  103.0 1.4 constant_dynamic-update-slice_fusion.1
  104.5 0.7 copy-done.3
  105.2 1.4 constant_dynamic-update-slice_fusion
  106.6 13.2 %fusion = bf16[1024,4,288]{0,2,1:T(8,128)(2,1)S(1)} fusion(f32[4,288]{1,0:T(4,128)S(1)} %bitcast.58, bf16[1024,8,448,1]{0,2,3,1:T(8,128)(2,1)} %bitcast.48, bf16[8,4,448,288]{2,3,1,0:T(8,128)(2,1)} %bitcast.63), kind=kOutput, calls=%fused_computation.1 | convolution fusion | flops 8458076160 | bytes 17961472 | tf_op jit(solution)/shard_map/tie,iyec->tyc/dot_general | solution.py:155
  119.8 1.5 copy-done.6
  121.8 0.9 copy.60
  122.7 3.5 %all-to-all-start.1 = ((bf16[4,256,288]{1,2,0:T(8,128)(2,1)}), bf16[4,256,288]{1,2,0:T(8,128)(2,1)S(1)}, u32[]{:S(2)}, u32[]{:S(2)}) async-start(bf16[4,256,288]{1,2,0:T(8,128)(2,1)} %copy.60), calls=%async_computation.1 | async-start | bytes 1179648 | tf_op jit(solution)/shard_map/all_to_all | solution.py:164
  126.7 7.8 %all-to-all-done.1 = bf16[4,256,288]{1,2,0:T(8,128)(2,1)S(1)} async-done(((bf16[4,256,288]{1,2,0:T(8,128)(2,1)}), bf16[4,256,288]{1,2,0:T(8,128)(2,1)S(1)}, u32[]{:S(2)}, u32[]{:S(2)}) %all-to-all-start.1) | async-done | bytes 589856 | tf_op jit(solution)/shard_map/all_to_all | solution.py:164
  136.2 0.9 pad_maximum_fusion.2
  137.1 1.6 slice.36
  138.7 1.4 all_to_all.26
  140.1 1.4 copy.58
  141.6 3.8 %all-to-all-start = ((bf16[4,256,864]{1,2,0:T(8,128)(2,1)}), bf16[4,256,864]{1,2,0:T(8,128)(2,1)S(1)}, u32[]{:S(2)}, u32[]{:S(2)}) async-start(bf16[4,256,864]{1,2,0:T(8,128)(2,1)} %copy.58), calls=%async_computation | async-start | bytes 3538944 | tf_op jit(solution)/shard_map/all_to_all | solution.py:166
  149.4 0.8 slice.38
  150.2 23.6 %all-to-all-done = bf16[4,256,864]{1,2,0:T(8,128)(2,1)S(1)} async-done(((bf16[4,256,864]{1,2,0:T(8,128)(2,1)}), bf16[4,256,864]{1,2,0:T(8,128)(2,1)S(1)}, u32[]{:S(2)}, u32[]{:S(2)}) %all-to-all-start) | async-done | bytes 1769504 | tf_op jit(solution)/shard_map/all_to_all | solution.py:166
  175.7 2.6 copy.66.q_ref
  178.3 40.3 %all-gather.5.cloned.1.call-done.k_ref.v_ref = bf16[4096,1024]{1,0:T(8,128)(2,1)} async-done(((bf16[256,1024]{1,0:T(8,128)(2,1)}), bf16[4096,1024]{1,0:T(8,128)(2,1)}) %all-gather.5.cloned.1.call-update) | async-done | bytes 8388624 | tf_op jit(solution)/shard_map/all_gather | solution.py:191
  218.6 46.0 %shard_map.68 = bf16[256,3584]{1,0:T(8,128)(2,1)} custom-call(s32[8]{0:T(128)} %pad_add_fusion.meta, bf16[256,3584]{1,0:T(8,128)(2,1)} %copy.66.q_ref, bf16[4096,1024]{1,0:T(8,128)(2,1)} %all-gather.5.cloned.1.call-done.k_ref.v_ref, bf16[4096,1024]{1,0:T(8,128)(2,1)} %all-gather.5.cloned.1.call-done.k_ref.v_ref), custom_call_target="tpu_custom_call" | custom-call | tf_op jit(solution)/shard_map/pallas_call | solution.py:106
  (64 shorter events, 8.3 us)
Async XLA Ops:
  7.2 2.8 %copy-start.13 = (f32[3584]{0:T(1024)S(1)}, f32[3584]{0:T(1024)}, u32[]{:S(2)}) copy-start(f32[3584]{0:T(1024)} %param.7) | copy-start | bytes 43012
  7.2 99.5 %all-gather.7.cloned.1.call-start = ((), (), s32[]{:S(2)}) async-start(), calls=%async_computation.3 | async-start | bytes 9732096 | tf_op jit(solution)/shard_map/all_gather | solution.py:153
  7.9 2.1 copy-start.5
  10.5 42.3 %collective-permute-start = (bf16[256,3584]{1,0:T(8,128)(2,1)S(1)}, bf16[256,3584]{1,0:T(8,128)(2,1)}, u32[]{:S(2)}, u32[]{:S(2)}) collective-permute-start(bf16[256,3584]{1,0:T(8,128)(2,1)S(1)} %fusion.3), channel_id=1, source_target_pairs={{0,1},{1,2},{2,3},{3,0},{4,5},{5,6},{6,7},{7,4},{8,9},{9,10},{10,1... | collective-permute-start | bytes 5505032 | tf_op jit(solution)/shard_map/ppermute | solution.py:148
  11.8 81.3 %collective-permute-start.1 = (bf16[256,3584]{1,0:T(8,128)(2,1)S(1)}, bf16[256,3584]{1,0:T(8,128)(2,1)}, u32[]{:S(2)}, u32[]{:S(2)}) collective-permute-start(bf16[256,3584]{1,0:T(8,128)(2,1)S(1)} %fusion.3), channel_id=1, source_target_pairs={{0,2},{1,3},{2,0},{3,1},{4,6},{5,7},{6,4},{7,5},{8,10},{9,11},{10,... | collective-permute-start | bytes 5505032 | tf_op jit(solution)/shard_map/ppermute | solution.py:148
  14.3 82.7 %collective-permute-start.2 = (bf16[256,3584]{1,0:T(8,128)(2,1)S(1)}, bf16[256,3584]{1,0:T(8,128)(2,1)}, u32[]{:S(2)}, u32[]{:S(2)}) collective-permute-start(bf16[256,3584]{1,0:T(8,128)(2,1)S(1)} %fusion.3), channel_id=1, source_target_pairs={{0,3},{1,0},{2,1},{3,2},{4,7},{5,4},{6,5},{7,6},{8,11},{9,8},{10,9... | collective-permute-start | bytes 5505032 | tf_op jit(solution)/shard_map/ppermute | solution.py:148
  15.4 2.3 copy-start.12
  15.4 2.4 copy-start.14
  18.1 1.5 copy-start
  19.9 2.9 %copy-start.4 = (bf16[1024,3584]{0,1:T(8,128)(2,1)}, bf16[1024,3584]{0,1:T(8,128)(2,1)S(1)}, u32[]{:S(2)}) copy-start(bf16[1024,3584]{0,1:T(8,128)(2,1)S(1)} %constant_dynamic-update-slice_fusion.3) | copy-start | bytes 22020100
  97.0 3.9 %copy-start.1 = (bf16[256,3584]{0,1:T(8,128)(2,1)S(1)}, bf16[256,3584]{0,1:T(8,128)(2,1)}, u32[]{:S(2)}) copy-start(bf16[256,3584]{0,1:T(8,128)(2,1)} %copy.54) | copy-start | bytes 5505028
  100.9 2.2 copy-start.2
  103.0 2.2 copy-start.3
  119.8 1.5 copy-start.6
  122.7 11.9 %all-to-all-start.1 = ((bf16[4,256,288]{1,2,0:T(8,128)(2,1)}), bf16[4,256,288]{1,2,0:T(8,128)(2,1)S(1)}, u32[]{:S(2)}, u32[]{:S(2)}) async-start(bf16[4,256,288]{1,2,0:T(8,128)(2,1)} %copy.60), calls=%async_computation.1 | async-start | bytes 1179648 | tf_op jit(solution)/shard_map/all_to_all | solution.py:164
  126.1 92.4 %all-gather.5.cloned.1.call-start = ((), (), s32[]{:S(2)}) async-start(), calls=%async_computation.2 | async-start | bytes 8912896 | tf_op jit(solution)/shard_map/all_gather | solution.py:191
  126.5 8.1 %copy-start.8 = (f32[256,64]{0,1:T(8,128)}, f32[256,64]{0,1:T(8,128)S(1)}, u32[]{:S(2)}) copy-start(f32[256,64]{0,1:T(8,128)S(1)} %get-tuple-element.10) | copy-start | bytes 196612
  126.5 8.1 %copy-start.10 = (f32[256,64]{0,1:T(8,128)}, f32[256,64]{0,1:T(8,128)S(1)}, u32[]{:S(2)}) copy-start(f32[256,64]{0,1:T(8,128)S(1)} %get-tuple-element.11) | copy-start | bytes 196612
  134.6 0.8 copy-start.7
  141.6 32.2 %all-to-all-start = ((bf16[4,256,864]{1,2,0:T(8,128)(2,1)}), bf16[4,256,864]{1,2,0:T(8,128)(2,1)S(1)}, u32[]{:S(2)}, u32[]{:S(2)}) async-start(bf16[4,256,864]{1,2,0:T(8,128)(2,1)} %copy.58), calls=%async_computation | async-start | bytes 3538944 | tf_op jit(solution)/shard_map/all_to_all | solution.py:166
  174.0 0.8 copy-start.9
  174.0 0.9 copy-start.11
Sparse Core Ops, SparseCore 0:
  10.2 54.5 all-gather.6
  137.2 81.3 all-gather.4

commit v5 on v4

--- a/solution.py
+++ b/solution.py
@@ -48,12 +48,9 @@
             heads = slice(h * HEAD_DIM, (h + 1) * HEAD_DIM)
             for c in range(BLOCK // LANES):
                 cols = slice(c * LANES, (c + 1) * LANES)
-                q = q_ref[cols, heads]
+                q = q_ref[heads, cols]
                 scores = (
-                    lax.dot_general(
-                        keys, q, (((1,), (1,)), ((), ())), preferred_element_type=jnp.float32
-                    )
-                    * scale
+                    jnp.dot(keys, q, preferred_element_type=jnp.float32) * scale
                     + bias_ref[:, cols]
                 )
                 m_prev = m_ref[h, :, cols]
@@ -76,8 +73,8 @@
             ).astype(o_ref.dtype)
 
 
-def flash(meta, queries, kv_all, steps):
-    rows = queries.shape[0]
+def flash(meta, queries_t, kv_all, steps):
+    rows = queries_t.shape[1]
     group = HEADS // KV_HEADS
     width = group * HEAD_DIM
 
@@ -91,7 +88,7 @@
         num_scalar_prefetch=1,
         grid=(KV_HEADS, steps),
         in_specs=[
-            pl.BlockSpec((rows, width), lambda g, t, meta: (0, g)),
+            pl.BlockSpec((width, rows), lambda g, t, meta: (g, 0)),
             pl.BlockSpec((BLOCK, HEAD_DIM), key_map),
             pl.BlockSpec((BLOCK, HEAD_DIM), value_map),
         ],
@@ -108,7 +105,7 @@
         grid_spec=spec,
         out_shape=jax.ShapeDtypeStruct((rows, HEADS * HEAD_DIM), jnp.bfloat16),
         compiler_params=pltpu.CompilerParams(dimension_semantics=("arbitrary", "arbitrary")),
-    )(meta, queries, kv_all, kv_all)
+    )(meta, queries_t, kv_all, kv_all)
 
 
 def norm_rows(values, gain):
@@ -194,7 +191,7 @@
         [ends, jnp.stack([gy_index, lead // BLOCK, 0, 0]).astype(jnp.int32)]
     ).astype(jnp.int32)
     steps = min(piece.shape[0] // BLOCK, 9)
-    attn = flash(meta, queries, piece, steps)
+    attn = flash(meta, jnp.transpose(queries), piece, steps)
     return (attn, kv_rows)
 
 

time: 272 us -> 266 us (0.978)
  the two profiles are of different devices: /device:TPU:121 before, /device:TPU:47 now
where the time goes in v5:
time: 266 us; the launch traced here: 263 us
  waiting for transfers between devices  138 us (52%)
  Pallas kernels  37.7 us (14%)
  local copies, waits for them, and re-layouts  34 us (13%)
  between operations  16.9 us (6%)
  starting transfers between devices  14.7 us (6%)
  matrix products  13.2 us (5%)
  other arithmetic  9.28 us (3%)
    ppermute x3, waiting for transfers between devices, project_joined(): shifted.append(lax.ppermute(normed, 'x', pairs))  65.6 us
    all_gather x1, waiting for transfers between devices, on_device(): piece = lax.all_gather(kv_rows, ('y', 'x'), axis=0, tiled=True)  42.9 us
    pallas_call x1, Pallas kernels, flash(): pl.pallas_call(flash_body, grid_spec=spec, out_shape=jax.ShapeDtypeStruct...  37.7 us
    all_to_all x1, waiting for transfers between devices, project_joined(): head = lax.all_to_all(head, 'x', split_axis=0, concat_axis=1, tiled=True)  22.2 us
    dot_general x1, matrix products, project_joined(): jnp.einsum('tie,iyec->tyc', grouped.reshape(grouped.shape[0], pieces.shap...  13.2 us
    ppermute x3, local copies, waits for them, and re-layouts, project_joined(): shifted.append(lax.ppermute(normed, 'x', pairs))  11.6 us
    unnamed x33, local copies, waits for them, and re-layouts  7.49 us
    all_to_all x1, starting transfers between devices, project_joined(): lax.all_to_all(block_out[:, n_y - 1], 'x', split_axis=0, concat_axis=1, t...  6.89 us
  transfers between devices with their start and end apart: 7, of which 5 were waited for; matrix products, arithmetic and copies ran while one was open for 12% of the time, Pallas kernels for 0%

profile of v5, /device:TPU:47, one launch (start us, length us, event | category | flops | bytes accessed | tf_op | source)
XLA Modules:
  0.0 263.3 jit_solution(17340135914858298181)
XLA Ops:
  7.9 2.1 fusion.1
  10.0 1.2 fusion.3
  11.5 2.1 collective-permute-start.1
  13.7 2.2 copy.78
  16.4 0.9 broadcast_in_dim.31
  18.2 2.9 %copy-done.4 = bf16[1024,3584]{0,1:T(8,128)(2,1)} copy-done((bf16[1024,3584]{0,1:T(8,128)(2,1)}, bf16[1024,3584]{0,1:T(8,128)(2,1)S(1)}, u32[]{:S(2)}) %copy-start.4) | copy-done | bytes 7340056
  21.1 31.3 %collective-permute-done = bf16[256,3584]{1,0:T(8,128)(2,1)} collective-permute-done((bf16[256,3584]{1,0:T(8,128)(2,1)S(1)}, bf16[256,3584]{1,0:T(8,128)(2,1)}, u32[]{:S(2)}, u32[]{:S(2)}) %collective-permute-start) | collective-permute-done | bytes 1835040 | tf_op jit(solution)/shard_map/ppermute | solution.py:145
  52.3 3.9 %copy.79 = bf16[256,3584]{0,1:T(8,128)(2,1)} copy(bf16[256,3584]{1,0:T(8,128)(2,1)} %collective-permute-done) | data formatting | bytes 3670016 | tf_op jit(solution)/shard_map/ppermute | solution.py:145
  56.2 3.8 %copy.80 = bf16[256,3584]{0,1:T(8,128)(2,1)} copy(bf16[256,3584]{1,0:T(8,128)(2,1)} %collective-permute-done.1) | data formatting | bytes 3670016 | tf_op jit(solution)/shard_map/ppermute | solution.py:145
  60.0 34.4 %collective-permute-done.2 = bf16[256,3584]{1,0:T(8,128)(2,1)} collective-permute-done((bf16[256,3584]{1,0:T(8,128)(2,1)S(1)}, bf16[256,3584]{1,0:T(8,128)(2,1)}, u32[]{:S(2)}, u32[]{:S(2)}) %collective-permute-start.2) | collective-permute-done | bytes 1835040 | tf_op jit(solution)/shard_map/ppermute | solution.py:145
  94.4 3.9 %copy.81 = bf16[256,3584]{0,1:T(8,128)(2,1)} copy(bf16[256,3584]{1,0:T(8,128)(2,1)} %collective-permute-done.2) | data formatting | bytes 3670016 | tf_op jit(solution)/shard_map/ppermute | solution.py:145
  98.3 1.4 constant_dynamic-update-slice_fusion.2
  99.8 0.7 copy-done.2
  100.5 1.4 constant_dynamic-update-slice_fusion.1
  101.9 0.7 copy-done.3
  102.7 1.5 constant_dynamic-update-slice_fusion
  104.1 13.2 %fusion = bf16[1024,4,288]{0,2,1:T(8,128)(2,1)S(1)} fusion(f32[4,288]{1,0:T(4,128)S(1)} %bitcast.60, bf16[1024,8,448,1]{0,2,3,1:T(8,128)(2,1)} %bitcast.50, bf16[8,4,448,288]{2,3,1,0:T(8,128)(2,1)} %bitcast.65), kind=kOutput, calls=%fused_computation.1 | convolution fusion | flops 8458076160 | bytes 17961472 | tf_op jit(solution)/shard_map/tie,iyec->tyc/dot_general | solution.py:152
  117.3 1.5 copy-done.6
  119.3 0.9 copy.85
  120.2 6.9 %all-to-all-start.1 = ((bf16[4,256,288]{1,2,0:T(8,128)(2,1)}), bf16[4,256,288]{1,2,0:T(8,128)(2,1)S(1)}, u32[]{:S(2)}, u32[]{:S(2)}) async-start(bf16[4,256,288]{1,2,0:T(8,128)(2,1)} %copy.85), calls=%async_computation.1 | async-start | bytes 1179648 | tf_op jit(solution)/shard_map/all_to_all | solution.py:161
  127.6 6.1 %all-to-all-done.1 = bf16[4,256,288]{1,2,0:T(8,128)(2,1)S(1)} async-done(((bf16[4,256,288]{1,2,0:T(8,128)(2,1)}), bf16[4,256,288]{1,2,0:T(8,128)(2,1)S(1)}, u32[]{:S(2)}, u32[]{:S(2)}) %all-to-all-start.1) | async-done | bytes 589856 | tf_op jit(solution)/shard_map/all_to_all | solution.py:161
  135.1 0.9 pad_maximum_fusion.2
  136.0 1.6 slice.36
  137.7 1.4 all_to_all.26
  139.0 1.4 copy.83
  140.5 5.3 %all-to-all-start = ((bf16[4,256,864]{1,2,0:T(8,128)(2,1)}), bf16[4,256,864]{1,2,0:T(8,128)(2,1)S(1)}, u32[]{:S(2)}, u32[]{:S(2)}) async-start(bf16[4,256,864]{1,2,0:T(8,128)(2,1)} %copy.83), calls=%async_computation | async-start | bytes 3538944 | tf_op jit(solution)/shard_map/all_to_all | solution.py:163
  145.8 0.7 fusion.4
  149.6 0.9 slice.38
  150.5 22.2 %all-to-all-done = bf16[4,256,864]{1,2,0:T(8,128)(2,1)S(1)} async-done(((bf16[4,256,864]{1,2,0:T(8,128)(2,1)}), bf16[4,256,864]{1,2,0:T(8,128)(2,1)S(1)}, u32[]{:S(2)}, u32[]{:S(2)}) %all-to-all-start) | async-done | bytes 1769504 | tf_op jit(solution)/shard_map/all_to_all | solution.py:163
  174.5 1.4 pad_maximum_fusion.1
  175.8 42.9 %all-gather.5.cloned.1.call-done.k_ref.v_ref = bf16[4096,1024]{1,0:T(8,128)(2,1)} async-done(((bf16[256,1024]{1,0:T(8,128)(2,1)}), bf16[4096,1024]{1,0:T(8,128)(2,1)}) %all-gather.5.cloned.1.call-update) | async-done | bytes 8388624 | tf_op jit(solution)/shard_map/all_gather | solution.py:188
  218.7 37.7 %shard_map.68 = bf16[256,3584]{1,0:T(8,128)(2,1)} custom-call(s32[8]{0:T(128)} %pad_add_fusion.meta, bf16[3584,256]{1,0:T(8,128)(2,1)} %bitcast.49, bf16[4096,1024]{1,0:T(8,128)(2,1)} %all-gather.5.cloned.1.call-done.k_ref.v_ref, bf16[4096,1024]{1,0:T(8,128)(2,1)} %all-gather.5.cloned.1.call-done.k_ref.v_ref), custom_call_target="tpu_custom_call" | custom-call | tf_op jit(solution)/shard_map/pallas_call | solution.py:103
  (61 shorter events, 6.9 us)
Async XLA Ops:
  7.2 97.0 %all-gather.7.cloned.1.call-start = ((), (), s32[]{:S(2)}) async-start(), calls=%async_computation.3 | async-start | bytes 9732096 | tf_op jit(solution)/shard_map/all_gather | solution.py:150
  7.9 2.1 copy-start.5
  11.2 4.7 %copy-start.12 = (f32[4608]{0:T(1024)S(1)}, f32[4608]{0:T(1024)}, u32[]{:S(2)}) copy-start(f32[4608]{0:T(1024)} %param.9) | copy-start | bytes 55300
  11.3 4.8 %copy-start.13 = (s32[1,4]{1,0:T(1,128)S(1)}, s32[1,4]{1,0:T(1,128)}, u32[]{:S(2)}) copy-start(s32[1,4]{1,0:T(1,128)} %param.6) | copy-start | bytes 52
  11.3 41.1 %collective-permute-start = (bf16[256,3584]{1,0:T(8,128)(2,1)S(1)}, bf16[256,3584]{1,0:T(8,128)(2,1)}, u32[]{:S(2)}, u32[]{:S(2)}) collective-permute-start(bf16[256,3584]{1,0:T(8,128)(2,1)S(1)} %fusion.3), channel_id=1, source_target_pairs={{0,1},{1,2},{2,3},{3,0},{4,5},{5,6},{6,7},{7,4},{8,9},{9,10},{10,1... | collective-permute-start | bytes 5505032 | tf_op jit(solution)/shard_map/ppermute | solution.py:145
  11.5 44.7 %collective-permute-start.1 = (bf16[256,3584]{1,0:T(8,128)(2,1)S(1)}, bf16[256,3584]{1,0:T(8,128)(2,1)}, u32[]{:S(2)}, u32[]{:S(2)}) collective-permute-start(bf16[256,3584]{1,0:T(8,128)(2,1)S(1)} %fusion.3), channel_id=1, source_target_pairs={{0,2},{1,3},{2,0},{3,1},{4,6},{5,7},{6,4},{7,5},{8,10},{9,11},{10,... | collective-permute-start | bytes 5505032 | tf_op jit(solution)/shard_map/ppermute | solution.py:145
  13.7 80.7 %collective-permute-start.2 = (bf16[256,3584]{1,0:T(8,128)(2,1)S(1)}, bf16[256,3584]{1,0:T(8,128)(2,1)}, u32[]{:S(2)}, u32[]{:S(2)}) collective-permute-start(bf16[256,3584]{1,0:T(8,128)(2,1)S(1)} %fusion.3), channel_id=1, source_target_pairs={{0,3},{1,0},{2,1},{3,2},{4,7},{5,4},{6,5},{7,6},{8,11},{9,8},{10,9... | collective-permute-start | bytes 5505032 | tf_op jit(solution)/shard_map/ppermute | solution.py:145
  16.4 1.5 copy-start
  18.2 2.9 %copy-start.4 = (bf16[1024,3584]{0,1:T(8,128)(2,1)}, bf16[1024,3584]{0,1:T(8,128)(2,1)S(1)}, u32[]{:S(2)}) copy-start(bf16[1024,3584]{0,1:T(8,128)(2,1)S(1)} %constant_dynamic-update-slice_fusion.3) | copy-start | bytes 22020100
  94.4 3.9 %copy-start.1 = (bf16[256,3584]{0,1:T(8,128)(2,1)S(1)}, bf16[256,3584]{0,1:T(8,128)(2,1)}, u32[]{:S(2)}) copy-start(bf16[256,3584]{0,1:T(8,128)(2,1)} %copy.79) | copy-start | bytes 5505028
  98.3 2.2 copy-start.2
  100.5 2.2 copy-start.3
  117.3 1.5 copy-start.6
  120.2 13.6 %all-to-all-start.1 = ((bf16[4,256,288]{1,2,0:T(8,128)(2,1)}), bf16[4,256,288]{1,2,0:T(8,128)(2,1)S(1)}, u32[]{:S(2)}, u32[]{:S(2)}) async-start(bf16[4,256,288]{1,2,0:T(8,128)(2,1)} %copy.85), calls=%async_computation.1 | async-start | bytes 1179648 | tf_op jit(solution)/shard_map/all_to_all | solution.py:161
  127.0 91.7 %all-gather.5.cloned.1.call-start = ((), (), s32[]{:S(2)}) async-start(), calls=%async_computation.2 | async-start | bytes 8912896 | tf_op jit(solution)/shard_map/all_gather | solution.py:188
  127.4 6.4 %copy-start.8 = (f32[256,64]{0,1:T(8,128)}, f32[256,64]{0,1:T(8,128)S(1)}, u32[]{:S(2)}) copy-start(f32[256,64]{0,1:T(8,128)S(1)} %get-tuple-element.10) | copy-start | bytes 196612
  127.4 6.4 %copy-start.10 = (f32[256,64]{0,1:T(8,128)}, f32[256,64]{0,1:T(8,128)S(1)}, u32[]{:S(2)}) copy-start(f32[256,64]{0,1:T(8,128)S(1)} %get-tuple-element.11) | copy-start | bytes 196612
  133.7 0.9 copy-start.7
  140.5 32.2 %all-to-all-start = ((bf16[4,256,864]{1,2,0:T(8,128)(2,1)}), bf16[4,256,864]{1,2,0:T(8,128)(2,1)S(1)}, u32[]{:S(2)}, u32[]{:S(2)}) async-start(bf16[4,256,864]{1,2,0:T(8,128)(2,1)} %copy.83), calls=%async_computation | async-start | bytes 3538944 | tf_op jit(solution)/shard_map/all_to_all | solution.py:163
  172.9 0.8 copy-start.9
  173.0 0.9 copy-start.11
Sparse Core Ops, SparseCore 0:
  10.2 56.1 all-gather.6
  136.2 82.5 all-gather.4

commit v6 on v5

--- a/solution.py
+++ b/solution.py
@@ -158,10 +158,21 @@
     bias_block = bias.reshape(n_y, n_x, width)
     bias_block = lax.dynamic_index_in_dim(bias_block, lax.axis_index("x"), 1, keepdims=False)
     block_out = (summed + bias_block[None]).astype(jnp.bfloat16)
-    tail = lax.all_to_all(block_out[:, n_y - 1], "x", split_axis=0, concat_axis=1, tiled=True)
-    head = block_out[:, : n_y - 1].reshape(block_out.shape[0], -1)
-    head = lax.all_to_all(head, "x", split_axis=0, concat_axis=1, tiled=True)
-    head = jnp.transpose(head.reshape(rows, n_x, n_y - 1, width), (0, 2, 1, 3))
+
+    def exchange(part):
+        mine = lax.dynamic_slice_in_dim(part, here * rows, rows, 0)
+        full = jnp.zeros((rows, n_x) + part.shape[1:], part.dtype)
+        full = lax.dynamic_update_slice_in_dim(full, mine[:, None], here, 1)
+        for step in range(1, n_x):
+            sent = lax.dynamic_slice_in_dim(part, ((here + step) % n_x) * rows, rows, 0)
+            pairs = [(s, (s + step) % n_x) for s in range(n_x)]
+            got = lax.ppermute(sent, "x", pairs)
+            full = lax.dynamic_update_slice_in_dim(full, got[:, None], (here - step) % n_x, 1)
+        return full
+
+    tail = exchange(block_out[:, n_y - 1]).reshape(rows, -1)
+    head = exchange(block_out[:, : n_y - 1])
+    head = jnp.transpose(head, (0, 2, 1, 3))
     return head.reshape(rows, -1), tail
 
 

time: 266 us -> 263 us (0.989)
  the two profiles are of different devices: /device:TPU:47 before, /device:TPU:15 now
where the time goes in v6:
time: 263 us; the launch traced here: 261 us
  waiting for transfers between devices  147 us (56%)
  Pallas kernels  37.7 us (14%)
  local copies, waits for them, and re-layouts  30.2 us (11%)
  between operations  16.7 us (6%)
  matrix products  13.2 us (5%)
  other arithmetic  8.57 us (3%)
  starting transfers between devices  8.2 us (3%)
    ppermute x3, waiting for transfers between devices, project_joined(): shifted.append(lax.ppermute(normed, 'x', pairs))  65.6 us
    all_gather x1, waiting for transfers between devices, on_device(): piece = lax.all_gather(kv_rows, ('y', 'x'), axis=0, tiled=True)  42.4 us
    ppermute x6, waiting for transfers between devices, exchange(): got = lax.ppermute(sent, 'x', pairs)  38.2 us
    pallas_call x1, Pallas kernels, flash(): pl.pallas_call(flash_body, grid_spec=spec, out_shape=jax.ShapeDtypeStruct...  37.7 us
    dot_general x1, matrix products, project_joined(): jnp.einsum('tie,iyec->tyc', grouped.reshape(grouped.shape[0], pieces.shap...  13.2 us
    ppermute x3, local copies, waits for them, and re-layouts, project_joined(): shifted.append(lax.ppermute(normed, 'x', pairs))  11.6 us
    unnamed x25, local copies, waits for them, and re-layouts  7.06 us
    ppermute x6, starting transfers between devices, exchange(): got = lax.ppermute(sent, 'x', pairs)  5.71 us
  transfers between devices with their start and end apart: 11, of which 9 were waited for; matrix products, arithmetic and copies ran while one was open for 11% of the time, Pallas kernels for 0%

profile of v6, /device:TPU:15, one launch (start us, length us, event | category | flops | bytes accessed | tf_op | source)
XLA Modules:
  0.0 261.4 jit_solution(5013750555480518361)
XLA Ops:
  7.2 0.7 all-gather.7.cloned.1.call-update
  8.0 2.1 fusion.1
  10.9 2.1 collective-permute-start.1
  13.0 2.3 copy.54
  15.7 0.9 broadcast_in_dim.60
  17.5 2.9 %copy-done.4 = bf16[1024,3584]{0,1:T(8,128)(2,1)} copy-done((bf16[1024,3584]{0,1:T(8,128)(2,1)}, bf16[1024,3584]{0,1:T(8,128)(2,1)S(1)}, u32[]{:S(2)}) %copy-start.4) | copy-done | bytes 7340056
  20.4 31.2 %collective-permute-done = bf16[256,3584]{1,0:T(8,128)(2,1)} collective-permute-done((bf16[256,3584]{1,0:T(8,128)(2,1)S(1)}, bf16[256,3584]{1,0:T(8,128)(2,1)}, u32[]{:S(2)}, u32[]{:S(2)}) %collective-permute-start) | collective-permute-done | bytes 1835040 | tf_op jit(solution)/shard_map/ppermute | solution.py:145
  51.7 3.8 %copy.55 = bf16[256,3584]{0,1:T(8,128)(2,1)} copy(bf16[256,3584]{1,0:T(8,128)(2,1)} %collective-permute-done) | data formatting | bytes 3670016 | tf_op jit(solution)/shard_map/ppermute | solution.py:145
  55.5 3.9 %copy.56 = bf16[256,3584]{0,1:T(8,128)(2,1)} copy(bf16[256,3584]{1,0:T(8,128)(2,1)} %collective-permute-done.1) | data formatting | bytes 3670016 | tf_op jit(solution)/shard_map/ppermute | solution.py:145
  59.4 34.4 %collective-permute-done.2 = bf16[256,3584]{1,0:T(8,128)(2,1)} collective-permute-done((bf16[256,3584]{1,0:T(8,128)(2,1)S(1)}, bf16[256,3584]{1,0:T(8,128)(2,1)}, u32[]{:S(2)}, u32[]{:S(2)}) %collective-permute-start.2) | collective-permute-done | bytes 1835040 | tf_op jit(solution)/shard_map/ppermute | solution.py:145
  93.7 3.9 %copy.57 = bf16[256,3584]{0,1:T(8,128)(2,1)} copy(bf16[256,3584]{1,0:T(8,128)(2,1)} %collective-permute-done.2) | data formatting | bytes 3670016 | tf_op jit(solution)/shard_map/ppermute | solution.py:145
  97.7 1.4 constant_dynamic-update-slice_fusion.2
  99.1 0.7 copy-done.2
  99.8 1.4 constant_dynamic-update-slice_fusion.1
  101.3 0.7 copy-done.3
  102.0 1.5 constant_dynamic-update-slice_fusion
  103.5 13.2 %fusion = bf16[1024,4,288]{0,2,1:T(8,128)(2,1)S(1)} fusion(f32[4,288]{1,0:T(4,128)S(1)} %bitcast.76, bf16[1024,8,448,1]{0,2,3,1:T(8,128)(2,1)} %bitcast.67, bf16[8,4,448,288]{2,3,1,0:T(8,128)(2,1)} %bitcast.81), kind=kOutput, calls=%fused_computation.1 | convolution fusion | flops 8458076160 | bytes 17961472 | tf_op jit(solution)/shard_map/tie,iyec->tyc/dot_general | solution.py:152
  116.6 1.5 copy-done.6
  118.3 3.5 %collective-permute-start.6 = (bf16[256,288]{0,1:T(8,128)(2,1)S(1)}, bf16[256,288]{0,1:T(8,128)(2,1)S(1)}, u32[]{:S(2)}, u32[]{:S(2)}) collective-permute-start(bf16[256,288]{0,1:T(8,128)(2,1)S(1)} %get-tuple-element.13), channel_id=1, source_target_pairs={{0,1},{1,2},{2,3},{3,0},{4,5},{5,6},{6,7},{7,4},{8,9},{9,10},{10,1... | collective-permute-start | bytes 442376 | tf_op jit(solution)/shard_map/ppermute | solution.py:169
  123.0 4.2 %collective-permute-done.6 = bf16[256,288]{0,1:T(8,128)(2,1)S(1)} collective-permute-done((bf16[256,288]{0,1:T(8,128)(2,1)S(1)}, bf16[256,288]{0,1:T(8,128)(2,1)S(1)}, u32[]{:S(2)}, u32[]{:S(2)}) %collective-permute-start.6) | collective-permute-done | bytes 147488 | tf_op jit(solution)/shard_map/ppermute | solution.py:169
  127.3 0.7 collective-permute-done.7
  128.0 3.9 %collective-permute-done.8 = bf16[256,288]{0,1:T(8,128)(2,1)S(1)} collective-permute-done((bf16[256,288]{0,1:T(8,128)(2,1)S(1)}, bf16[256,288]{0,1:T(8,128)(2,1)S(1)}, u32[]{:S(2)}, u32[]{:S(2)}) %collective-permute-start.8) | collective-permute-done | bytes 147488 | tf_op jit(solution)/shard_map/ppermute | solution.py:169
  133.4 0.9 pad_maximum_fusion.2
  134.2 1.6 slice.36
  135.9 1.2 constant_dynamic-slice_fusion
  140.6 1.5 collective-permute-start.5
  142.3 5.5 %collective-permute-done.3 = bf16[256,3,288]{0,2,1:T(8,128)(2,1)S(1)} collective-permute-done((bf16[256,3,288]{0,2,1:T(8,128)(2,1)}, bf16[256,3,288]{0,2,1:T(8,128)(2,1)S(1)}, u32[]{:S(2)}, u32[]{:S(2)}) %collective-permute-start.3) | collective-permute-done | bytes 442400 | tf_op jit(solution)/shard_map/ppermute | solution.py:169
  147.8 5.1 %collective-permute-done.4 = bf16[256,3,288]{0,2,1:T(8,128)(2,1)S(1)} collective-permute-done((bf16[256,3,288]{0,2,1:T(8,128)(2,1)}, bf16[256,3,288]{0,2,1:T(8,128)(2,1)S(1)}, u32[]{:S(2)}, u32[]{:S(2)}) %collective-permute-start.4) | collective-permute-done | bytes 442400 | tf_op jit(solution)/shard_map/ppermute | solution.py:169
  152.9 18.8 %collective-permute-done.5 = bf16[256,3,288]{0,2,1:T(8,128)(2,1)S(1)} collective-permute-done((bf16[256,3,288]{0,2,1:T(8,128)(2,1)}, bf16[256,3,288]{0,2,1:T(8,128)(2,1)S(1)}, u32[]{:S(2)}, u32[]{:S(2)}) %collective-permute-start.5) | collective-permute-done | bytes 442400 | tf_op jit(solution)/shard_map/ppermute | solution.py:169
  172.9 1.5 pad_maximum_fusion.1
  174.4 42.4 %all-gather.5.cloned.1.call-done.k_ref.v_ref = bf16[4096,1024]{1,0:T(8,128)(2,1)} async-done(((bf16[256,1024]{1,0:T(8,128)(2,1)}), bf16[4096,1024]{1,0:T(8,128)(2,1)}) %all-gather.5.cloned.1.call-update) | async-done | bytes 8388624 | tf_op jit(solution)/shard_map/all_gather | solution.py:199
  216.8 37.7 %shard_map.68 = bf16[256,3584]{1,0:T(8,128)(2,1)} custom-call(s32[8]{0:T(128)} %pad_add_fusion.meta, bf16[3584,256]{1,0:T(8,128)(2,1)} %bitcast.66, bf16[4096,1024]{1,0:T(8,128)(2,1)} %all-gather.5.cloned.1.call-done.k_ref.v_ref, bf16[4096,1024]{1,0:T(8,128)(2,1)} %all-gather.5.cloned.1.call-done.k_ref.v_ref), custom_call_target="tpu_custom_call" | custom-call | tf_op jit(solution)/shard_map/pallas_call | solution.py:103
  (67 shorter events, 7.7 us)
Async XLA Ops:
  7.2 2.9 %copy-start.8 = (f32[3584]{0:T(1024)S(1)}, f32[3584]{0:T(1024)}, u32[]{:S(2)}) copy-start(f32[3584]{0:T(1024)} %param.7) | copy-start | bytes 43012
  7.2 96.3 %all-gather.7.cloned.1.call-start = ((), (), s32[]{:S(2)}) async-start(), calls=%async_computation.1 | async-start | bytes 9732096 | tf_op jit(solution)/shard_map/all_gather | solution.py:150
  7.9 208.9 %all-gather.5.cloned.1.call-start = ((), (), s32[]{:S(2)}) async-start(), calls=%async_computation | async-start | bytes 8912896 | tf_op jit(solution)/shard_map/all_gather | solution.py:199
  8.0 2.1 copy-start.5
  10.6 41.1 %collective-permute-start = (bf16[256,3584]{1,0:T(8,128)(2,1)S(1)}, bf16[256,3584]{1,0:T(8,128)(2,1)}, u32[]{:S(2)}, u32[]{:S(2)}) collective-permute-start(bf16[256,3584]{1,0:T(8,128)(2,1)S(1)} %fusion.3), channel_id=1, source_target_pairs={{0,1},{1,2},{2,3},{3,0},{4,5},{5,6},{6,7},{7,4},{8,9},{9,10},{10,1... | collective-permute-start | bytes 5505032 | tf_op jit(solution)/shard_map/ppermute | solution.py:145
  10.9 44.6 %collective-permute-start.1 = (bf16[256,3584]{1,0:T(8,128)(2,1)S(1)}, bf16[256,3584]{1,0:T(8,128)(2,1)}, u32[]{:S(2)}, u32[]{:S(2)}) collective-permute-start(bf16[256,3584]{1,0:T(8,128)(2,1)S(1)} %fusion.3), channel_id=1, source_target_pairs={{0,2},{1,3},{2,0},{3,1},{4,6},{5,7},{6,4},{7,5},{8,10},{9,11},{10,... | collective-permute-start | bytes 5505032 | tf_op jit(solution)/shard_map/ppermute | solution.py:145
  13.0 80.7 %collective-permute-start.2 = (bf16[256,3584]{1,0:T(8,128)(2,1)S(1)}, bf16[256,3584]{1,0:T(8,128)(2,1)}, u32[]{:S(2)}, u32[]{:S(2)}) collective-permute-start(bf16[256,3584]{1,0:T(8,128)(2,1)S(1)} %fusion.3), channel_id=1, source_target_pairs={{0,3},{1,0},{2,1},{3,2},{4,7},{5,4},{6,5},{7,6},{8,11},{9,8},{10,9... | collective-permute-start | bytes 5505032 | tf_op jit(solution)/shard_map/ppermute | solution.py:145
  13.0 2.3 copy-start.7
  13.0 2.4 copy-start.9
  15.7 1.5 copy-start
  17.5 2.9 %copy-start.4 = (bf16[1024,3584]{0,1:T(8,128)(2,1)}, bf16[1024,3584]{0,1:T(8,128)(2,1)S(1)}, u32[]{:S(2)}) copy-start(bf16[1024,3584]{0,1:T(8,128)(2,1)S(1)} %constant_dynamic-update-slice_fusion.3) | copy-start | bytes 22020100
  93.7 3.9 %copy-start.1 = (bf16[256,3584]{0,1:T(8,128)(2,1)S(1)}, bf16[256,3584]{0,1:T(8,128)(2,1)}, u32[]{:S(2)}) copy-start(bf16[256,3584]{0,1:T(8,128)(2,1)} %copy.55) | copy-start | bytes 5505028
  97.7 2.2 copy-start.2
  99.8 2.2 copy-start.3
  116.6 1.5 copy-start.6
  118.3 8.9 %collective-permute-start.6 = (bf16[256,288]{0,1:T(8,128)(2,1)S(1)}, bf16[256,288]{0,1:T(8,128)(2,1)S(1)}, u32[]{:S(2)}, u32[]{:S(2)}) collective-permute-start(bf16[256,288]{0,1:T(8,128)(2,1)S(1)} %get-tuple-element.13), channel_id=1, source_target_pairs={{0,1},{1,2},{2,3},{3,0},{4,5},{5,6},{6,7},{7,4},{8,9},{9,10},{10,1... | collective-permute-start | bytes 442376 | tf_op jit(solution)/shard_map/ppermute | solution.py:169
  122.3 5.7 %collective-permute-start.7 = (bf16[256,288]{0,1:T(8,128)(2,1)S(1)}, bf16[256,288]{0,1:T(8,128)(2,1)S(1)}, u32[]{:S(2)}, u32[]{:S(2)}) collective-permute-start(bf16[256,288]{0,1:T(8,128)(2,1)S(1)} %get-tuple-element.12), channel_id=1, source_target_pairs={{0,2},{1,3},{2,0},{3,1},{4,6},{5,7},{6,4},{7,5},{8,10},{9,11},{10,... | collective-permute-start | bytes 442376 | tf_op jit(solution)/shard_map/ppermute | solution.py:169
  122.4 9.5 %collective-permute-start.8 = (bf16[256,288]{0,1:T(8,128)(2,1)S(1)}, bf16[256,288]{0,1:T(8,128)(2,1)S(1)}, u32[]{:S(2)}, u32[]{:S(2)}) collective-permute-start(bf16[256,288]{0,1:T(8,128)(2,1)S(1)} %get-tuple-element.11), channel_id=1, source_target_pairs={{0,3},{1,0},{2,1},{3,2},{4,7},{5,4},{6,5},{7,6},{8,11},{9,8},{10,9... | collective-permute-start | bytes 442376 | tf_op jit(solution)/shard_map/ppermute | solution.py:169
  137.0 10.7 %collective-permute-start.3 = (bf16[256,3,288]{0,2,1:T(8,128)(2,1)}, bf16[256,3,288]{0,2,1:T(8,128)(2,1)S(1)}, u32[]{:S(2)}, u32[]{:S(2)}) collective-permute-start(bf16[256,3,288]{0,2,1:T(8,128)(2,1)} %get-tuple-element.6), channel_id=1, source_target_pairs={{0,1},{1,2},{2,3},{3,0},{4,5},{5,6},{6,7},{7,4},{8,9},{9,10},{10,1... | collective-permute-start | bytes 1327112 | tf_op jit(solution)/shard_map/ppermute | solution.py:169
  139.9 13.0 %collective-permute-start.4 = (bf16[256,3,288]{0,2,1:T(8,128)(2,1)}, bf16[256,3,288]{0,2,1:T(8,128)(2,1)S(1)}, u32[]{:S(2)}, u32[]{:S(2)}) collective-permute-start(bf16[256,3,288]{0,2,1:T(8,128)(2,1)} %get-tuple-element.5), channel_id=1, source_target_pairs={{0,2},{1,3},{2,0},{3,1},{4,6},{5,7},{6,4},{7,5},{8,10},{9,11},{10,... | collective-permute-start | bytes 1327112 | tf_op jit(solution)/shard_map/ppermute | solution.py:169
  140.6 31.1 %collective-permute-start.5 = (bf16[256,3,288]{0,2,1:T(8,128)(2,1)}, bf16[256,3,288]{0,2,1:T(8,128)(2,1)S(1)}, u32[]{:S(2)}, u32[]{:S(2)}) collective-permute-start(bf16[256,3,288]{0,2,1:T(8,128)(2,1)} %get-tuple-element.4), channel_id=1, source_target_pairs={{0,3},{1,0},{2,1},{3,2},{4,7},{5,4},{6,5},{7,6},{8,11},{9,8},{10,9... | collective-permute-start | bytes 1327112 | tf_op jit(solution)/shard_map/ppermute | solution.py:169
Sparse Core Ops, SparseCore 0:
  10.2 57.9 all-gather.6
  134.4 82.4 all-gather.4

commit v7 on v6

--- a/solution.py
+++ b/solution.py
@@ -149,12 +149,8 @@
         grouped = lax.dynamic_update_slice_in_dim(grouped, piece, at, 0)
     pieces = lax.all_gather(weight, ("z", "c", "y"), axis=0, tiled=False)
     pieces = pieces.reshape(-1, n_y, weight.shape[0], width)
-    summed = jnp.einsum(
-        "tie,iyec->tyc",
-        grouped.reshape(grouped.shape[0], pieces.shape[0], weight.shape[0]),
-        pieces,
-        preferred_element_type=jnp.float32,
-    )
+    pieces = jnp.transpose(pieces, (0, 2, 1, 3)).reshape(grouped.shape[1], n_y, width)
+    summed = jnp.einsum("td,dyc->tyc", grouped, pieces, preferred_element_type=jnp.float32)
     bias_block = bias.reshape(n_y, n_x, width)
     bias_block = lax.dynamic_index_in_dim(bias_block, lax.axis_index("x"), 1, keepdims=False)
     block_out = (summed + bias_block[None]).astype(jnp.bfloat16)

time: 263 us -> 291 us (1.11)
  the two profiles are of different devices: /device:TPU:15 before, /device:TPU:63 now
where the time goes in v7:
time: 291 us; the launch traced here: 288 us
  waiting for transfers between devices  155 us (53%)
  local copies, waits for them, and re-layouts  48 us (16%)
  Pallas kernels  37.7 us (13%)
  between operations  17.1 us (6%)
  matrix products  13.3 us (5%)
  other arithmetic  9.77 us (3%)
  starting transfers between devices  7.26 us (2%)
    ppermute x3, waiting for transfers between devices, project_joined(): shifted.append(lax.ppermute(normed, 'x', pairs))  74.3 us
    all_gather x1, waiting for transfers between devices, on_device(): piece = lax.all_gather(kv_rows, ('y', 'x'), axis=0, tiled=True)  41.3 us
    ppermute x6, waiting for transfers between devices, exchange(): got = lax.ppermute(sent, 'x', pairs)  38.6 us
    pallas_call x1, Pallas kernels, flash(): pl.pallas_call(flash_body, grid_spec=spec, out_shape=jax.ShapeDtypeStruct...  37.7 us
    reshape x1, local copies, waits for them, and re-layouts, project_joined(): jnp.transpose(pieces, (0, 2, 1, 3)).reshape(grouped.shape[1], n_y, width)  17.1 us
    dot_general x1, matrix products, project_joined(): jnp.einsum('td,dyc->tyc', grouped, pieces, preferred_element_type=jnp.flo...  13.3 us
    reshape x1, local copies, waits for them, and re-layouts, project_joined(): pieces = pieces.reshape(-1, n_y, weight.shape[0], width)  12.8 us
    dynamic_update_slice x3, local copies, waits for them, and re-layouts, project_joined(): grouped = lax.dynamic_update_slice_in_dim(grouped, piece, at, 0)  8.84 us
  transfers between devices with their start and end apart: 11, of which 9 were waited for; matrix products, arithmetic and copies ran while one was open for 8% of the time, Pallas kernels for 0%

profile of v7, /device:TPU:63, one launch (start us, length us, event | category | flops | bytes accessed | tf_op | source)
XLA Modules:
  0.0 288.0 jit_solution(12877057527456263008)
XLA Ops:
  7.2 0.7 all-gather.7.cloned.1.call-update
  8.0 1.9 fusion.2
  9.9 3.5 %broadcast_in_dim.60 = bf16[1024,3584]{1,0:T(8,128)(2,1)} broadcast(bf16[]{:T(256)} %constant.111.clone.1), dimensions={} | broadcast | bytes 7340034 | tf_op jit(solution)/shard_map/broadcast_in_dim | solution.py:146
  13.4 1.9 constant_dynamic-update-slice_fusion.3
  15.4 2.2 collective-permute-start.1
  18.0 38.3 %collective-permute-done = bf16[256,3584]{1,0:T(8,128)(2,1)} collective-permute-done((bf16[256,3584]{1,0:T(8,128)(2,1)S(1)}, bf16[256,3584]{1,0:T(8,128)(2,1)}, u32[]{:S(2)}, u32[]{:S(2)}) %collective-permute-start) | collective-permute-done | bytes 1835040 | tf_op jit(solution)/shard_map/ppermute | solution.py:145
  56.3 3.0 %constant_dynamic-update-slice_fusion.2 = bf16[1024,3584]{1,0:T(8,128)(2,1)} fusion(bf16[1024,3584]{1,0:T(8,128)(2,1)} %get-tuple-element.2, bf16[256,3584]{1,0:T(8,128)(2,1)} %collective-permute-done, s32[]{:T(128)S(6)} %select_n.112), kind=kLoop, calls=%fused_computation.38 | loop fusion | bytes 3670020 | tf_op jit(solution)/shard_map/dynamic_update_slice | solution.py:149
  59.3 3.0 %constant_dynamic-update-slice_fusion.1 = bf16[1024,3584]{1,0:T(8,128)(2,1)} fusion(bf16[1024,3584]{1,0:T(8,128)(2,1)} %constant_dynamic-update-slice_fusion.2, bf16[256,3584]{1,0:T(8,128)(2,1)} %collective-permute-done.1, s32[]{:T(128)S(6)} %select_n.114), kind=kLoop, calls=%fused_computation.37 | loop fusion | bytes 3670020 | tf_op jit(solution)/shard_map/dynamic_update_slice | solution.py:149
  62.3 36.0 %collective-permute-done.2 = bf16[256,3584]{1,0:T(8,128)(2,1)} collective-permute-done((bf16[256,3584]{1,0:T(8,128)(2,1)S(1)}, bf16[256,3584]{1,0:T(8,128)(2,1)}, u32[]{:S(2)}, u32[]{:S(2)}) %collective-permute-start.2) | collective-permute-done | bytes 1835040 | tf_op jit(solution)/shard_map/ppermute | solution.py:145
  98.3 2.8 constant_dynamic-update-slice_fusion
  101.1 12.8 %copy.56 = bf16[8,4,448,288]{2,0,3,1:T(8,128)(2,1)} copy(bf16[8,4,448,288]{2,3,1,0:T(8,128)(2,1)} %bitcast.66) | data formatting | bytes 16515072 | tf_op jit(solution)/shard_map/reshape | solution.py:151
  113.9 17.1 %reshape.151 = bf16[3584,4,288]{0,2,1:T(8,128)(2,1)} reshape(bf16[8,448,4,288]{1,0,3,2:T(8,128)(2,1)} %bitcast.65) | data formatting | bytes 16515072 | tf_op jit(solution)/shard_map/reshape | solution.py:152
  131.0 13.3 %add_convert_fusion = bf16[1024,4,288]{0,2,1:T(8,128)(2,1)S(1)} fusion(bf16[3584,4,288]{0,2,1:T(8,128)(2,1)} %reshape.151, bf16[1024,3584]{1,0:T(8,128)(2,1)} %constant_dynamic-update-slice_fusion, f32[4,288]{1,0:T(4,128)S(1)} %bitcast.76), kind=kOutput, calls=%fused_computation.3 | convolution fusion | flops 8458076160 | bytes 17961472 | tf_op jit(solution)/shard_map/td,dyc->tyc/dot_general | solution.py:153
  144.3 1.5 copy-done.1
  146.0 2.7 collective-permute-start.6
  149.3 0.6 collective-permute-start.8
  149.9 1.4 collective-permute-done.6
  151.3 3.6 %collective-permute-done.7 = bf16[256,288]{0,1:T(8,128)(2,1)S(1)} collective-permute-done((bf16[256,288]{0,1:T(8,128)(2,1)S(1)}, bf16[256,288]{0,1:T(8,128)(2,1)S(1)}, u32[]{:S(2)}, u32[]{:S(2)}) %collective-permute-start.7) | collective-permute-done | bytes 147488 | tf_op jit(solution)/shard_map/ppermute | solution.py:165
  154.9 4.2 %collective-permute-done.8 = bf16[256,288]{0,1:T(8,128)(2,1)S(1)} collective-permute-done((bf16[256,288]{0,1:T(8,128)(2,1)S(1)}, bf16[256,288]{0,1:T(8,128)(2,1)S(1)}, u32[]{:S(2)}, u32[]{:S(2)}) %collective-permute-start.8) | collective-permute-done | bytes 147488 | tf_op jit(solution)/shard_map/ppermute | solution.py:165
  160.6 0.9 pad_maximum_fusion.2
  161.5 1.6 slice.36
  163.1 1.2 constant_dynamic-slice_fusion
  164.3 0.7 fusion.7
  167.8 0.6 pad_add_fusion.meta
  168.4 1.5 collective-permute-start.5
  170.1 5.0 %collective-permute-done.3 = bf16[256,3,288]{0,2,1:T(8,128)(2,1)S(1)} collective-permute-done((bf16[256,3,288]{0,2,1:T(8,128)(2,1)}, bf16[256,3,288]{0,2,1:T(8,128)(2,1)S(1)}, u32[]{:S(2)}, u32[]{:S(2)}) %collective-permute-start.3) | collective-permute-done | bytes 442400 | tf_op jit(solution)/shard_map/ppermute | solution.py:165
  175.1 7.3 %collective-permute-done.4 = bf16[256,3,288]{0,2,1:T(8,128)(2,1)S(1)} collective-permute-done((bf16[256,3,288]{0,2,1:T(8,128)(2,1)}, bf16[256,3,288]{0,2,1:T(8,128)(2,1)S(1)}, u32[]{:S(2)}, u32[]{:S(2)}) %collective-permute-start.4) | collective-permute-done | bytes 442400 | tf_op jit(solution)/shard_map/ppermute | solution.py:165
  182.5 17.0 %collective-permute-done.5 = bf16[256,3,288]{0,2,1:T(8,128)(2,1)S(1)} collective-permute-done((bf16[256,3,288]{0,2,1:T(8,128)(2,1)}, bf16[256,3,288]{0,2,1:T(8,128)(2,1)S(1)}, u32[]{:S(2)}, u32[]{:S(2)}) %collective-permute-start.5) | collective-permute-done | bytes 442400 | tf_op jit(solution)/shard_map/ppermute | solution.py:165
  200.1 0.6 subtract_convert_fusion
  200.8 1.4 pad_maximum_fusion.1
  202.2 41.3 %all-gather.5.cloned.1.call-done.k_ref.v_ref = bf16[4096,1024]{1,0:T(8,128)(2,1)} async-done(((bf16[256,1024]{1,0:T(8,128)(2,1)}), bf16[4096,1024]{1,0:T(8,128)(2,1)}) %all-gather.5.cloned.1.call-update) | async-done | bytes 8388624 | tf_op jit(solution)/shard_map/all_gather | solution.py:195
  243.5 37.7 %shard_map.68 = bf16[256,3584]{1,0:T(8,128)(2,1)} custom-call(s32[8]{0:T(128)} %pad_add_fusion.meta, bf16[3584,256]{1,0:T(8,128)(2,1)} %bitcast.67, bf16[4096,1024]{1,0:T(8,128)(2,1)} %all-gather.5.cloned.1.call-done.k_ref.v_ref, bf16[4096,1024]{1,0:T(8,128)(2,1)} %all-gather.5.cloned.1.call-done.k_ref.v_ref), custom_call_target="tpu_custom_call" | custom-call | tf_op jit(solution)/shard_map/pallas_call | solution.py:103
  (54 shorter events, 3.7 us)
Async XLA Ops:
  7.2 94.0 %all-gather.7.cloned.1.call-start = ((), (), s32[]{:S(2)}) async-start(), calls=%async_computation.1 | async-start | bytes 9732096 | tf_op jit(solution)/shard_map/all_gather | solution.py:150
  7.9 235.6 %all-gather.5.cloned.1.call-start = ((), (), s32[]{:S(2)}) async-start(), calls=%async_computation | async-start | bytes 8912896 | tf_op jit(solution)/shard_map/all_gather | solution.py:195
  9.9 3.5 %copy-start = (bf16[256,3584]{1,0:T(8,128)(2,1)S(1)}, bf16[256,3584]{1,0:T(8,128)(2,1)}, u32[]{:S(2)}) copy-start(bf16[256,3584]{1,0:T(8,128)(2,1)} %param.5) | copy-start | bytes 5505028
  9.9 3.5 %copy-start.3 = (f32[3584]{0:T(1024)S(1)}, f32[3584]{0:T(1024)}, u32[]{:S(2)}) copy-start(f32[3584]{0:T(1024)} %param.7) | copy-start | bytes 43012
  13.4 4.1 %copy-start.2 = (f32[4608]{0:T(1024)S(1)}, f32[4608]{0:T(1024)}, u32[]{:S(2)}) copy-start(f32[4608]{0:T(1024)} %param.9) | copy-start | bytes 55300
  13.4 4.3 %copy-start.4 = (s32[1,4]{1,0:T(1,128)S(1)}, s32[1,4]{1,0:T(1,128)}, u32[]{:S(2)}) copy-start(s32[1,4]{1,0:T(1,128)} %param.6) | copy-start | bytes 52
  15.3 41.0 %collective-permute-start = (bf16[256,3584]{1,0:T(8,128)(2,1)S(1)}, bf16[256,3584]{1,0:T(8,128)(2,1)}, u32[]{:S(2)}, u32[]{:S(2)}) collective-permute-start(bf16[256,3584]{1,0:T(8,128)(2,1)S(1)} %get-tuple-element.3), channel_id=1, source_target_pairs={{0,1},{1,2},{2,3},{3,0},{4,5},{5,6},{6,7},{7,4},{8,9},{9,10},{10,1... | collective-permute-start | bytes 5505032 | tf_op jit(solution)/shard_map/ppermute | solution.py:145
  15.4 43.9 %collective-permute-start.1 = (bf16[256,3584]{1,0:T(8,128)(2,1)S(1)}, bf16[256,3584]{1,0:T(8,128)(2,1)}, u32[]{:S(2)}, u32[]{:S(2)}) collective-permute-start(bf16[256,3584]{1,0:T(8,128)(2,1)S(1)} %get-tuple-element.3), channel_id=1, source_target_pairs={{0,2},{1,3},{2,0},{3,1},{4,6},{5,7},{6,4},{7,5},{8,10},{9,11},{10,... | collective-permute-start | bytes 5505032 | tf_op jit(solution)/shard_map/ppermute | solution.py:145
  17.6 80.7 %collective-permute-start.2 = (bf16[256,3584]{1,0:T(8,128)(2,1)S(1)}, bf16[256,3584]{1,0:T(8,128)(2,1)}, u32[]{:S(2)}, u32[]{:S(2)}) collective-permute-start(bf16[256,3584]{1,0:T(8,128)(2,1)S(1)} %get-tuple-element.3), channel_id=1, source_target_pairs={{0,3},{1,0},{2,1},{3,2},{4,7},{5,4},{6,5},{7,6},{8,11},{9,8},{10,9... | collective-permute-start | bytes 5505032 | tf_op jit(solution)/shard_map/ppermute | solution.py:145
  144.3 1.5 copy-start.1
  146.0 5.3 %collective-permute-start.6 = (bf16[256,288]{0,1:T(8,128)(2,1)S(1)}, bf16[256,288]{0,1:T(8,128)(2,1)S(1)}, u32[]{:S(2)}, u32[]{:S(2)}) collective-permute-start(bf16[256,288]{0,1:T(8,128)(2,1)S(1)} %get-tuple-element.15), channel_id=1, source_target_pairs={{0,1},{1,2},{2,3},{3,0},{4,5},{5,6},{6,7},{7,4},{8,9},{9,10},{10,1... | collective-permute-start | bytes 442376 | tf_op jit(solution)/shard_map/ppermute | solution.py:165
  149.2 5.7 %collective-permute-start.7 = (bf16[256,288]{0,1:T(8,128)(2,1)S(1)}, bf16[256,288]{0,1:T(8,128)(2,1)S(1)}, u32[]{:S(2)}, u32[]{:S(2)}) collective-permute-start(bf16[256,288]{0,1:T(8,128)(2,1)S(1)} %get-tuple-element.14), channel_id=1, source_target_pairs={{0,2},{1,3},{2,0},{3,1},{4,6},{5,7},{6,4},{7,5},{8,10},{9,11},{10,... | collective-permute-start | bytes 442376 | tf_op jit(solution)/shard_map/ppermute | solution.py:165
  149.3 9.8 %collective-permute-start.8 = (bf16[256,288]{0,1:T(8,128)(2,1)S(1)}, bf16[256,288]{0,1:T(8,128)(2,1)S(1)}, u32[]{:S(2)}, u32[]{:S(2)}) collective-permute-start(bf16[256,288]{0,1:T(8,128)(2,1)S(1)} %get-tuple-element.13), channel_id=1, source_target_pairs={{0,3},{1,0},{2,1},{3,2},{4,7},{5,4},{6,5},{7,6},{8,11},{9,8},{10,9... | collective-permute-start | bytes 442376 | tf_op jit(solution)/shard_map/ppermute | solution.py:165
  164.3 10.9 %collective-permute-start.3 = (bf16[256,3,288]{0,2,1:T(8,128)(2,1)}, bf16[256,3,288]{0,2,1:T(8,128)(2,1)S(1)}, u32[]{:S(2)}, u32[]{:S(2)}) collective-permute-start(bf16[256,3,288]{0,2,1:T(8,128)(2,1)} %get-tuple-element.8), channel_id=1, source_target_pairs={{0,1},{1,2},{2,3},{3,0},{4,5},{5,6},{6,7},{7,4},{8,9},{9,10},{10,1... | collective-permute-start | bytes 1327112 | tf_op jit(solution)/shard_map/ppermute | solution.py:165
  167.7 14.7 %collective-permute-start.4 = (bf16[256,3,288]{0,2,1:T(8,128)(2,1)}, bf16[256,3,288]{0,2,1:T(8,128)(2,1)S(1)}, u32[]{:S(2)}, u32[]{:S(2)}) collective-permute-start(bf16[256,3,288]{0,2,1:T(8,128)(2,1)} %get-tuple-element.7), channel_id=1, source_target_pairs={{0,2},{1,3},{2,0},{3,1},{4,6},{5,7},{6,4},{7,5},{8,10},{9,11},{10,... | collective-permute-start | bytes 1327112 | tf_op jit(solution)/shard_map/ppermute | solution.py:165
  168.4 31.1 %collective-permute-start.5 = (bf16[256,3,288]{0,2,1:T(8,128)(2,1)}, bf16[256,3,288]{0,2,1:T(8,128)(2,1)S(1)}, u32[]{:S(2)}, u32[]{:S(2)}) collective-permute-start(bf16[256,3,288]{0,2,1:T(8,128)(2,1)} %get-tuple-element.6), channel_id=1, source_target_pairs={{0,3},{1,0},{2,1},{3,2},{4,7},{5,4},{6,5},{7,6},{8,11},{9,8},{10,9... | collective-permute-start | bytes 1327112 | tf_op jit(solution)/shard_map/ppermute | solution.py:165
Sparse Core Ops, SparseCore 0:
  10.2 55.9 all-gather.6
  161.6 81.8 all-gather.4

commit v8 on v7

--- a/solution.py
+++ b/solution.py
@@ -143,31 +143,31 @@
     for step in range(1, n_x):
         pairs = [(s, (s + step) % n_x) for s in range(n_x)]
         shifted.append(lax.ppermute(normed, "x", pairs))
-    grouped = jnp.zeros((n_x * rows, normed.shape[1]), normed.dtype)
-    for step, piece in enumerate(shifted):
-        at = ((here - step) % n_x) * rows
-        grouped = lax.dynamic_update_slice_in_dim(grouped, piece, at, 0)
     pieces = lax.all_gather(weight, ("z", "c", "y"), axis=0, tiled=False)
     pieces = pieces.reshape(-1, n_y, weight.shape[0], width)
-    pieces = jnp.transpose(pieces, (0, 2, 1, 3)).reshape(grouped.shape[1], n_y, width)
-    summed = jnp.einsum("td,dyc->tyc", grouped, pieces, preferred_element_type=jnp.float32)
     bias_block = bias.reshape(n_y, n_x, width)
-    bias_block = lax.dynamic_index_in_dim(bias_block, lax.axis_index("x"), 1, keepdims=False)
-    block_out = (summed + bias_block[None]).astype(jnp.bfloat16)
-
-    def exchange(part):
-        mine = lax.dynamic_slice_in_dim(part, here * rows, rows, 0)
-        full = jnp.zeros((rows, n_x) + part.shape[1:], part.dtype)
-        full = lax.dynamic_update_slice_in_dim(full, mine[:, None], here, 1)
+    bias_block = lax.dynamic_index_in_dim(bias_block, here, 1, keepdims=False)
+    outs = []
+    for piece in shifted:
+        summed = jnp.einsum(
+            "tie,iyec->tyc",
+            piece.reshape(rows, pieces.shape[0], weight.shape[0]),
+            pieces,
+            preferred_element_type=jnp.float32,
+        )
+        outs.append((summed + bias_block[None]).astype(jnp.bfloat16))
+
+    def exchange(take):
+        full = jnp.zeros((rows, n_x) + take(outs[0]).shape[1:], outs[0].dtype)
+        full = lax.dynamic_update_slice_in_dim(full, take(outs[0])[:, None], here, 1)
         for step in range(1, n_x):
-            sent = lax.dynamic_slice_in_dim(part, ((here + step) % n_x) * rows, rows, 0)
             pairs = [(s, (s + step) % n_x) for s in range(n_x)]
-            got = lax.ppermute(sent, "x", pairs)
+            got = lax.ppermute(take(outs[(n_x - step) % n_x]), "x", pairs)
             full = lax.dynamic_update_slice_in_dim(full, got[:, None], (here - step) % n_x, 1)
         return full
 
-    tail = exchange(block_out[:, n_y - 1]).reshape(rows, -1)
-    head = exchange(block_out[:, : n_y - 1])
+    tail = exchange(lambda out: out[:, n_y - 1]).reshape(rows, -1)
+    head = exchange(lambda out: out[:, : n_y - 1])
     head = jnp.transpose(head, (0, 2, 1, 3))
     return head.reshape(rows, -1), tail
 

time: 291 us -> 256 us (0.88)
  the two profiles are of different devices: /device:TPU:63 before, /device:TPU:23 now
where the time goes in v8:
time: 256 us; the launch traced here: 253 us
  waiting for transfers between devices  154 us (60%)
  Pallas kernels  37.7 us (15%)
  matrix products  18.9 us (7%)
  between operations  17 us (7%)
  other arithmetic  10 us (4%)
  local copies, waits for them, and re-layouts  7.74 us (3%)
  starting transfers between devices  7.14 us (3%)
    ppermute x3, waiting for transfers between devices, project_joined(): shifted.append(lax.ppermute(normed, 'x', pairs))  76.3 us
    all_gather x1, waiting for transfers between devices, on_device(): piece = lax.all_gather(kv_rows, ('y', 'x'), axis=0, tiled=True)  42.5 us
    pallas_call x1, Pallas kernels, flash(): pl.pallas_call(flash_body, grid_spec=spec, out_shape=jax.ShapeDtypeStruct...  37.7 us
    ppermute x6, waiting for transfers between devices, exchange(): got = lax.ppermute(take(outs[(n_x - step) % n_x]), 'x', pairs)  35 us
    dot_general x4, matrix products, project_joined(): jnp.einsum('tie,iyec->tyc', piece.reshape(rows, pieces.shape[0], weight.s...  18.9 us
  transfers between devices with their start and end apart: 11, of which 6 were waited for; matrix products, arithmetic and copies ran while one was open for 13% of the time, Pallas kernels for 0%

profile of v8, /device:TPU:23, one launch (start us, length us, event | category | flops | bytes accessed | tf_op | source)
XLA Modules:
  0.0 253.0 jit_solution(5578295273336679175)
XLA Ops:
  7.2 0.7 all-gather.7.cloned.1.call-update
  7.9 2.9 %copy.60 = bf16[256,3584]{0,1:T(8,128)(2,1)S(1)} copy(bf16[256,3584]{1,0:T(8,128)(2,1)} %param.5) | data formatting | bytes 3670016 | tf_op args[0]
  10.9 0.5 fusion
  11.6 2.5 fusion.2
  14.0 0.5 collective-permute-start
  14.6 0.8 collective-permute-start.2
  15.4 1.8 collective-permute-start.4
  18.0 0.8 copy.72
  18.7 0.7 copy.70
  19.5 76.3 %collective-permute-done = bf16[256,3584]{0,1:T(8,128)(2,1)} collective-permute-done((bf16[256,3584]{0,1:T(8,128)(2,1)}, bf16[256,3584]{0,1:T(8,128)(2,1)}, u32[]{:S(2)}, u32[]{:S(2)}) %collective-permute-start) | collective-permute-done | bytes 1835040 | tf_op jit(solution)/shard_map/ppermute | solution.py:145
  95.8 6.8 %fusion.9 = bf16[256,4,288]{0,2,1:T(8,128)(2,1)S(1)} fusion(bf16[256,8,448,1]{0,2,3,1:T(8,128)(2,1)} %bitcast.59, bf16[8,4,448,288]{2,3,1,0:T(8,128)(2,1)} %bitcast.137, f32[4,288]{1,0:T(4,128)S(1)} %bitcast.129), kind=kOutput, calls=%fused_computation.19 | convolution fusion | flops 2114519040 | bytes 10686976 | tf_op jit(solution)/shard_map/tie,iyec->tyc/dot_general | solution.py:152
  102.7 4.1 %fusion.8 = bf16[256,4,288]{0,2,1:T(8,128)(2,1)S(1)} fusion(bf16[256,8,448,1]{0,2,3,1:T(8,128)(2,1)} %bitcast.61, bf16[8,4,448,288]{2,3,1,0:T(8,128)(2,1)S(1)} %bitcast.138, f32[4,288]{1,0:T(4,128)S(1)} %bitcast.130), kind=kOutput, calls=%fused_computation.18 | convolution fusion | flops 2114519040 | bytes 10686976 | tf_op jit(solution)/shard_map/tie,iyec->tyc/dot_general | solution.py:152
  107.1 4.0 %fusion.10 = bf16[256,4,288]{0,2,1:T(8,128)(2,1)S(1)} fusion(bf16[256,8,448,1]{0,2,3,1:T(8,128)(2,1)} %bitcast.57, bf16[8,4,448,288]{2,3,1,0:T(8,128)(2,1)S(1)} %bitcast.139, f32[4,288]{1,0:T(4,128)S(1)} %bitcast.131), kind=kOutput, calls=%fused_computation.20 | convolution fusion | flops 2114519040 | bytes 10686976 | tf_op jit(solution)/shard_map/tie,iyec->tyc/dot_general | solution.py:152
  111.2 4.0 %fusion.7 = bf16[256,4,288]{0,2,1:T(8,128)(2,1)S(1)} fusion(bf16[256,8,448,1]{0,2,3,1:T(8,128)(2,1)} %bitcast.63, bf16[8,4,448,288]{2,3,1,0:T(8,128)(2,1)S(1)} %bitcast.140, f32[4,288]{1,0:T(4,128)S(1)} %bitcast.132), kind=kOutput, calls=%fused_computation.17 | convolution fusion | flops 2114519040 | bytes 10686976 | tf_op jit(solution)/shard_map/tie,iyec->tyc/dot_general | solution.py:152
  115.2 1.4 collective-permute-start.8
  116.8 4.8 %collective-permute-done.8 = bf16[256,288]{0,1:T(8,128)(2,1)S(1)} collective-permute-done((bf16[256,288]{0,1:T(8,128)(2,1)S(1)}, bf16[256,288]{0,1:T(8,128)(2,1)S(1)}, u32[]{:S(2)}, u32[]{:S(2)}) %collective-permute-start.8) | collective-permute-done | bytes 147488 | tf_op jit(solution)/shard_map/ppermute | solution.py:165
  122.3 1.2 subtract_convert_fusion.1
  123.5 0.4 pad_maximum_fusion.3
  124.0 0.9 pad_maximum_fusion.2
  124.9 1.8 slice.61
  126.7 1.5 collective-permute-start.1
  128.1 0.7 fusion.12
  131.4 0.7 pad_add_fusion.meta
  132.2 0.6 collective-permute-start.5
  133.0 2.7 %collective-permute-done.1 = bf16[256,3,288]{0,2,1:T(8,128)(2,1)S(1)} collective-permute-done((bf16[256,3,288]{0,2,1:T(8,128)(2,1)}, bf16[256,3,288]{0,2,1:T(8,128)(2,1)S(1)}, u32[]{:S(2)}, u32[]{:S(2)}) %collective-permute-start.1) | collective-permute-done | bytes 442400 | tf_op jit(solution)/shard_map/ppermute | solution.py:165
  135.7 6.3 %collective-permute-done.3 = bf16[256,3,288]{0,2,1:T(8,128)(2,1)S(1)} collective-permute-done((bf16[256,3,288]{0,2,1:T(8,128)(2,1)S(1)}, bf16[256,3,288]{0,2,1:T(8,128)(2,1)S(1)}, u32[]{:S(2)}, u32[]{:S(2)}) %collective-permute-start.3) | collective-permute-done | bytes 442400 | tf_op jit(solution)/shard_map/ppermute | solution.py:165
  142.0 21.2 %collective-permute-done.5 = bf16[256,3,288]{0,2,1:T(8,128)(2,1)S(1)} collective-permute-done((bf16[256,3,288]{0,2,1:T(8,128)(2,1)S(1)}, bf16[256,3,288]{0,2,1:T(8,128)(2,1)S(1)}, u32[]{:S(2)}, u32[]{:S(2)}) %collective-permute-start.5) | collective-permute-done | bytes 442400 | tf_op jit(solution)/shard_map/ppermute | solution.py:165
  163.4 0.4 convert.18
  163.9 0.6 subtract_convert_fusion
  164.5 1.4 pad_maximum_fusion.1
  166.0 42.5 %all-gather.5.cloned.1.call-done.k_ref.v_ref = bf16[4096,1024]{1,0:T(8,128)(2,1)} async-done(((bf16[256,1024]{1,0:T(8,128)(2,1)}), bf16[4096,1024]{1,0:T(8,128)(2,1)}) %all-gather.5.cloned.1.call-update) | async-done | bytes 8388624 | tf_op jit(solution)/shard_map/all_gather | solution.py:195
  208.5 37.7 %shard_map.68 = bf16[256,3584]{1,0:T(8,128)(2,1)} custom-call(s32[8]{0:T(128)} %pad_add_fusion.meta, bf16[3584,256]{1,0:T(8,128)(2,1)} %bitcast.120, bf16[4096,1024]{1,0:T(8,128)(2,1)} %all-gather.5.cloned.1.call-done.k_ref.v_ref, bf16[4096,1024]{1,0:T(8,128)(2,1)} %all-gather.5.cloned.1.call-done.k_ref.v_ref), custom_call_target="tpu_custom_call" | custom-call | tf_op jit(solution)/shard_map/pallas_call | solution.py:103
  (59 shorter events, 2.8 us)
Async XLA Ops:
  7.2 88.6 %all-gather.7.cloned.1.call-start = ((), (), s32[]{:S(2)}) async-start(), calls=%async_computation.1 | async-start | bytes 9732096 | tf_op jit(solution)/shard_map/all_gather | solution.py:146
  7.9 200.6 %all-gather.5.cloned.1.call-start = ((), (), s32[]{:S(2)}) async-start(), calls=%async_computation | async-start | bytes 8912896 | tf_op jit(solution)/shard_map/all_gather | solution.py:195
  10.8 0.7 copy-start.4
  11.6 5.7 %copy-start.5 = (s32[1,4]{1,0:T(1,128)S(1)}, s32[1,4]{1,0:T(1,128)}, u32[]{:S(2)}) copy-start(s32[1,4]{1,0:T(1,128)} %param.6) | copy-start | bytes 52
  11.6 5.9 %copy-start.3 = (f32[4608]{0:T(1024)S(1)}, f32[4608]{0:T(1024)}, u32[]{:S(2)}) copy-start(f32[4608]{0:T(1024)} %param.9) | copy-start | bytes 55300
  14.0 81.7 %collective-permute-start = (bf16[256,3584]{0,1:T(8,128)(2,1)}, bf16[256,3584]{0,1:T(8,128)(2,1)}, u32[]{:S(2)}, u32[]{:S(2)}) collective-permute-start(bf16[256,3584]{0,1:T(8,128)(2,1)} %fusion.2), channel_id=1, source_target_pairs={{0,3},{1,0},{2,1},{3,2},{4,7},{5,4},{6,5},{7,6},{8,11},{9,8},{10,9... | collective-permute-start | bytes 5505032 | tf_op jit(solution)/shard_map/ppermute | solution.py:145
  14.6 88.1 %collective-permute-start.2 = (bf16[256,3584]{0,1:T(8,128)(2,1)}, bf16[256,3584]{0,1:T(8,128)(2,1)}, u32[]{:S(2)}, u32[]{:S(2)}) collective-permute-start(bf16[256,3584]{0,1:T(8,128)(2,1)} %fusion.2), channel_id=1, source_target_pairs={{0,2},{1,3},{2,0},{3,1},{4,6},{5,7},{6,4},{7,5},{8,10},{9,11},{10,... | collective-permute-start | bytes 5505032 | tf_op jit(solution)/shard_map/ppermute | solution.py:145
  15.4 95.7 %collective-permute-start.4 = (bf16[256,3584]{0,1:T(8,128)(2,1)}, bf16[256,3584]{0,1:T(8,128)(2,1)}, u32[]{:S(2)}, u32[]{:S(2)}) collective-permute-start(bf16[256,3584]{0,1:T(8,128)(2,1)} %fusion.2), channel_id=1, source_target_pairs={{0,1},{1,2},{2,3},{3,0},{4,5},{5,6},{6,7},{7,4},{8,9},{9,10},{10,1... | collective-permute-start | bytes 5505032 | tf_op jit(solution)/shard_map/ppermute | solution.py:145
  95.8 6.9 %copy-start.6 = (bf16[32,448,288]{1,2,0:T(8,128)(2,1)S(1)}, bf16[32,448,288]{1,2,0:T(8,128)(2,1)}, u32[]{:S(2)}) copy-start(bf16[32,448,288]{1,2,0:T(8,128)(2,1)} %all-gather.7.cloned.1.call-done) | copy-start | bytes 24772612
  102.6 4.2 %copy-start.2 = (bf16[256,4,288]{0,2,1:T(8,128)(2,1)}, bf16[256,4,288]{0,2,1:T(8,128)(2,1)S(1)}, u32[]{:S(2)}) copy-start(bf16[256,4,288]{0,2,1:T(8,128)(2,1)S(1)} %fusion.9) | copy-start | bytes 1769476
  102.6 14.1 %collective-permute-start.6 = (bf16[256,288]{0,1:T(8,128)(2,1)S(1)}, bf16[256,288]{0,1:T(8,128)(2,1)S(1)}, u32[]{:S(2)}, u32[]{:S(2)}) collective-permute-start(bf16[256,288]{0,1:T(8,128)(2,1)S(1)} %slice_bitcast_fusion.3), channel_id=1, source_target_pairs={{0,1},{1,2},{2,3},{3,0},{4,5},{5,6},{6,7},{7,4},{8,9},{9,10},{10,1... | collective-permute-start | bytes 442376 | tf_op jit(solution)/shard_map/ppermute | solution.py:165
  106.9 9.9 %collective-permute-start.7 = (bf16[256,288]{0,1:T(8,128)(2,1)S(1)}, bf16[256,288]{0,1:T(8,128)(2,1)S(1)}, u32[]{:S(2)}, u32[]{:S(2)}) collective-permute-start(bf16[256,288]{0,1:T(8,128)(2,1)S(1)} %slice_bitcast_fusion.2), channel_id=1, source_target_pairs={{0,2},{1,3},{2,0},{3,1},{4,6},{5,7},{6,4},{7,5},{8,10},{9,11},{10,... | collective-permute-start | bytes 442376 | tf_op jit(solution)/shard_map/ppermute | solution.py:165
  115.2 6.4 %copy-start = (bf16[256,4,288]{0,2,1:T(8,128)(2,1)}, bf16[256,4,288]{0,2,1:T(8,128)(2,1)S(1)}, u32[]{:S(2)}) copy-start(bf16[256,4,288]{0,2,1:T(8,128)(2,1)S(1)} %fusion.7) | copy-start | bytes 1769476
  115.2 6.3 %collective-permute-start.8 = (bf16[256,288]{0,1:T(8,128)(2,1)S(1)}, bf16[256,288]{0,1:T(8,128)(2,1)S(1)}, u32[]{:S(2)}, u32[]{:S(2)}) collective-permute-start(bf16[256,288]{0,1:T(8,128)(2,1)S(1)} %slice_bitcast_fusion.1), channel_id=1, source_target_pairs={{0,3},{1,0},{2,1},{3,2},{4,7},{5,4},{6,5},{7,6},{8,11},{9,8},{10,9... | collective-permute-start | bytes 442376 | tf_op jit(solution)/shard_map/ppermute | solution.py:165
  123.9 8.2 %copy-start.1 = (bf16[256,4,288]{0,2,1:T(8,128)(2,1)S(1)}, bf16[256,4,288]{0,2,1:T(8,128)(2,1)}, u32[]{:S(2)}) copy-start(bf16[256,4,288]{0,2,1:T(8,128)(2,1)} %copy-done) | copy-start | bytes 1769476
  126.7 9.0 %collective-permute-start.1 = (bf16[256,3,288]{0,2,1:T(8,128)(2,1)}, bf16[256,3,288]{0,2,1:T(8,128)(2,1)S(1)}, u32[]{:S(2)}, u32[]{:S(2)}) collective-permute-start(bf16[256,3,288]{0,2,1:T(8,128)(2,1)} %slice.61), channel_id=1, source_target_pairs={{0,1},{1,2},{2,3},{3,0},{4,5},{5,6},{6,7},{7,4},{8,9},{9,10},{10,1... | collective-permute-start | bytes 1327112 | tf_op jit(solution)/shard_map/ppermute | solution.py:165
  132.1 9.9 %collective-permute-start.3 = (bf16[256,3,288]{0,2,1:T(8,128)(2,1)S(1)}, bf16[256,3,288]{0,2,1:T(8,128)(2,1)S(1)}, u32[]{:S(2)}, u32[]{:S(2)}) collective-permute-start(bf16[256,3,288]{0,2,1:T(8,128)(2,1)S(1)} %slice.62), channel_id=1, source_target_pairs={{0,2},{1,3},{2,0},{3,1},{4,6},{5,7},{6,4},{7,5},{8,10},{9,11},{10,... | collective-permute-start | bytes 1327112 | tf_op jit(solution)/shard_map/ppermute | solution.py:165
  132.2 31.1 %collective-permute-start.5 = (bf16[256,3,288]{0,2,1:T(8,128)(2,1)S(1)}, bf16[256,3,288]{0,2,1:T(8,128)(2,1)S(1)}, u32[]{:S(2)}, u32[]{:S(2)}) collective-permute-start(bf16[256,3,288]{0,2,1:T(8,128)(2,1)S(1)} %slice.63), channel_id=1, source_target_pairs={{0,3},{1,0},{2,1},{3,2},{4,7},{5,4},{6,5},{7,6},{8,11},{9,8},{10,9... | collective-permute-start | bytes 1327112 | tf_op jit(solution)/shard_map/ppermute | solution.py:165
Sparse Core Ops, SparseCore 0:
  10.2 57.8 all-gather.6
  125.0 83.4 all-gather.4

commit v9 on v8

--- a/solution.py
+++ b/solution.py
@@ -19,8 +19,8 @@
 
 
 def flash_body(meta, q_ref, k_ref, v_ref, o_ref, bias_ref, m_ref, l_ref, acc_ref):
-    step = pl.program_id(1)
-    last = pl.num_programs(1) - 1
+    step = pl.program_id(0)
+    last = pl.num_programs(0) - 1
     first = meta[4] * BLOCK
     block = jnp.minimum(meta[5] + step, meta[4])
     group = HEADS // KV_HEADS
@@ -41,33 +41,36 @@
             qstart = jnp.where(end <= qcol, end, qstart)
         allowed = (krow >= qstart) & (krow <= qcol)
         bias_ref[...] = jnp.where(allowed, 0.0, -1e30).astype(jnp.float32)
-        keys = k_ref[...]
-        values = jnp.transpose(v_ref[...].astype(jnp.float32)).astype(jnp.bfloat16)
         scale = 1.0 / HEAD_DIM**0.5
-        for h in range(group):
-            heads = slice(h * HEAD_DIM, (h + 1) * HEAD_DIM)
-            for c in range(BLOCK // LANES):
-                cols = slice(c * LANES, (c + 1) * LANES)
-                q = q_ref[heads, cols]
-                scores = (
-                    jnp.dot(keys, q, preferred_element_type=jnp.float32) * scale
-                    + bias_ref[:, cols]
-                )
-                m_prev = m_ref[h, :, cols]
-                m_new = jnp.maximum(m_prev, jnp.max(scores, axis=0, keepdims=True))
-                shrink = jnp.exp(m_prev - m_new)
-                weights = jnp.exp(scores - m_new)
-                l_ref[h, :, cols] = l_ref[h, :, cols] * shrink + jnp.sum(
-                    weights, axis=0, keepdims=True
-                )
-                acc_ref[h, :, cols] = acc_ref[h, :, cols] * shrink + jnp.dot(
-                    values, weights.astype(jnp.bfloat16), preferred_element_type=jnp.float32
-                )
-                m_ref[h, :, cols] = m_new
+        for g in range(KV_HEADS):
+            dims = slice(g * HEAD_DIM, (g + 1) * HEAD_DIM)
+            keys = k_ref[:, dims]
+            values = jnp.transpose(v_ref[:, dims].astype(jnp.float32)).astype(jnp.bfloat16)
+            for hh in range(group):
+                h = g * group + hh
+                heads = slice(h * HEAD_DIM, (h + 1) * HEAD_DIM)
+                for c in range(BLOCK // LANES):
+                    cols = slice(c * LANES, (c + 1) * LANES)
+                    q = q_ref[heads, cols]
+                    scores = (
+                        jnp.dot(keys, q, preferred_element_type=jnp.float32) * scale
+                        + bias_ref[:, cols]
+                    )
+                    m_prev = m_ref[h, :, cols]
+                    m_new = jnp.maximum(m_prev, jnp.max(scores, axis=0, keepdims=True))
+                    shrink = jnp.exp(m_prev - m_new)
+                    weights = jnp.exp(scores - m_new)
+                    l_ref[h, :, cols] = l_ref[h, :, cols] * shrink + jnp.sum(
+                        weights, axis=0, keepdims=True
+                    )
+                    acc_ref[h, :, cols] = acc_ref[h, :, cols] * shrink + jnp.dot(
+                        values, weights.astype(jnp.bfloat16), preferred_element_type=jnp.float32
+                    )
+                    m_ref[h, :, cols] = m_new
 
     @pl.when(step == last)
     def _():
-        for h in range(group):
+        for h in range(HEADS):
             o_ref[:, h * HEAD_DIM : (h + 1) * HEAD_DIM] = jnp.transpose(
                 acc_ref[h] / l_ref[h]
             ).astype(o_ref.dtype)
@@ -75,36 +78,36 @@
 
 def flash(meta, queries_t, kv_all, steps):
     rows = queries_t.shape[1]
-    group = HEADS // KV_HEADS
-    width = group * HEAD_DIM
-
-    def key_map(g, t, meta):
-        return (jnp.minimum(meta[5] + t, meta[4]), g)
-
-    def value_map(g, t, meta):
-        return (jnp.minimum(meta[5] + t, meta[4]), KV_HEADS + g)
+    width = HEADS * HEAD_DIM
+    kdim = KV_HEADS * HEAD_DIM
+
+    def key_map(t, meta):
+        return (jnp.minimum(meta[5] + t, meta[4]), 0)
+
+    def value_map(t, meta):
+        return (jnp.minimum(meta[5] + t, meta[4]), 1)
 
     spec = pltpu.PrefetchScalarGridSpec(
         num_scalar_prefetch=1,
-        grid=(KV_HEADS, steps),
+        grid=(steps,),
         in_specs=[
-            pl.BlockSpec((width, rows), lambda g, t, meta: (g, 0)),
-            pl.BlockSpec((BLOCK, HEAD_DIM), key_map),
-            pl.BlockSpec((BLOCK, HEAD_DIM), value_map),
+            pl.BlockSpec((width, rows), lambda t, meta: (0, 0)),
+            pl.BlockSpec((BLOCK, kdim), key_map),
+            pl.BlockSpec((BLOCK, kdim), value_map),
         ],
-        out_specs=pl.BlockSpec((rows, width), lambda g, t, meta: (0, g)),
+        out_specs=pl.BlockSpec((rows, width), lambda t, meta: (0, 0)),
         scratch_shapes=[
             pltpu.VMEM((BLOCK, rows), jnp.float32),
-            pltpu.VMEM((group, 1, rows), jnp.float32),
-            pltpu.VMEM((group, 1, rows), jnp.float32),
-            pltpu.VMEM((group, HEAD_DIM, rows), jnp.float32),
+            pltpu.VMEM((HEADS, 1, rows), jnp.float32),
+            pltpu.VMEM((HEADS, 1, rows), jnp.float32),
+            pltpu.VMEM((HEADS, HEAD_DIM, rows), jnp.float32),
         ],
     )
     return pl.pallas_call(
         flash_body,
         grid_spec=spec,
-        out_shape=jax.ShapeDtypeStruct((rows, HEADS * HEAD_DIM), jnp.bfloat16),
-        compiler_params=pltpu.CompilerParams(dimension_semantics=("arbitrary", "arbitrary")),
+        out_shape=jax.ShapeDtypeStruct((rows, width), jnp.bfloat16),
+        compiler_params=pltpu.CompilerParams(dimension_semantics=("arbitrary",)),
     )(meta, queries_t, kv_all, kv_all)
 
 

time: 256 us -> 248 us (0.969)
  the two profiles are of different devices: /device:TPU:23 before, /device:TPU:29 now
where the time goes in v9:
time: 248 us; the launch traced here: 247 us
  waiting for transfers between devices  123 us (50%)
  starting transfers between devices  38.3 us (15%)
  Pallas kernels  32 us (13%)
  matrix products  18.8 us (8%)
  between operations  17 us (7%)
  other arithmetic  10 us (4%)
  local copies, waits for them, and re-layouts  7.75 us (3%)
    all_gather x1, waiting for transfers between devices, on_device(): piece = lax.all_gather(kv_rows, ('y', 'x'), axis=0, tiled=True)  45 us
    ppermute x3, waiting for transfers between devices, project_joined(): shifted.append(lax.ppermute(normed, 'x', pairs))  36.3 us
    ppermute x6, starting transfers between devices, exchange(): got = lax.ppermute(take(outs[(n_x - step) % n_x]), 'x', pairs)  35.5 us
    pallas_call x1, Pallas kernels, flash(): pl.pallas_call(flash_body, grid_spec=spec, out_shape=jax.ShapeDtypeStruct...  32 us
    ppermute x6, waiting for transfers between devices, exchange(): got = lax.ppermute(take(outs[(n_x - step) % n_x]), 'x', pairs)  28.6 us
    dot_general x4, matrix products, project_joined(): jnp.einsum('tie,iyec->tyc', piece.reshape(rows, pieces.shape[0], weight.s...  18.8 us
    all_gather x1, waiting for transfers between devices, project_joined(): pieces = lax.all_gather(weight, ('z', 'c', 'y'), axis=0, tiled=False)  12.8 us
  transfers between devices with their start and end apart: 11, of which 6 were waited for; matrix products, arithmetic and copies ran while one was open for 13% of the time, Pallas kernels for 0%

profile of v9, /device:TPU:29, one launch (start us, length us, event | category | flops | bytes accessed | tf_op | source)
XLA Modules:
  0.0 247.2 jit_solution(9705059273683968814)
XLA Ops:
  7.2 0.7 all-gather.7.cloned.1.call-update
  7.9 2.9 %copy.60 = bf16[256,3584]{0,1:T(8,128)(2,1)S(1)} copy(bf16[256,3584]{1,0:T(8,128)(2,1)} %param.5) | data formatting | bytes 3670016 | tf_op args[0]
  10.9 0.5 fusion
  11.6 2.5 %fusion.2 = bf16[256,3584]{0,1:T(8,128)(2,1)} fusion(bf16[256,3584]{0,1:T(8,128)(2,1)S(1)} %copy.60, f32[3584]{0:T(1024)S(1)} %copy-done.4, f32[256]{0:T(256)S(1)} %add_rsqrt_fusion), kind=kLoop, calls=%fused_computation.4 | loop fusion | flops 3670016 | bytes 3685376 | tf_op jit(solution)/shard_map/convert_element_type | solution.py:117
  14.3 2.5 collective-permute-start.2
  17.5 0.8 copy.72
  18.3 0.7 copy.70
  19.0 36.3 %collective-permute-done = bf16[256,3584]{0,1:T(8,128)(2,1)} collective-permute-done((bf16[256,3584]{0,1:T(8,128)(2,1)}, bf16[256,3584]{0,1:T(8,128)(2,1)}, u32[]{:S(2)}, u32[]{:S(2)}) %collective-permute-start) | collective-permute-done | bytes 1835040 | tf_op jit(solution)/shard_map/ppermute | solution.py:148
  55.3 12.8 %all-gather.7.cloned.1.call-done = bf16[32,448,288]{1,2,0:T(8,128)(2,1)} async-done(((bf16[1,448,288]{1,2,0:T(8,128)(2,1)}), bf16[32,448,288]{1,2,0:T(8,128)(2,1)}) %all-gather.7.cloned.1.call-update) | async-done | bytes 8257552 | tf_op jit(solution)/shard_map/all_gather | solution.py:149
  68.0 6.8 %fusion.9 = bf16[256,4,288]{0,2,1:T(8,128)(2,1)S(1)} fusion(bf16[256,8,448,1]{0,2,3,1:T(8,128)(2,1)} %bitcast.59, bf16[8,4,448,288]{2,3,1,0:T(8,128)(2,1)} %bitcast.137, f32[4,288]{1,0:T(4,128)S(1)} %bitcast.129), kind=kOutput, calls=%fused_computation.19 | convolution fusion | flops 2114519040 | bytes 10686976 | tf_op jit(solution)/shard_map/tie,iyec->tyc/dot_general | solution.py:155
  74.8 28.8 %collective-permute-start.6 = (bf16[256,288]{0,1:T(8,128)(2,1)S(1)}, bf16[256,288]{0,1:T(8,128)(2,1)S(1)}, u32[]{:S(2)}, u32[]{:S(2)}) collective-permute-start(bf16[256,288]{0,1:T(8,128)(2,1)S(1)} %slice_bitcast_fusion.3), channel_id=1, source_target_pairs={{0,1},{1,2},{2,3},{3,0},{4,5},{5,6},{6,7},{7,4},{8,9},{9,10},{10,1... | collective-permute-start | bytes 442376 | tf_op jit(solution)/shard_map/ppermute | solution.py:168
  103.6 4.0 %fusion.8 = bf16[256,4,288]{0,2,1:T(8,128)(2,1)S(1)} fusion(bf16[256,8,448,1]{0,2,3,1:T(8,128)(2,1)} %bitcast.61, bf16[8,4,448,288]{2,3,1,0:T(8,128)(2,1)S(1)} %bitcast.138, f32[4,288]{1,0:T(4,128)S(1)} %bitcast.130), kind=kOutput, calls=%fused_computation.18 | convolution fusion | flops 2114519040 | bytes 10686976 | tf_op jit(solution)/shard_map/tie,iyec->tyc/dot_general | solution.py:155
  107.9 4.0 %fusion.10 = bf16[256,4,288]{0,2,1:T(8,128)(2,1)S(1)} fusion(bf16[256,8,448,1]{0,2,3,1:T(8,128)(2,1)} %bitcast.57, bf16[8,4,448,288]{2,3,1,0:T(8,128)(2,1)S(1)} %bitcast.139, f32[4,288]{1,0:T(4,128)S(1)} %bitcast.131), kind=kOutput, calls=%fused_computation.20 | convolution fusion | flops 2114519040 | bytes 10686976 | tf_op jit(solution)/shard_map/tie,iyec->tyc/dot_general | solution.py:155
  112.0 4.0 %fusion.7 = bf16[256,4,288]{0,2,1:T(8,128)(2,1)S(1)} fusion(bf16[256,8,448,1]{0,2,3,1:T(8,128)(2,1)} %bitcast.63, bf16[8,4,448,288]{2,3,1,0:T(8,128)(2,1)S(1)} %bitcast.140, f32[4,288]{1,0:T(4,128)S(1)} %bitcast.132), kind=kOutput, calls=%fused_computation.17 | convolution fusion | flops 2114519040 | bytes 10686976 | tf_op jit(solution)/shard_map/tie,iyec->tyc/dot_general | solution.py:155
  116.0 1.4 collective-permute-start.8
  117.5 2.6 %collective-permute-done.8 = bf16[256,288]{0,1:T(8,128)(2,1)S(1)} collective-permute-done((bf16[256,288]{0,1:T(8,128)(2,1)S(1)}, bf16[256,288]{0,1:T(8,128)(2,1)S(1)}, u32[]{:S(2)}, u32[]{:S(2)}) %collective-permute-start.8) | collective-permute-done | bytes 147488 | tf_op jit(solution)/shard_map/ppermute | solution.py:168
  120.8 1.2 subtract_convert_fusion.1
  122.1 0.4 pad_maximum_fusion.3
  122.5 0.9 pad_maximum_fusion.2
  123.4 1.8 slice.61
  125.2 2.4 collective-permute-start.1
  127.6 0.7 fusion.12
  130.9 0.7 pad_add_fusion.meta
  131.6 0.7 collective-permute-start.3
  132.2 2.1 collective-permute-start.5
  134.6 14.7 %collective-permute-done.3 = bf16[256,3,288]{0,2,1:T(8,128)(2,1)S(1)} collective-permute-done((bf16[256,3,288]{0,2,1:T(8,128)(2,1)S(1)}, bf16[256,3,288]{0,2,1:T(8,128)(2,1)S(1)}, u32[]{:S(2)}, u32[]{:S(2)}) %collective-permute-start.3) | collective-permute-done | bytes 442400 | tf_op jit(solution)/shard_map/ppermute | solution.py:168
  149.3 11.3 %collective-permute-done.5 = bf16[256,3,288]{0,2,1:T(8,128)(2,1)S(1)} collective-permute-done((bf16[256,3,288]{0,2,1:T(8,128)(2,1)S(1)}, bf16[256,3,288]{0,2,1:T(8,128)(2,1)S(1)}, u32[]{:S(2)}, u32[]{:S(2)}) %collective-permute-start.5) | collective-permute-done | bytes 442400 | tf_op jit(solution)/shard_map/ppermute | solution.py:168
  160.8 0.4 convert.18
  161.3 0.6 subtract_convert_fusion
  161.9 1.4 pad_maximum_fusion.1
  163.3 45.0 %all-gather.5.cloned.1.call-done.k_ref.v_ref = bf16[4096,1024]{1,0:T(8,128)(2,1)} async-done(((bf16[256,1024]{1,0:T(8,128)(2,1)}), bf16[4096,1024]{1,0:T(8,128)(2,1)}) %all-gather.5.cloned.1.call-update) | async-done | bytes 8388624 | tf_op jit(solution)/shard_map/all_gather | solution.py:198
  208.4 32.0 %shard_map.68 = bf16[256,3584]{1,0:T(8,128)(2,1)} custom-call(s32[8]{0:T(128)} %pad_add_fusion.meta, bf16[3584,256]{1,0:T(8,128)(2,1)} %bitcast.120, bf16[4096,1024]{1,0:T(8,128)(2,1)} %all-gather.5.cloned.1.call-done.k_ref.v_ref, bf16[4096,1024]{1,0:T(8,128)(2,1)} %all-gather.5.cloned.1.call-done.k_ref.v_ref), custom_call_target="tpu_custom_call" | custom-call | tf_op jit(solution)/shard_map/pallas_call | solution.py:106
  (59 shorter events, 2.9 us)
Async XLA Ops:
  7.2 60.8 %all-gather.7.cloned.1.call-start = ((), (), s32[]{:S(2)}) async-start(), calls=%async_computation.1 | async-start | bytes 9732096 | tf_op jit(solution)/shard_map/all_gather | solution.py:149
  7.9 200.5 %all-gather.5.cloned.1.call-start = ((), (), s32[]{:S(2)}) async-start(), calls=%async_computation | async-start | bytes 8912896 | tf_op jit(solution)/shard_map/all_gather | solution.py:198
  10.8 0.7 copy-start.4
  11.6 5.2 %copy-start.5 = (s32[1,4]{1,0:T(1,128)S(1)}, s32[1,4]{1,0:T(1,128)}, u32[]{:S(2)}) copy-start(s32[1,4]{1,0:T(1,128)} %param.6) | copy-start | bytes 52
  11.6 5.4 %copy-start.3 = (f32[4608]{0:T(1024)S(1)}, f32[4608]{0:T(1024)}, u32[]{:S(2)}) copy-start(f32[4608]{0:T(1024)} %param.9) | copy-start | bytes 55300
  14.0 41.2 %collective-permute-start = (bf16[256,3584]{0,1:T(8,128)(2,1)}, bf16[256,3584]{0,1:T(8,128)(2,1)}, u32[]{:S(2)}, u32[]{:S(2)}) collective-permute-start(bf16[256,3584]{0,1:T(8,128)(2,1)} %fusion.2), channel_id=1, source_target_pairs={{0,3},{1,0},{2,1},{3,2},{4,7},{5,4},{6,5},{7,6},{8,11},{9,8},{10,9... | collective-permute-start | bytes 5505032 | tf_op jit(solution)/shard_map/ppermute | solution.py:148
  14.3 89.3 %collective-permute-start.2 = (bf16[256,3584]{0,1:T(8,128)(2,1)}, bf16[256,3584]{0,1:T(8,128)(2,1)}, u32[]{:S(2)}, u32[]{:S(2)}) collective-permute-start(bf16[256,3584]{0,1:T(8,128)(2,1)} %fusion.2), channel_id=1, source_target_pairs={{0,2},{1,3},{2,0},{3,1},{4,6},{5,7},{6,4},{7,5},{8,10},{9,11},{10,... | collective-permute-start | bytes 5505032 | tf_op jit(solution)/shard_map/ppermute | solution.py:148
  16.7 95.2 %collective-permute-start.4 = (bf16[256,3584]{0,1:T(8,128)(2,1)}, bf16[256,3584]{0,1:T(8,128)(2,1)}, u32[]{:S(2)}, u32[]{:S(2)}) collective-permute-start(bf16[256,3584]{0,1:T(8,128)(2,1)} %fusion.2), channel_id=1, source_target_pairs={{0,1},{1,2},{2,3},{3,0},{4,5},{5,6},{6,7},{7,4},{8,9},{9,10},{10,1... | collective-permute-start | bytes 5505032 | tf_op jit(solution)/shard_map/ppermute | solution.py:148
  68.0 35.6 %copy-start.6 = (bf16[32,448,288]{1,2,0:T(8,128)(2,1)S(1)}, bf16[32,448,288]{1,2,0:T(8,128)(2,1)}, u32[]{:S(2)}) copy-start(bf16[32,448,288]{1,2,0:T(8,128)(2,1)} %all-gather.7.cloned.1.call-done) | copy-start | bytes 24772612
  74.8 32.8 %copy-start.2 = (bf16[256,4,288]{0,2,1:T(8,128)(2,1)}, bf16[256,4,288]{0,2,1:T(8,128)(2,1)S(1)}, u32[]{:S(2)}) copy-start(bf16[256,4,288]{0,2,1:T(8,128)(2,1)S(1)} %fusion.9) | copy-start | bytes 1769476
  74.8 42.6 %collective-permute-start.6 = (bf16[256,288]{0,1:T(8,128)(2,1)S(1)}, bf16[256,288]{0,1:T(8,128)(2,1)S(1)}, u32[]{:S(2)}, u32[]{:S(2)}) collective-permute-start(bf16[256,288]{0,1:T(8,128)(2,1)S(1)} %slice_bitcast_fusion.3), channel_id=1, source_target_pairs={{0,1},{1,2},{2,3},{3,0},{4,5},{5,6},{6,7},{7,4},{8,9},{9,10},{10,1... | collective-permute-start | bytes 442376 | tf_op jit(solution)/shard_map/ppermute | solution.py:168
  107.7 9.8 %collective-permute-start.7 = (bf16[256,288]{0,1:T(8,128)(2,1)S(1)}, bf16[256,288]{0,1:T(8,128)(2,1)S(1)}, u32[]{:S(2)}, u32[]{:S(2)}) collective-permute-start(bf16[256,288]{0,1:T(8,128)(2,1)S(1)} %slice_bitcast_fusion.2), channel_id=1, source_target_pairs={{0,2},{1,3},{2,0},{3,1},{4,6},{5,7},{6,4},{7,5},{8,10},{9,11},{10,... | collective-permute-start | bytes 442376 | tf_op jit(solution)/shard_map/ppermute | solution.py:168
  116.0 4.2 %copy-start = (bf16[256,4,288]{0,2,1:T(8,128)(2,1)}, bf16[256,4,288]{0,2,1:T(8,128)(2,1)S(1)}, u32[]{:S(2)}) copy-start(bf16[256,4,288]{0,2,1:T(8,128)(2,1)S(1)} %fusion.7) | copy-start | bytes 1769476
  116.0 4.1 %collective-permute-start.8 = (bf16[256,288]{0,1:T(8,128)(2,1)S(1)}, bf16[256,288]{0,1:T(8,128)(2,1)S(1)}, u32[]{:S(2)}, u32[]{:S(2)}) collective-permute-start(bf16[256,288]{0,1:T(8,128)(2,1)S(1)} %slice_bitcast_fusion.1), channel_id=1, source_target_pairs={{0,3},{1,0},{2,1},{3,2},{4,7},{5,4},{6,5},{7,6},{8,11},{9,8},{10,9... | collective-permute-start | bytes 442376 | tf_op jit(solution)/shard_map/ppermute | solution.py:168
  122.4 9.1 %copy-start.1 = (bf16[256,4,288]{0,2,1:T(8,128)(2,1)S(1)}, bf16[256,4,288]{0,2,1:T(8,128)(2,1)}, u32[]{:S(2)}) copy-start(bf16[256,4,288]{0,2,1:T(8,128)(2,1)} %copy-done) | copy-start | bytes 1769476
  125.2 9.3 %collective-permute-start.1 = (bf16[256,3,288]{0,2,1:T(8,128)(2,1)}, bf16[256,3,288]{0,2,1:T(8,128)(2,1)S(1)}, u32[]{:S(2)}, u32[]{:S(2)}) collective-permute-start(bf16[256,3,288]{0,2,1:T(8,128)(2,1)} %slice.61), channel_id=1, source_target_pairs={{0,1},{1,2},{2,3},{3,0},{4,5},{5,6},{6,7},{7,4},{8,9},{9,10},{10,1... | collective-permute-start | bytes 1327112 | tf_op jit(solution)/shard_map/ppermute | solution.py:168
  131.6 17.7 %collective-permute-start.3 = (bf16[256,3,288]{0,2,1:T(8,128)(2,1)S(1)}, bf16[256,3,288]{0,2,1:T(8,128)(2,1)S(1)}, u32[]{:S(2)}, u32[]{:S(2)}) collective-permute-start(bf16[256,3,288]{0,2,1:T(8,128)(2,1)S(1)} %slice.62), channel_id=1, source_target_pairs={{0,2},{1,3},{2,0},{3,1},{4,6},{5,7},{6,4},{7,5},{8,10},{9,11},{10,... | collective-permute-start | bytes 1327112 | tf_op jit(solution)/shard_map/ppermute | solution.py:168
  132.2 28.4 %collective-permute-start.5 = (bf16[256,3,288]{0,2,1:T(8,128)(2,1)S(1)}, bf16[256,3,288]{0,2,1:T(8,128)(2,1)S(1)}, u32[]{:S(2)}, u32[]{:S(2)}) collective-permute-start(bf16[256,3,288]{0,2,1:T(8,128)(2,1)S(1)} %slice.63), channel_id=1, source_target_pairs={{0,3},{1,0},{2,1},{3,2},{4,7},{5,4},{6,5},{7,6},{8,11},{9,8},{10,9... | collective-permute-start | bytes 1327112 | tf_op jit(solution)/shard_map/ppermute | solution.py:168
Sparse Core Ops, SparseCore 0:
  10.2 57.7 all-gather.6
  123.5 84.8 all-gather.4

commit v10 on v9

--- a/solution.py
+++ b/solution.py
@@ -150,27 +150,30 @@
     pieces = pieces.reshape(-1, n_y, weight.shape[0], width)
     bias_block = bias.reshape(n_y, n_x, width)
     bias_block = lax.dynamic_index_in_dim(bias_block, here, 1, keepdims=False)
-    outs = []
-    for piece in shifted:
-        summed = jnp.einsum(
-            "tie,iyec->tyc",
-            piece.reshape(rows, pieces.shape[0], weight.shape[0]),
-            pieces,
-            preferred_element_type=jnp.float32,
-        )
-        outs.append((summed + bias_block[None]).astype(jnp.bfloat16))
-
-    def exchange(take):
-        full = jnp.zeros((rows, n_x) + take(outs[0]).shape[1:], outs[0].dtype)
-        full = lax.dynamic_update_slice_in_dim(full, take(outs[0])[:, None], here, 1)
+    def project(part, part_bias):
+        outs = []
+        for piece in shifted:
+            summed = jnp.einsum(
+                "tie,iyec->tyc",
+                piece.reshape(rows, pieces.shape[0], weight.shape[0]),
+                part,
+                preferred_element_type=jnp.float32,
+            )
+            outs.append((summed + part_bias[None]).astype(jnp.bfloat16))
+        return outs
+
+    def exchange(outs):
+        full = jnp.zeros((rows, n_x) + outs[0].shape[1:], outs[0].dtype)
+        full = lax.dynamic_update_slice_in_dim(full, outs[0][:, None], here, 1)
         for step in range(1, n_x):
             pairs = [(s, (s + step) % n_x) for s in range(n_x)]
-            got = lax.ppermute(take(outs[(n_x - step) % n_x]), "x", pairs)
+            got = lax.ppermute(outs[(n_x - step) % n_x], "x", pairs)
             full = lax.dynamic_update_slice_in_dim(full, got[:, None], (here - step) % n_x, 1)
         return full
 
-    tail = exchange(lambda out: out[:, n_y - 1]).reshape(rows, -1)
-    head = exchange(lambda out: out[:, : n_y - 1])
+    tail = exchange(project(pieces[:, n_y - 1 :], bias_block[n_y - 1 :]))
+    tail = tail.reshape(rows, -1)
+    head = exchange(project(pieces[:, : n_y - 1], bias_block[: n_y - 1]))
     head = jnp.transpose(head, (0, 2, 1, 3))
     return head.reshape(rows, -1), tail
 

time: 248 us -> 232 us (0.935)
  the two profiles are of different devices: /device:TPU:29 before, /device:TPU:19 now
where the time goes in v10:
time: 232 us
  waiting for transfers between devices  128 us (55%)
  Pallas kernels  32 us (14%)
  matrix products  26.3 us (11%)
  between operations  17 us (7%)
  starting transfers between devices  14.7 us (6%)
  other arithmetic  8.93 us (4%)
  local copies, waits for them, and re-layouts  5.07 us (2%)
    ppermute x3, waiting for transfers between devices, project_joined(): shifted.append(lax.ppermute(normed, 'x', pairs))  56.3 us
    all_gather x1, waiting for transfers between devices, on_device(): piece = lax.all_gather(kv_rows, ('y', 'x'), axis=0, tiled=True)  37.7 us
    pallas_call x1, Pallas kernels, flash(): pl.pallas_call(flash_body, grid_spec=spec, out_shape=jax.ShapeDtypeStruct...  32 us
    dot_general x8, matrix products, project(): jnp.einsum('tie,iyec->tyc', piece.reshape(rows, pieces.shape[0], weight.s...  26.3 us
    ppermute x6, waiting for transfers between devices, exchange(): got = lax.ppermute(outs[(n_x - step) % n_x], 'x', pairs)  20.2 us
    all_gather x1, waiting for transfers between devices, project_joined(): pieces = lax.all_gather(weight, ('z', 'c', 'y'), axis=0, tiled=False)  12.9 us
    ppermute x6, starting transfers between devices, exchange(): got = lax.ppermute(outs[(n_x - step) % n_x], 'x', pairs)  10.7 us
  transfers between devices with their start and end apart: 11, of which 6 were waited for; matrix products, arithmetic and copies ran while one was open for 16% of the time, Pallas kernels for 0%

profile of v10, /device:TPU:19, one launch (start us, length us, event | category | flops | bytes accessed | tf_op | source)
XLA Modules:
  0.0 231.9 jit_solution(2460060474887364671)
XLA Ops:
  7.2 0.7 all-gather.7.cloned.1.call-update
  7.9 2.9 %copy.67 = bf16[256,3584]{0,1:T(8,128)(2,1)S(1)} copy(bf16[256,3584]{1,0:T(8,128)(2,1)} %param.5) | data formatting | bytes 3670016 | tf_op args[0]
  10.9 0.5 fusion.8
  11.6 2.5 %fusion.10 = bf16[256,3584]{0,1:T(8,128)(2,1)} fusion(bf16[256,3584]{0,1:T(8,128)(2,1)S(1)} %copy.67, f32[3584]{0:T(1024)S(1)} %copy-done.1, f32[256]{0:T(256)S(1)} %add_rsqrt_fusion), kind=kLoop, calls=%fused_computation.12 | loop fusion | flops 3670016 | bytes 3685376 | tf_op jit(solution)/shard_map/convert_element_type | solution.py:117
  14.0 1.2 collective-permute-start.4
  15.3 0.8 collective-permute-start.2
  16.1 1.9 collective-permute-start
  18.9 36.3 %collective-permute-done.4 = bf16[256,3584]{0,1:T(8,128)(2,1)} collective-permute-done((bf16[256,3584]{0,1:T(8,128)(2,1)}, bf16[256,3584]{0,1:T(8,128)(2,1)}, u32[]{:S(2)}, u32[]{:S(2)}) %collective-permute-start.4) | collective-permute-done | bytes 1835040 | tf_op jit(solution)/shard_map/ppermute | solution.py:148
  55.3 12.9 %all-gather.7.cloned.1.call-done = bf16[32,448,288]{1,2,0:T(8,128)(2,1)} async-done(((bf16[1,448,288]{1,2,0:T(8,128)(2,1)}), bf16[32,448,288]{1,2,0:T(8,128)(2,1)}) %all-gather.7.cloned.1.call-update) | async-done | bytes 8257552 | tf_op jit(solution)/shard_map/all_gather | solution.py:149
  68.2 3.1 %fusion.73 = bf16[256,1,288]{0,2,1:T(8,128)(2,1)S(1)} fusion(bf16[256,8,448]{0,2,1:T(8,128)(2,1)} %bitcast.24, bf16[8,4,448,288]{2,3,1,0:T(8,128)(2,1)} %bitcast.229, f32[288]{0:T(512)S(1)} %fusion.74), kind=kOutput, calls=%fused_computation.52 | convolution fusion | flops 528629760 | bytes 4342912 | tf_op jit(solution)/shard_map/tie,iyec->tyc/dot_general | solution.py:156
  71.6 3.4 %fusion.72 = bf16[256,1,288]{0,2,1:T(8,128)(2,1)S(1)} fusion(bf16[256,8,448]{0,2,1:T(8,128)(2,1)} %bitcast.18, bf16[8,4,448,288]{2,3,1,0:T(8,128)(2,1)} %bitcast.230, f32[288]{0:T(512)S(1)} %fusion.74), kind=kOutput, calls=%fused_computation.51 | convolution fusion | flops 528629760 | bytes 4342912 | tf_op jit(solution)/shard_map/tie,iyec->tyc/dot_general | solution.py:156
  75.0 1.9 collective-permute-start.7
  76.9 20.0 %collective-permute-done = bf16[256,3584]{0,1:T(8,128)(2,1)S(1)} collective-permute-done((bf16[256,3584]{0,1:T(8,128)(2,1)}, bf16[256,3584]{0,1:T(8,128)(2,1)S(1)}, u32[]{:S(2)}, u32[]{:S(2)}) %collective-permute-start) | collective-permute-done | bytes 1835040 | tf_op jit(solution)/shard_map/ppermute | solution.py:148
  96.9 0.7 fusion.71
  97.6 0.6 copy-done.4
  98.2 4.3 %collective-permute-start.6 = (bf16[256,1,288]{0,2,1:T(8,128)(2,1)S(1)}, bf16[256,1,288]{0,2,1:T(8,128)(2,1)S(1)}, u32[]{:S(2)}, u32[]{:S(2)}) collective-permute-start(bf16[256,1,288]{0,2,1:T(8,128)(2,1)S(1)} %fusion.71), channel_id=1, source_target_pairs={{0,1},{1,2},{2,3},{3,0},{4,5},{5,6},{6,7},{7,4},{8,9},{9,10},{10,1... | collective-permute-start | bytes 442376 | tf_op jit(solution)/shard_map/ppermute | solution.py:170
  102.6 2.2 fusion.70
  104.8 1.7 collective-permute-done.6
  108.0 0.9 pad_maximum_fusion.2
  108.9 0.7 fusion.75
  112.2 0.6 pad_add_fusion.meta
  112.8 5.5 %fusion.39 = bf16[256,3,288]{0,2,1:T(8,128)(2,1)S(1)} fusion(bf16[256,8,448,1]{0,2,3,1:T(8,128)(2,1)} %bitcast.79, bf16[8,4,448,288]{2,3,1,0:T(8,128)(2,1)} %bitcast.231, f32[3,288]{1,0:T(4,128)S(1)} %bitcast.221), kind=kOutput, calls=%fused_computation.30 | convolution fusion | flops 1585889280 | bytes 9358720 | tf_op jit(solution)/shard_map/tie,iyec->tyc/dot_general | solution.py:156
  118.3 2.9 %collective-permute-start.5 = (bf16[256,3,288]{0,2,1:T(8,128)(2,1)S(1)}, bf16[256,3,288]{0,2,1:T(8,128)(2,1)S(1)}, u32[]{:S(2)}, u32[]{:S(2)}) collective-permute-start(bf16[256,3,288]{0,2,1:T(8,128)(2,1)S(1)} %fusion.39), channel_id=1, source_target_pairs={{0,3},{1,0},{2,1},{3,2},{4,7},{5,4},{6,5},{7,6},{8,11},{9,8},{10,9... | collective-permute-start | bytes 1327112 | tf_op jit(solution)/shard_map/ppermute | solution.py:170
  121.3 6.0 %fusion.48 = bf16[256,3,288]{0,2,1:T(8,128)(2,1)S(1)} fusion(bf16[256,8,448,1]{0,2,3,1:T(8,128)(2,1)} %bitcast.77, bf16[8,4,448,288]{2,3,1,0:T(8,128)(2,1)} %bitcast.232, f32[3,288]{1,0:T(4,128)S(1)} %bitcast.222), kind=kOutput, calls=%fused_computation.33 | convolution fusion | flops 1585889280 | bytes 9358720 | tf_op jit(solution)/shard_map/tie,iyec->tyc/dot_general | solution.py:156
  127.8 1.9 fusion.45
  129.7 0.7 collective-permute-start.1
  130.6 3.5 %fusion.54 = bf16[256,4,3,288]{0,3,1,2:T(8,128)(2,1)S(1)} fusion(bf16[256,4,3,288]{0,3,1,2:T(8,128)(2,1)S(1)} %broadcast_in_dim.65, s32[]{:T(128)S(6)} %select_n.53, bf16[256,8,448,1]{0,2,3,1:T(8,128)(2,1)} %bitcast.73, bf16[8,4,448,288]{2,3,1,0:T(8,128)(2,1)S(1)} %bitcast.238, f32[3,288]{1,0:T(4,128)S(1)} %bitcast.224), kind=kOutput, calls=%fused_computation.35 | convolution fusion | flops 1585889280 | bytes 9361412 | tf_op jit(solution)/shard_map/tie,iyec->tyc/dot_general | solution.py:156
  134.1 18.4 %collective-permute-done.1 = bf16[256,3,288]{0,2,1:T(8,128)(2,1)S(1)} collective-permute-done((bf16[256,3,288]{0,2,1:T(8,128)(2,1)S(1)}, bf16[256,3,288]{0,2,1:T(8,128)(2,1)S(1)}, u32[]{:S(2)}, u32[]{:S(2)}) %collective-permute-start.1) | collective-permute-done | bytes 442400 | tf_op jit(solution)/shard_map/ppermute | solution.py:170
  153.3 0.6 subtract_convert_fusion
  153.9 1.4 pad_maximum_fusion.1
  155.3 37.7 %all-gather.5.cloned.1.call-done.k_ref.v_ref = bf16[4096,1024]{1,0:T(8,128)(2,1)} async-done(((bf16[256,1024]{1,0:T(8,128)(2,1)}), bf16[4096,1024]{1,0:T(8,128)(2,1)}) %all-gather.5.cloned.1.call-update) | async-done | bytes 8388624 | tf_op jit(solution)/shard_map/all_gather | solution.py:201
  193.0 32.0 %shard_map.68 = bf16[256,3584]{1,0:T(8,128)(2,1)} custom-call(s32[8]{0:T(128)} %pad_add_fusion.meta, bf16[3584,256]{1,0:T(8,128)(2,1)} %bitcast.212, bf16[4096,1024]{1,0:T(8,128)(2,1)} %all-gather.5.cloned.1.call-done.k_ref.v_ref, bf16[4096,1024]{1,0:T(8,128)(2,1)} %all-gather.5.cloned.1.call-done.k_ref.v_ref), custom_call_target="tpu_custom_call" | custom-call | tf_op jit(solution)/shard_map/pallas_call | solution.py:106
  (61 shorter events, 4.4 us)
Async XLA Ops:
  7.2 61.0 %all-gather.7.cloned.1.call-start = ((), (), s32[]{:S(2)}) async-start(), calls=%async_computation.1 | async-start | bytes 9732096 | tf_op jit(solution)/shard_map/all_gather | solution.py:149
  7.9 185.1 %all-gather.5.cloned.1.call-start = ((), (), s32[]{:S(2)}) async-start(), calls=%async_computation | async-start | bytes 8912896 | tf_op jit(solution)/shard_map/all_gather | solution.py:201
  10.8 0.7 copy-start.1
  11.6 6.4 %copy-start.2 = (s32[1,4]{1,0:T(1,128)S(1)}, s32[1,4]{1,0:T(1,128)}, u32[]{:S(2)}) copy-start(s32[1,4]{1,0:T(1,128)} %param.6) | copy-start | bytes 52
  11.6 6.6 %copy-start = (f32[4608]{0:T(1024)S(1)}, f32[4608]{0:T(1024)}, u32[]{:S(2)}) copy-start(f32[4608]{0:T(1024)} %param.9) | copy-start | bytes 55300
  14.0 41.2 %collective-permute-start.4 = (bf16[256,3584]{0,1:T(8,128)(2,1)}, bf16[256,3584]{0,1:T(8,128)(2,1)}, u32[]{:S(2)}, u32[]{:S(2)}) collective-permute-start(bf16[256,3584]{0,1:T(8,128)(2,1)} %fusion.10), channel_id=1, source_target_pairs={{0,1},{1,2},{2,3},{3,0},{4,5},{5,6},{6,7},{7,4},{8,9},{9,10},{10,1... | collective-permute-start | bytes 5505032 | tf_op jit(solution)/shard_map/ppermute | solution.py:148
  15.3 56.3 %collective-permute-start.2 = (bf16[256,3584]{0,1:T(8,128)(2,1)}, bf16[256,3584]{0,1:T(8,128)(2,1)}, u32[]{:S(2)}, u32[]{:S(2)}) collective-permute-start(bf16[256,3584]{0,1:T(8,128)(2,1)} %fusion.10), channel_id=1, source_target_pairs={{0,2},{1,3},{2,0},{3,1},{4,6},{5,7},{6,4},{7,5},{8,10},{9,11},{10,... | collective-permute-start | bytes 5505032 | tf_op jit(solution)/shard_map/ppermute | solution.py:148
  16.1 80.8 %collective-permute-start = (bf16[256,3584]{0,1:T(8,128)(2,1)}, bf16[256,3584]{0,1:T(8,128)(2,1)S(1)}, u32[]{:S(2)}, u32[]{:S(2)}) collective-permute-start(bf16[256,3584]{0,1:T(8,128)(2,1)} %fusion.10), channel_id=1, source_target_pairs={{0,3},{1,0},{2,1},{3,2},{4,7},{5,4},{6,5},{7,6},{8,11},{9,8},{10,9... | collective-permute-start | bytes 5505032 | tf_op jit(solution)/shard_map/ppermute | solution.py:148
  68.2 28.7 %copy-start.3 = (bf16[32,448,288]{1,2,0:T(8,128)(2,1)S(1)}, bf16[32,448,288]{1,2,0:T(8,128)(2,1)}, u32[]{:S(2)}) copy-start(bf16[32,448,288]{1,2,0:T(8,128)(2,1)} %all-gather.7.cloned.1.call-done) | copy-start | bytes 24772612
  71.3 35.3 %collective-permute-start.8 = (bf16[256,1,288]{0,2,1:T(8,128)(2,1)S(1)}, bf16[256,1,288]{0,2,1:T(8,128)(2,1)S(1)}, u32[]{:S(2)}, u32[]{:S(2)}) collective-permute-start(bf16[256,1,288]{0,2,1:T(8,128)(2,1)S(1)} %fusion.73), channel_id=1, source_target_pairs={{0,3},{1,0},{2,1},{3,2},{4,7},{5,4},{6,5},{7,6},{8,11},{9,8},{10,9... | collective-permute-start | bytes 442376 | tf_op jit(solution)/shard_map/ppermute | solution.py:170
  75.0 31.5 %collective-permute-start.7 = (bf16[256,1,288]{0,2,1:T(8,128)(2,1)S(1)}, bf16[256,1,288]{0,2,1:T(8,128)(2,1)S(1)}, u32[]{:S(2)}, u32[]{:S(2)}) collective-permute-start(bf16[256,1,288]{0,2,1:T(8,128)(2,1)S(1)} %fusion.72), channel_id=1, source_target_pairs={{0,2},{1,3},{2,0},{3,1},{4,6},{5,7},{6,4},{7,5},{8,10},{9,11},{10,... | collective-permute-start | bytes 442376 | tf_op jit(solution)/shard_map/ppermute | solution.py:170
  96.9 1.3 copy-start.4
  98.2 8.3 %collective-permute-start.6 = (bf16[256,1,288]{0,2,1:T(8,128)(2,1)S(1)}, bf16[256,1,288]{0,2,1:T(8,128)(2,1)S(1)}, u32[]{:S(2)}, u32[]{:S(2)}) collective-permute-start(bf16[256,1,288]{0,2,1:T(8,128)(2,1)S(1)} %fusion.71), channel_id=1, source_target_pairs={{0,1},{1,2},{2,3},{3,0},{4,5},{5,6},{6,7},{7,4},{8,9},{9,10},{10,1... | collective-permute-start | bytes 442376 | tf_op jit(solution)/shard_map/ppermute | solution.py:170
  112.8 15.0 %slice-start = ((s8[9437184]{0:T(1024)(128)(4,1)}), s8[4194304]{0:T(1024)(128)(4,1)S(1)}, s32[]{:S(2)}) async-start(s8[9437184]{0:T(1024)(128)(4,1)} %bitcast.235), calls=%async_computation.2 | async-start | bytes 8388608
  112.8 15.0 %slice-start.1 = ((s8[9437184]{0:T(1024)(128)(4,1)}), s8[4194304]{0:T(1024)(128)(4,1)S(1)}, s32[]{:S(2)}) async-start(s8[9437184]{0:T(1024)(128)(4,1)} %bitcast.235), calls=%async_computation.3 | async-start | bytes 8388608
  118.3 34.3 %collective-permute-start.5 = (bf16[256,3,288]{0,2,1:T(8,128)(2,1)S(1)}, bf16[256,3,288]{0,2,1:T(8,128)(2,1)S(1)}, u32[]{:S(2)}, u32[]{:S(2)}) collective-permute-start(bf16[256,3,288]{0,2,1:T(8,128)(2,1)S(1)} %fusion.39), channel_id=1, source_target_pairs={{0,3},{1,0},{2,1},{3,2},{4,7},{5,4},{6,5},{7,6},{8,11},{9,8},{10,9... | collective-permute-start | bytes 1327112 | tf_op jit(solution)/shard_map/ppermute | solution.py:170
  121.3 6.6 %slice-start.2 = ((s8[9437184]{0:T(1024)(128)(4,1)}), s8[1048576]{0:T(1024)(128)(4,1)S(1)}, s32[]{:S(2)}) async-start(s8[9437184]{0:T(1024)(128)(4,1)} %bitcast.235), calls=%async_computation.4 | async-start | bytes 2097152
  121.3 6.6 %copy-start.5 = (bf16[256,3584]{0,1:T(8,128)(2,1)S(1)}, bf16[256,3584]{0,1:T(8,128)(2,1)}, u32[]{:S(2)}) copy-start(bf16[256,3584]{0,1:T(8,128)(2,1)} %copy-done.4) | copy-start | bytes 5505028
  127.3 25.3 %collective-permute-start.3 = (bf16[256,3,288]{0,2,1:T(8,128)(2,1)S(1)}, bf16[256,3,288]{0,2,1:T(8,128)(2,1)S(1)}, u32[]{:S(2)}, u32[]{:S(2)}) collective-permute-start(bf16[256,3,288]{0,2,1:T(8,128)(2,1)S(1)} %fusion.48), channel_id=1, source_target_pairs={{0,2},{1,3},{2,0},{3,1},{4,6},{5,7},{6,4},{7,5},{8,10},{9,11},{10,... | collective-permute-start | bytes 1327112 | tf_op jit(solution)/shard_map/ppermute | solution.py:170
  129.7 22.8 %collective-permute-start.1 = (bf16[256,3,288]{0,2,1:T(8,128)(2,1)S(1)}, bf16[256,3,288]{0,2,1:T(8,128)(2,1)S(1)}, u32[]{:S(2)}, u32[]{:S(2)}) collective-permute-start(bf16[256,3,288]{0,2,1:T(8,128)(2,1)S(1)} %fusion.45), channel_id=1, source_target_pairs={{0,1},{1,2},{2,3},{3,0},{4,5},{5,6},{6,7},{7,4},{8,9},{9,10},{10,1... | collective-permute-start | bytes 1327112 | tf_op jit(solution)/shard_map/ppermute | solution.py:170
Sparse Core Ops, SparseCore 0:
  10.2 57.9 all-gather.6
  109.0 83.9 all-gather.4

commit v11 on v10

--- a/solution.py
+++ b/solution.py
@@ -41,7 +41,7 @@
             qstart = jnp.where(end <= qcol, end, qstart)
         allowed = (krow >= qstart) & (krow <= qcol)
         bias_ref[...] = jnp.where(allowed, 0.0, -1e30).astype(jnp.float32)
-        scale = 1.0 / HEAD_DIM**0.5
+        scale = math.log2(math.e) / HEAD_DIM**0.5
         for g in range(KV_HEADS):
             dims = slice(g * HEAD_DIM, (g + 1) * HEAD_DIM)
             keys = k_ref[:, dims]
@@ -53,13 +53,12 @@
                     cols = slice(c * LANES, (c + 1) * LANES)
                     q = q_ref[heads, cols]
                     scores = (
-                        jnp.dot(keys, q, preferred_element_type=jnp.float32) * scale
-                        + bias_ref[:, cols]
+                        jnp.dot(keys, q, preferred_element_type=jnp.float32) + bias_ref[:, cols]
                     )
                     m_prev = m_ref[h, :, cols]
                     m_new = jnp.maximum(m_prev, jnp.max(scores, axis=0, keepdims=True))
-                    shrink = jnp.exp(m_prev - m_new)
-                    weights = jnp.exp(scores - m_new)
+                    shrink = jnp.exp2((m_prev - m_new) * scale)
+                    weights = jnp.exp2((scores - m_new) * scale)
                     l_ref[h, :, cols] = l_ref[h, :, cols] * shrink + jnp.sum(
                         weights, axis=0, keepdims=True
                     )

time: 232 us -> 230 us (level)
  the two profiles are of different devices: /device:TPU:19 before, /device:TPU:47 now
where the time goes in v11:
time: 230 us; the launch traced here: 226 us
  waiting for transfers between devices  130 us (57%)
  Pallas kernels  26.6 us (12%)
  matrix products  25.8 us (11%)
  between operations  17 us (7%)
  starting transfers between devices  12.7 us (6%)
  other arithmetic  8.93 us (4%)
  local copies, waits for them, and re-layouts  5.07 us (2%)
    ppermute x3, waiting for transfers between devices, project_joined(): shifted.append(lax.ppermute(normed, 'x', pairs))  60.6 us
    all_gather x1, waiting for transfers between devices, on_device(): piece = lax.all_gather(kv_rows, ('y', 'x'), axis=0, tiled=True)  38.2 us
    pallas_call x1, Pallas kernels, flash(): pl.pallas_call(flash_body, grid_spec=spec, out_shape=jax.ShapeDtypeStruct...  26.6 us
    dot_general x8, matrix products, project(): jnp.einsum('tie,iyec->tyc', piece.reshape(rows, pieces.shape[0], weight.s...  25.8 us
    ppermute x6, waiting for transfers between devices, exchange(): got = lax.ppermute(outs[(n_x - step) % n_x], 'x', pairs)  19.3 us
    all_gather x1, waiting for transfers between devices, project_joined(): pieces = lax.all_gather(weight, ('z', 'c', 'y'), axis=0, tiled=False)  11.1 us
    ppermute x6, starting transfers between devices, exchange(): got = lax.ppermute(outs[(n_x - step) % n_x], 'x', pairs)  10.3 us
  transfers between devices with their start and end apart: 11, of which 6 were waited for; matrix products, arithmetic and copies ran while one was open for 16% of the time, Pallas kernels for 0%

profile of v11, /device:TPU:47, one launch (start us, length us, event | category | flops | bytes accessed | tf_op | source)
XLA Modules:
  0.0 226.1 jit_solution(10907477741485470000)
XLA Ops:
  7.2 0.7 all-gather.7.cloned.1.call-update
  7.9 2.9 %copy.67 = bf16[256,3584]{0,1:T(8,128)(2,1)S(1)} copy(bf16[256,3584]{1,0:T(8,128)(2,1)} %param.5) | data formatting | bytes 3670016 | tf_op args[0]
  10.9 0.5 fusion.8
  11.6 2.5 %fusion.10 = bf16[256,3584]{0,1:T(8,128)(2,1)} fusion(bf16[256,3584]{0,1:T(8,128)(2,1)S(1)} %copy.67, f32[3584]{0:T(1024)S(1)} %copy-done.1, f32[256]{0:T(256)S(1)} %add_rsqrt_fusion), kind=kLoop, calls=%fused_computation.12 | loop fusion | flops 3670016 | bytes 3685376 | tf_op jit(solution)/shard_map/convert_element_type | solution.py:116
  14.2 2.1 collective-permute-start.2
  17.3 37.9 %collective-permute-done.4 = bf16[256,3584]{0,1:T(8,128)(2,1)} collective-permute-done((bf16[256,3584]{0,1:T(8,128)(2,1)}, bf16[256,3584]{0,1:T(8,128)(2,1)}, u32[]{:S(2)}, u32[]{:S(2)}) %collective-permute-start.4) | collective-permute-done | bytes 1835040 | tf_op jit(solution)/shard_map/ppermute | solution.py:147
  55.3 11.1 %all-gather.7.cloned.1.call-done = bf16[32,448,288]{1,2,0:T(8,128)(2,1)} async-done(((bf16[1,448,288]{1,2,0:T(8,128)(2,1)}), bf16[32,448,288]{1,2,0:T(8,128)(2,1)}) %all-gather.7.cloned.1.call-update) | async-done | bytes 8257552 | tf_op jit(solution)/shard_map/all_gather | solution.py:148
  66.4 3.1 %fusion.73 = bf16[256,1,288]{0,2,1:T(8,128)(2,1)S(1)} fusion(bf16[256,8,448]{0,2,1:T(8,128)(2,1)} %bitcast.24, bf16[8,4,448,288]{2,3,1,0:T(8,128)(2,1)} %bitcast.229, f32[288]{0:T(512)S(1)} %fusion.74), kind=kOutput, calls=%fused_computation.52 | convolution fusion | flops 528629760 | bytes 4342912 | tf_op jit(solution)/shard_map/tie,iyec->tyc/dot_general | solution.py:155
  69.4 0.6 collective-permute-start.8
  70.1 3.1 %fusion.72 = bf16[256,1,288]{0,2,1:T(8,128)(2,1)S(1)} fusion(bf16[256,8,448]{0,2,1:T(8,128)(2,1)} %bitcast.18, bf16[8,4,448,288]{2,3,1,0:T(8,128)(2,1)} %bitcast.230, f32[288]{0:T(512)S(1)} %fusion.74), kind=kOutput, calls=%fused_computation.51 | convolution fusion | flops 528629760 | bytes 4342912 | tf_op jit(solution)/shard_map/tie,iyec->tyc/dot_general | solution.py:155
  73.2 1.2 collective-permute-start.7
  74.5 22.7 %collective-permute-done = bf16[256,3584]{0,1:T(8,128)(2,1)S(1)} collective-permute-done((bf16[256,3584]{0,1:T(8,128)(2,1)}, bf16[256,3584]{0,1:T(8,128)(2,1)S(1)}, u32[]{:S(2)}, u32[]{:S(2)}) %collective-permute-start) | collective-permute-done | bytes 1835040 | tf_op jit(solution)/shard_map/ppermute | solution.py:147
  97.2 0.7 fusion.71
  97.9 0.6 copy-done.4
  98.5 3.3 %collective-permute-start.6 = (bf16[256,1,288]{0,2,1:T(8,128)(2,1)S(1)}, bf16[256,1,288]{0,2,1:T(8,128)(2,1)S(1)}, u32[]{:S(2)}, u32[]{:S(2)}) collective-permute-start(bf16[256,1,288]{0,2,1:T(8,128)(2,1)S(1)} %fusion.71), channel_id=1, source_target_pairs={{0,1},{1,2},{2,3},{3,0},{4,5},{5,6},{6,7},{7,4},{8,9},{9,10},{10,1... | collective-permute-start | bytes 442376 | tf_op jit(solution)/shard_map/ppermute | solution.py:169
  101.8 2.2 fusion.70
  104.1 1.8 collective-permute-done.6
  107.3 0.9 pad_maximum_fusion.2
  108.2 0.7 fusion.75
  111.5 0.6 pad_add_fusion.meta
  112.1 5.5 %fusion.39 = bf16[256,3,288]{0,2,1:T(8,128)(2,1)S(1)} fusion(bf16[256,8,448,1]{0,2,3,1:T(8,128)(2,1)} %bitcast.79, bf16[8,4,448,288]{2,3,1,0:T(8,128)(2,1)} %bitcast.231, f32[3,288]{1,0:T(4,128)S(1)} %bitcast.221), kind=kOutput, calls=%fused_computation.30 | convolution fusion | flops 1585889280 | bytes 9358720 | tf_op jit(solution)/shard_map/tie,iyec->tyc/dot_general | solution.py:155
  117.6 2.5 %collective-permute-start.5 = (bf16[256,3,288]{0,2,1:T(8,128)(2,1)S(1)}, bf16[256,3,288]{0,2,1:T(8,128)(2,1)S(1)}, u32[]{:S(2)}, u32[]{:S(2)}) collective-permute-start(bf16[256,3,288]{0,2,1:T(8,128)(2,1)S(1)} %fusion.39), channel_id=1, source_target_pairs={{0,3},{1,0},{2,1},{3,2},{4,7},{5,4},{6,5},{7,6},{8,11},{9,8},{10,9... | collective-permute-start | bytes 1327112 | tf_op jit(solution)/shard_map/ppermute | solution.py:169
  120.1 5.9 %fusion.48 = bf16[256,3,288]{0,2,1:T(8,128)(2,1)S(1)} fusion(bf16[256,8,448,1]{0,2,3,1:T(8,128)(2,1)} %bitcast.77, bf16[8,4,448,288]{2,3,1,0:T(8,128)(2,1)} %bitcast.232, f32[3,288]{1,0:T(4,128)S(1)} %bitcast.222), kind=kOutput, calls=%fused_computation.33 | convolution fusion | flops 1585889280 | bytes 9358720 | tf_op jit(solution)/shard_map/tie,iyec->tyc/dot_general | solution.py:155
  126.0 2.6 %collective-permute-start.3 = (bf16[256,3,288]{0,2,1:T(8,128)(2,1)S(1)}, bf16[256,3,288]{0,2,1:T(8,128)(2,1)S(1)}, u32[]{:S(2)}, u32[]{:S(2)}) collective-permute-start(bf16[256,3,288]{0,2,1:T(8,128)(2,1)S(1)} %fusion.48), channel_id=1, source_target_pairs={{0,2},{1,3},{2,0},{3,1},{4,6},{5,7},{6,4},{7,5},{8,10},{9,11},{10,... | collective-permute-start | bytes 1327112 | tf_op jit(solution)/shard_map/ppermute | solution.py:169
  128.5 1.9 fusion.45
  130.7 3.5 %fusion.54 = bf16[256,4,3,288]{0,3,1,2:T(8,128)(2,1)S(1)} fusion(bf16[256,4,3,288]{0,3,1,2:T(8,128)(2,1)S(1)} %broadcast_in_dim.65, s32[]{:T(128)S(6)} %select_n.53, bf16[256,8,448,1]{0,2,3,1:T(8,128)(2,1)} %bitcast.73, bf16[8,4,448,288]{2,3,1,0:T(8,128)(2,1)S(1)} %bitcast.238, f32[3,288]{1,0:T(4,128)S(1)} %bitcast.224), kind=kOutput, calls=%fused_computation.35 | convolution fusion | flops 1585889280 | bytes 9361412 | tf_op jit(solution)/shard_map/tie,iyec->tyc/dot_general | solution.py:155
  134.2 17.5 %collective-permute-done.1 = bf16[256,3,288]{0,2,1:T(8,128)(2,1)S(1)} collective-permute-done((bf16[256,3,288]{0,2,1:T(8,128)(2,1)S(1)}, bf16[256,3,288]{0,2,1:T(8,128)(2,1)S(1)}, u32[]{:S(2)}, u32[]{:S(2)}) %collective-permute-start.1) | collective-permute-done | bytes 442400 | tf_op jit(solution)/shard_map/ppermute | solution.py:169
  152.0 0.4 convert.18
  152.4 0.6 subtract_convert_fusion
  153.1 1.4 pad_maximum_fusion.1
  154.5 38.2 %all-gather.5.cloned.1.call-done.k_ref.v_ref = bf16[4096,1024]{1,0:T(8,128)(2,1)} async-done(((bf16[256,1024]{1,0:T(8,128)(2,1)}), bf16[4096,1024]{1,0:T(8,128)(2,1)}) %all-gather.5.cloned.1.call-update) | async-done | bytes 8388624 | tf_op jit(solution)/shard_map/all_gather | solution.py:200
  192.7 26.6 %shard_map.68 = bf16[256,3584]{1,0:T(8,128)(2,1)} custom-call(s32[8]{0:T(128)} %pad_add_fusion.meta, bf16[3584,256]{1,0:T(8,128)(2,1)} %bitcast.212, bf16[4096,1024]{1,0:T(8,128)(2,1)} %all-gather.5.cloned.1.call-done.k_ref.v_ref, bf16[4096,1024]{1,0:T(8,128)(2,1)} %all-gather.5.cloned.1.call-done.k_ref.v_ref), custom_call_target="tpu_custom_call" | custom-call | tf_op jit(solution)/shard_map/pallas_call | solution.py:105
  (61 shorter events, 3.3 us)
Async XLA Ops:
  7.2 59.2 %all-gather.7.cloned.1.call-start = ((), (), s32[]{:S(2)}) async-start(), calls=%async_computation.1 | async-start | bytes 9732096 | tf_op jit(solution)/shard_map/all_gather | solution.py:148
  7.9 184.8 %all-gather.5.cloned.1.call-start = ((), (), s32[]{:S(2)}) async-start(), calls=%async_computation | async-start | bytes 8912896 | tf_op jit(solution)/shard_map/all_gather | solution.py:200
  10.8 0.7 copy-start.1
  11.6 4.8 %copy-start.2 = (s32[1,4]{1,0:T(1,128)S(1)}, s32[1,4]{1,0:T(1,128)}, u32[]{:S(2)}) copy-start(s32[1,4]{1,0:T(1,128)} %param.6) | copy-start | bytes 52
  11.6 5.0 %copy-start = (f32[4608]{0:T(1024)S(1)}, f32[4608]{0:T(1024)}, u32[]{:S(2)}) copy-start(f32[4608]{0:T(1024)} %param.9) | copy-start | bytes 55300
  14.0 41.2 %collective-permute-start.4 = (bf16[256,3584]{0,1:T(8,128)(2,1)}, bf16[256,3584]{0,1:T(8,128)(2,1)}, u32[]{:S(2)}, u32[]{:S(2)}) collective-permute-start(bf16[256,3584]{0,1:T(8,128)(2,1)} %fusion.10), channel_id=1, source_target_pairs={{0,1},{1,2},{2,3},{3,0},{4,5},{5,6},{6,7},{7,4},{8,9},{9,10},{10,1... | collective-permute-start | bytes 5505032 | tf_op jit(solution)/shard_map/ppermute | solution.py:147
  14.2 55.8 %collective-permute-start.2 = (bf16[256,3584]{0,1:T(8,128)(2,1)}, bf16[256,3584]{0,1:T(8,128)(2,1)}, u32[]{:S(2)}, u32[]{:S(2)}) collective-permute-start(bf16[256,3584]{0,1:T(8,128)(2,1)} %fusion.10), channel_id=1, source_target_pairs={{0,2},{1,3},{2,0},{3,1},{4,6},{5,7},{6,4},{7,5},{8,10},{9,11},{10,... | collective-permute-start | bytes 5505032 | tf_op jit(solution)/shard_map/ppermute | solution.py:147
  16.4 80.8 %collective-permute-start = (bf16[256,3584]{0,1:T(8,128)(2,1)}, bf16[256,3584]{0,1:T(8,128)(2,1)S(1)}, u32[]{:S(2)}, u32[]{:S(2)}) collective-permute-start(bf16[256,3584]{0,1:T(8,128)(2,1)} %fusion.10), channel_id=1, source_target_pairs={{0,3},{1,0},{2,1},{3,2},{4,7},{5,4},{6,5},{7,6},{8,11},{9,8},{10,9... | collective-permute-start | bytes 5505032 | tf_op jit(solution)/shard_map/ppermute | solution.py:147
  66.4 30.8 %copy-start.3 = (bf16[32,448,288]{1,2,0:T(8,128)(2,1)S(1)}, bf16[32,448,288]{1,2,0:T(8,128)(2,1)}, u32[]{:S(2)}) copy-start(bf16[32,448,288]{1,2,0:T(8,128)(2,1)} %all-gather.7.cloned.1.call-done) | copy-start | bytes 24772612
  69.4 36.4 %collective-permute-start.8 = (bf16[256,1,288]{0,2,1:T(8,128)(2,1)S(1)}, bf16[256,1,288]{0,2,1:T(8,128)(2,1)S(1)}, u32[]{:S(2)}, u32[]{:S(2)}) collective-permute-start(bf16[256,1,288]{0,2,1:T(8,128)(2,1)S(1)} %fusion.73), channel_id=1, source_target_pairs={{0,3},{1,0},{2,1},{3,2},{4,7},{5,4},{6,5},{7,6},{8,11},{9,8},{10,9... | collective-permute-start | bytes 442376 | tf_op jit(solution)/shard_map/ppermute | solution.py:169
  73.2 32.6 %collective-permute-start.7 = (bf16[256,1,288]{0,2,1:T(8,128)(2,1)S(1)}, bf16[256,1,288]{0,2,1:T(8,128)(2,1)S(1)}, u32[]{:S(2)}, u32[]{:S(2)}) collective-permute-start(bf16[256,1,288]{0,2,1:T(8,128)(2,1)S(1)} %fusion.72), channel_id=1, source_target_pairs={{0,2},{1,3},{2,0},{3,1},{4,6},{5,7},{6,4},{7,5},{8,10},{9,11},{10,... | collective-permute-start | bytes 442376 | tf_op jit(solution)/shard_map/ppermute | solution.py:169
  97.2 1.3 copy-start.4
  98.5 7.3 %collective-permute-start.6 = (bf16[256,1,288]{0,2,1:T(8,128)(2,1)S(1)}, bf16[256,1,288]{0,2,1:T(8,128)(2,1)S(1)}, u32[]{:S(2)}, u32[]{:S(2)}) collective-permute-start(bf16[256,1,288]{0,2,1:T(8,128)(2,1)S(1)} %fusion.71), channel_id=1, source_target_pairs={{0,1},{1,2},{2,3},{3,0},{4,5},{5,6},{6,7},{7,4},{8,9},{9,10},{10,1... | collective-permute-start | bytes 442376 | tf_op jit(solution)/shard_map/ppermute | solution.py:169
  112.1 16.4 %slice-start = ((s8[9437184]{0:T(1024)(128)(4,1)}), s8[4194304]{0:T(1024)(128)(4,1)S(1)}, s32[]{:S(2)}) async-start(s8[9437184]{0:T(1024)(128)(4,1)} %bitcast.235), calls=%async_computation.2 | async-start | bytes 8388608
  112.1 16.4 %slice-start.1 = ((s8[9437184]{0:T(1024)(128)(4,1)}), s8[4194304]{0:T(1024)(128)(4,1)S(1)}, s32[]{:S(2)}) async-start(s8[9437184]{0:T(1024)(128)(4,1)} %bitcast.235), calls=%async_computation.3 | async-start | bytes 8388608
  117.6 34.2 %collective-permute-start.5 = (bf16[256,3,288]{0,2,1:T(8,128)(2,1)S(1)}, bf16[256,3,288]{0,2,1:T(8,128)(2,1)S(1)}, u32[]{:S(2)}, u32[]{:S(2)}) collective-permute-start(bf16[256,3,288]{0,2,1:T(8,128)(2,1)S(1)} %fusion.39), channel_id=1, source_target_pairs={{0,3},{1,0},{2,1},{3,2},{4,7},{5,4},{6,5},{7,6},{8,11},{9,8},{10,9... | collective-permute-start | bytes 1327112 | tf_op jit(solution)/shard_map/ppermute | solution.py:169
  120.1 8.4 %slice-start.2 = ((s8[9437184]{0:T(1024)(128)(4,1)}), s8[1048576]{0:T(1024)(128)(4,1)S(1)}, s32[]{:S(2)}) async-start(s8[9437184]{0:T(1024)(128)(4,1)} %bitcast.235), calls=%async_computation.4 | async-start | bytes 2097152
  120.1 8.4 %copy-start.5 = (bf16[256,3584]{0,1:T(8,128)(2,1)S(1)}, bf16[256,3584]{0,1:T(8,128)(2,1)}, u32[]{:S(2)}) copy-start(bf16[256,3584]{0,1:T(8,128)(2,1)} %copy-done.4) | copy-start | bytes 5505028
  126.0 25.8 %collective-permute-start.3 = (bf16[256,3,288]{0,2,1:T(8,128)(2,1)S(1)}, bf16[256,3,288]{0,2,1:T(8,128)(2,1)S(1)}, u32[]{:S(2)}, u32[]{:S(2)}) collective-permute-start(bf16[256,3,288]{0,2,1:T(8,128)(2,1)S(1)} %fusion.48), channel_id=1, source_target_pairs={{0,2},{1,3},{2,0},{3,1},{4,6},{5,7},{6,4},{7,5},{8,10},{9,11},{10,... | collective-permute-start | bytes 1327112 | tf_op jit(solution)/shard_map/ppermute | solution.py:169
  130.5 21.3 %collective-permute-start.1 = (bf16[256,3,288]{0,2,1:T(8,128)(2,1)S(1)}, bf16[256,3,288]{0,2,1:T(8,128)(2,1)S(1)}, u32[]{:S(2)}, u32[]{:S(2)}) collective-permute-start(bf16[256,3,288]{0,2,1:T(8,128)(2,1)S(1)} %fusion.45), channel_id=1, source_target_pairs={{0,1},{1,2},{2,3},{3,0},{4,5},{5,6},{6,7},{7,4},{8,9},{9,10},{10,1... | collective-permute-start | bytes 1327112 | tf_op jit(solution)/shard_map/ppermute | solution.py:169
Sparse Core Ops, SparseCore 0:
  10.2 56.1 all-gather.6
  108.3 84.3 all-gather.4

commit v12 on v11

--- a/solution.py
+++ b/solution.py
@@ -45,7 +45,7 @@
         for g in range(KV_HEADS):
             dims = slice(g * HEAD_DIM, (g + 1) * HEAD_DIM)
             keys = k_ref[:, dims]
-            values = jnp.transpose(v_ref[:, dims].astype(jnp.float32)).astype(jnp.bfloat16)
+            values = jnp.transpose(v_ref[:, dims])
             for hh in range(group):
                 h = g * group + hh
                 heads = slice(h * HEAD_DIM, (h + 1) * HEAD_DIM)

time: 230 us -> 229 us (level)
  the two profiles are of different devices: /device:TPU:47 before, /device:TPU:28 now
where the time goes in v12:
time: 229 us; the launch traced here: 225 us
  waiting for transfers between devices  131 us (57%)
  matrix products  25.7 us (11%)
  Pallas kernels  25.7 us (11%)
  between operations  17 us (7%)
  starting transfers between devices  11.7 us (5%)
  other arithmetic  8.93 us (4%)
  local copies, waits for them, and re-layouts  5.07 us (2%)
    ppermute x3, waiting for transfers between devices, project_joined(): shifted.append(lax.ppermute(normed, 'x', pairs))  63.2 us
    all_gather x1, waiting for transfers between devices, on_device(): piece = lax.all_gather(kv_rows, ('y', 'x'), axis=0, tiled=True)  37 us
    pallas_call x1, Pallas kernels, flash(): pl.pallas_call(flash_body, grid_spec=spec, out_shape=jax.ShapeDtypeStruct...  25.7 us
    dot_general x8, matrix products, project(): jnp.einsum('tie,iyec->tyc', piece.reshape(rows, pieces.shape[0], weight.s...  25.7 us
    ppermute x6, waiting for transfers between devices, exchange(): got = lax.ppermute(outs[(n_x - step) % n_x], 'x', pairs)  20 us
    all_gather x1, waiting for transfers between devices, project_joined(): pieces = lax.all_gather(weight, ('z', 'c', 'y'), axis=0, tiled=False)  10.4 us
    ppermute x6, starting transfers between devices, exchange(): got = lax.ppermute(outs[(n_x - step) % n_x], 'x', pairs)  8.48 us
  transfers between devices with their start and end apart: 11, of which 6 were waited for; matrix products, arithmetic and copies ran while one was open for 16% of the time, Pallas kernels for 0%

profile of v12, /device:TPU:28, one launch (start us, length us, event | category | flops | bytes accessed | tf_op | source)
XLA Modules:
  0.0 225.3 jit_solution(11473343122381668848)
XLA Ops:
  7.2 0.7 all-gather.7.cloned.1.call-update
  7.9 2.9 %copy.67 = bf16[256,3584]{0,1:T(8,128)(2,1)S(1)} copy(bf16[256,3584]{1,0:T(8,128)(2,1)} %param.5) | data formatting | bytes 3670016 | tf_op args[0]
  10.9 0.5 fusion.8
  11.6 2.5 %fusion.10 = bf16[256,3584]{0,1:T(8,128)(2,1)} fusion(bf16[256,3584]{0,1:T(8,128)(2,1)S(1)} %copy.67, f32[3584]{0:T(1024)S(1)} %copy-done.1, f32[256]{0:T(256)S(1)} %add_rsqrt_fusion), kind=kLoop, calls=%fused_computation.12 | loop fusion | flops 3670016 | bytes 3685376 | tf_op jit(solution)/shard_map/convert_element_type | solution.py:116
  14.0 1.2 collective-permute-start.4
  15.2 0.8 collective-permute-start.2
  16.0 1.1 collective-permute-start
  18.1 39.1 %collective-permute-done.4 = bf16[256,3584]{0,1:T(8,128)(2,1)} collective-permute-done((bf16[256,3584]{0,1:T(8,128)(2,1)}, bf16[256,3584]{0,1:T(8,128)(2,1)}, u32[]{:S(2)}, u32[]{:S(2)}) %collective-permute-start.4) | collective-permute-done | bytes 1835040 | tf_op jit(solution)/shard_map/ppermute | solution.py:147
  57.3 10.4 %all-gather.7.cloned.1.call-done = bf16[32,448,288]{1,2,0:T(8,128)(2,1)} async-done(((bf16[1,448,288]{1,2,0:T(8,128)(2,1)}), bf16[32,448,288]{1,2,0:T(8,128)(2,1)}) %all-gather.7.cloned.1.call-update) | async-done | bytes 8257552 | tf_op jit(solution)/shard_map/all_gather | solution.py:148
  67.7 3.1 %fusion.73 = bf16[256,1,288]{0,2,1:T(8,128)(2,1)S(1)} fusion(bf16[256,8,448]{0,2,1:T(8,128)(2,1)} %bitcast.24, bf16[8,4,448,288]{2,3,1,0:T(8,128)(2,1)} %bitcast.229, f32[288]{0:T(512)S(1)} %fusion.74), kind=kOutput, calls=%fused_computation.52 | convolution fusion | flops 528629760 | bytes 4342912 | tf_op jit(solution)/shard_map/tie,iyec->tyc/dot_general | solution.py:155
  70.7 0.6 collective-permute-start.8
  71.4 24.1 %collective-permute-done.2 = bf16[256,3584]{0,1:T(8,128)(2,1)} collective-permute-done((bf16[256,3584]{0,1:T(8,128)(2,1)}, bf16[256,3584]{0,1:T(8,128)(2,1)}, u32[]{:S(2)}, u32[]{:S(2)}) %collective-permute-start.2) | collective-permute-done | bytes 1835040 | tf_op jit(solution)/shard_map/ppermute | solution.py:147
  95.4 2.9 %fusion.72 = bf16[256,1,288]{0,2,1:T(8,128)(2,1)S(1)} fusion(bf16[256,8,448]{0,2,1:T(8,128)(2,1)} %bitcast.18, bf16[8,4,448,288]{2,3,1,0:T(8,128)(2,1)} %bitcast.230, f32[288]{0:T(512)S(1)} %fusion.74), kind=kOutput, calls=%fused_computation.51 | convolution fusion | flops 528629760 | bytes 4342912 | tf_op jit(solution)/shard_map/tie,iyec->tyc/dot_general | solution.py:155
  98.4 2.8 %collective-permute-start.7 = (bf16[256,1,288]{0,2,1:T(8,128)(2,1)S(1)}, bf16[256,1,288]{0,2,1:T(8,128)(2,1)S(1)}, u32[]{:S(2)}, u32[]{:S(2)}) collective-permute-start(bf16[256,1,288]{0,2,1:T(8,128)(2,1)S(1)} %fusion.72), channel_id=1, source_target_pairs={{0,2},{1,3},{2,0},{3,1},{4,6},{5,7},{6,4},{7,5},{8,10},{9,11},{10,... | collective-permute-start | bytes 442376 | tf_op jit(solution)/shard_map/ppermute | solution.py:169
  101.1 0.7 fusion.71
  101.9 0.6 copy-done.4
  102.5 2.2 fusion.70
  104.7 3.6 %collective-permute-done.6 = bf16[256,1,288]{0,2,1:T(8,128)(2,1)S(1)} collective-permute-done((bf16[256,1,288]{0,2,1:T(8,128)(2,1)S(1)}, bf16[256,1,288]{0,2,1:T(8,128)(2,1)S(1)}, u32[]{:S(2)}, u32[]{:S(2)}) %collective-permute-start.6) | collective-permute-done | bytes 147488 | tf_op jit(solution)/shard_map/ppermute | solution.py:169
  109.9 0.9 pad_maximum_fusion.2
  110.7 0.7 fusion.75
  114.0 0.6 pad_add_fusion.meta
  114.6 5.5 %fusion.39 = bf16[256,3,288]{0,2,1:T(8,128)(2,1)S(1)} fusion(bf16[256,8,448,1]{0,2,3,1:T(8,128)(2,1)} %bitcast.79, bf16[8,4,448,288]{2,3,1,0:T(8,128)(2,1)} %bitcast.231, f32[3,288]{1,0:T(4,128)S(1)} %bitcast.221), kind=kOutput, calls=%fused_computation.30 | convolution fusion | flops 1585889280 | bytes 9358720 | tf_op jit(solution)/shard_map/tie,iyec->tyc/dot_general | solution.py:155
  120.4 5.9 %fusion.48 = bf16[256,3,288]{0,2,1:T(8,128)(2,1)S(1)} fusion(bf16[256,8,448,1]{0,2,3,1:T(8,128)(2,1)} %bitcast.77, bf16[8,4,448,288]{2,3,1,0:T(8,128)(2,1)} %bitcast.232, f32[3,288]{1,0:T(4,128)S(1)} %bitcast.222), kind=kOutput, calls=%fused_computation.33 | convolution fusion | flops 1585889280 | bytes 9358720 | tf_op jit(solution)/shard_map/tie,iyec->tyc/dot_general | solution.py:155
  126.3 2.7 %collective-permute-start.3 = (bf16[256,3,288]{0,2,1:T(8,128)(2,1)S(1)}, bf16[256,3,288]{0,2,1:T(8,128)(2,1)S(1)}, u32[]{:S(2)}, u32[]{:S(2)}) collective-permute-start(bf16[256,3,288]{0,2,1:T(8,128)(2,1)S(1)} %fusion.48), channel_id=1, source_target_pairs={{0,2},{1,3},{2,0},{3,1},{4,6},{5,7},{6,4},{7,5},{8,10},{9,11},{10,... | collective-permute-start | bytes 1327112 | tf_op jit(solution)/shard_map/ppermute | solution.py:169
  129.0 1.9 fusion.45
  130.9 2.1 collective-permute-start.1
  133.2 3.4 %fusion.54 = bf16[256,4,3,288]{0,3,1,2:T(8,128)(2,1)S(1)} fusion(bf16[256,4,3,288]{0,3,1,2:T(8,128)(2,1)S(1)} %broadcast_in_dim.65, s32[]{:T(128)S(6)} %select_n.53, bf16[256,8,448,1]{0,2,3,1:T(8,128)(2,1)} %bitcast.73, bf16[8,4,448,288]{2,3,1,0:T(8,128)(2,1)S(1)} %bitcast.238, f32[3,288]{1,0:T(4,128)S(1)} %bitcast.224), kind=kOutput, calls=%fused_computation.35 | convolution fusion | flops 1585889280 | bytes 9361412 | tf_op jit(solution)/shard_map/tie,iyec->tyc/dot_general | solution.py:155
  136.7 16.4 %collective-permute-done.1 = bf16[256,3,288]{0,2,1:T(8,128)(2,1)S(1)} collective-permute-done((bf16[256,3,288]{0,2,1:T(8,128)(2,1)S(1)}, bf16[256,3,288]{0,2,1:T(8,128)(2,1)S(1)}, u32[]{:S(2)}, u32[]{:S(2)}) %collective-permute-start.1) | collective-permute-done | bytes 442400 | tf_op jit(solution)/shard_map/ppermute | solution.py:169
  153.8 0.6 subtract_convert_fusion
  154.4 1.4 pad_maximum_fusion.1
  155.8 37.0 %all-gather.5.cloned.1.call-done.k_ref.v_ref = bf16[4096,1024]{1,0:T(8,128)(2,1)} async-done(((bf16[256,1024]{1,0:T(8,128)(2,1)}), bf16[4096,1024]{1,0:T(8,128)(2,1)}) %all-gather.5.cloned.1.call-update) | async-done | bytes 8388624 | tf_op jit(solution)/shard_map/all_gather | solution.py:200
  192.8 25.7 %shard_map.68 = bf16[256,3584]{1,0:T(8,128)(2,1)} custom-call(s32[8]{0:T(128)} %pad_add_fusion.meta, bf16[3584,256]{1,0:T(8,128)(2,1)} %bitcast.212, bf16[4096,1024]{1,0:T(8,128)(2,1)} %all-gather.5.cloned.1.call-done.k_ref.v_ref, bf16[4096,1024]{1,0:T(8,128)(2,1)} %all-gather.5.cloned.1.call-done.k_ref.v_ref), custom_call_target="tpu_custom_call" | custom-call | tf_op jit(solution)/shard_map/pallas_call | solution.py:105
  (61 shorter events, 3.8 us)
Async XLA Ops:
  7.2 60.5 %all-gather.7.cloned.1.call-start = ((), (), s32[]{:S(2)}) async-start(), calls=%async_computation.1 | async-start | bytes 9732096 | tf_op jit(solution)/shard_map/all_gather | solution.py:148
  7.9 184.9 %all-gather.5.cloned.1.call-start = ((), (), s32[]{:S(2)}) async-start(), calls=%async_computation | async-start | bytes 8912896 | tf_op jit(solution)/shard_map/all_gather | solution.py:200
  10.8 0.7 copy-start.1
  11.6 5.6 %copy-start.2 = (s32[1,4]{1,0:T(1,128)S(1)}, s32[1,4]{1,0:T(1,128)}, u32[]{:S(2)}) copy-start(s32[1,4]{1,0:T(1,128)} %param.6) | copy-start | bytes 52
  11.6 5.8 %copy-start = (f32[4608]{0:T(1024)S(1)}, f32[4608]{0:T(1024)}, u32[]{:S(2)}) copy-start(f32[4608]{0:T(1024)} %param.9) | copy-start | bytes 55300
  14.0 43.2 %collective-permute-start.4 = (bf16[256,3584]{0,1:T(8,128)(2,1)}, bf16[256,3584]{0,1:T(8,128)(2,1)}, u32[]{:S(2)}, u32[]{:S(2)}) collective-permute-start(bf16[256,3584]{0,1:T(8,128)(2,1)} %fusion.10), channel_id=1, source_target_pairs={{0,1},{1,2},{2,3},{3,0},{4,5},{5,6},{6,7},{7,4},{8,9},{9,10},{10,1... | collective-permute-start | bytes 5505032 | tf_op jit(solution)/shard_map/ppermute | solution.py:147
  15.2 80.2 %collective-permute-start.2 = (bf16[256,3584]{0,1:T(8,128)(2,1)}, bf16[256,3584]{0,1:T(8,128)(2,1)}, u32[]{:S(2)}, u32[]{:S(2)}) collective-permute-start(bf16[256,3584]{0,1:T(8,128)(2,1)} %fusion.10), channel_id=1, source_target_pairs={{0,2},{1,3},{2,0},{3,1},{4,6},{5,7},{6,4},{7,5},{8,10},{9,11},{10,... | collective-permute-start | bytes 5505032 | tf_op jit(solution)/shard_map/ppermute | solution.py:147
  16.0 85.1 %collective-permute-start = (bf16[256,3584]{0,1:T(8,128)(2,1)}, bf16[256,3584]{0,1:T(8,128)(2,1)S(1)}, u32[]{:S(2)}, u32[]{:S(2)}) collective-permute-start(bf16[256,3584]{0,1:T(8,128)(2,1)} %fusion.10), channel_id=1, source_target_pairs={{0,3},{1,0},{2,1},{3,2},{4,7},{5,4},{6,5},{7,6},{8,11},{9,8},{10,9... | collective-permute-start | bytes 5505032 | tf_op jit(solution)/shard_map/ppermute | solution.py:147
  67.7 33.5 %copy-start.3 = (bf16[32,448,288]{1,2,0:T(8,128)(2,1)S(1)}, bf16[32,448,288]{1,2,0:T(8,128)(2,1)}, u32[]{:S(2)}) copy-start(bf16[32,448,288]{1,2,0:T(8,128)(2,1)} %all-gather.7.cloned.1.call-done) | copy-start | bytes 24772612
  70.7 37.7 %collective-permute-start.8 = (bf16[256,1,288]{0,2,1:T(8,128)(2,1)S(1)}, bf16[256,1,288]{0,2,1:T(8,128)(2,1)S(1)}, u32[]{:S(2)}, u32[]{:S(2)}) collective-permute-start(bf16[256,1,288]{0,2,1:T(8,128)(2,1)S(1)} %fusion.73), channel_id=1, source_target_pairs={{0,3},{1,0},{2,1},{3,2},{4,7},{5,4},{6,5},{7,6},{8,11},{9,8},{10,9... | collective-permute-start | bytes 442376 | tf_op jit(solution)/shard_map/ppermute | solution.py:169
  98.4 10.0 %collective-permute-start.7 = (bf16[256,1,288]{0,2,1:T(8,128)(2,1)S(1)}, bf16[256,1,288]{0,2,1:T(8,128)(2,1)S(1)}, u32[]{:S(2)}, u32[]{:S(2)}) collective-permute-start(bf16[256,1,288]{0,2,1:T(8,128)(2,1)S(1)} %fusion.72), channel_id=1, source_target_pairs={{0,2},{1,3},{2,0},{3,1},{4,6},{5,7},{6,4},{7,5},{8,10},{9,11},{10,... | collective-permute-start | bytes 442376 | tf_op jit(solution)/shard_map/ppermute | solution.py:169
  101.1 1.3 copy-start.4
  102.4 5.9 %collective-permute-start.6 = (bf16[256,1,288]{0,2,1:T(8,128)(2,1)S(1)}, bf16[256,1,288]{0,2,1:T(8,128)(2,1)S(1)}, u32[]{:S(2)}, u32[]{:S(2)}) collective-permute-start(bf16[256,1,288]{0,2,1:T(8,128)(2,1)S(1)} %fusion.71), channel_id=1, source_target_pairs={{0,1},{1,2},{2,3},{3,0},{4,5},{5,6},{6,7},{7,4},{8,9},{9,10},{10,1... | collective-permute-start | bytes 442376 | tf_op jit(solution)/shard_map/ppermute | solution.py:169
  114.6 14.4 %slice-start = ((s8[9437184]{0:T(1024)(128)(4,1)}), s8[4194304]{0:T(1024)(128)(4,1)S(1)}, s32[]{:S(2)}) async-start(s8[9437184]{0:T(1024)(128)(4,1)} %bitcast.235), calls=%async_computation.2 | async-start | bytes 8388608
  114.6 14.4 %slice-start.1 = ((s8[9437184]{0:T(1024)(128)(4,1)}), s8[4194304]{0:T(1024)(128)(4,1)S(1)}, s32[]{:S(2)}) async-start(s8[9437184]{0:T(1024)(128)(4,1)} %bitcast.235), calls=%async_computation.3 | async-start | bytes 8388608
  120.1 33.0 %collective-permute-start.5 = (bf16[256,3,288]{0,2,1:T(8,128)(2,1)S(1)}, bf16[256,3,288]{0,2,1:T(8,128)(2,1)S(1)}, u32[]{:S(2)}, u32[]{:S(2)}) collective-permute-start(bf16[256,3,288]{0,2,1:T(8,128)(2,1)S(1)} %fusion.39), channel_id=1, source_target_pairs={{0,3},{1,0},{2,1},{3,2},{4,7},{5,4},{6,5},{7,6},{8,11},{9,8},{10,9... | collective-permute-start | bytes 1327112 | tf_op jit(solution)/shard_map/ppermute | solution.py:169
  120.4 8.6 %slice-start.2 = ((s8[9437184]{0:T(1024)(128)(4,1)}), s8[1048576]{0:T(1024)(128)(4,1)S(1)}, s32[]{:S(2)}) async-start(s8[9437184]{0:T(1024)(128)(4,1)} %bitcast.235), calls=%async_computation.4 | async-start | bytes 2097152
  120.4 8.6 %copy-start.5 = (bf16[256,3584]{0,1:T(8,128)(2,1)S(1)}, bf16[256,3584]{0,1:T(8,128)(2,1)}, u32[]{:S(2)}) copy-start(bf16[256,3584]{0,1:T(8,128)(2,1)} %copy-done.4) | copy-start | bytes 5505028
  126.3 26.7 %collective-permute-start.3 = (bf16[256,3,288]{0,2,1:T(8,128)(2,1)S(1)}, bf16[256,3,288]{0,2,1:T(8,128)(2,1)S(1)}, u32[]{:S(2)}, u32[]{:S(2)}) collective-permute-start(bf16[256,3,288]{0,2,1:T(8,128)(2,1)S(1)} %fusion.48), channel_id=1, source_target_pairs={{0,2},{1,3},{2,0},{3,1},{4,6},{5,7},{6,4},{7,5},{8,10},{9,11},{10,... | collective-permute-start | bytes 1327112 | tf_op jit(solution)/shard_map/ppermute | solution.py:169
  130.9 22.1 %collective-permute-start.1 = (bf16[256,3,288]{0,2,1:T(8,128)(2,1)S(1)}, bf16[256,3,288]{0,2,1:T(8,128)(2,1)S(1)}, u32[]{:S(2)}, u32[]{:S(2)}) collective-permute-start(bf16[256,3,288]{0,2,1:T(8,128)(2,1)S(1)} %fusion.45), channel_id=1, source_target_pairs={{0,1},{1,2},{2,3},{3,0},{4,5},{5,6},{6,7},{7,4},{8,9},{9,10},{10,1... | collective-permute-start | bytes 1327112 | tf_op jit(solution)/shard_map/ppermute | solution.py:169
Sparse Core Ops, SparseCore 0:
  10.2 57.3 all-gather.6
  110.9 81.8 all-gather.4
